TPU v7x, 256 devices: a whole 4x4x8 slice. The times are simulated.
256 devices in a mesh: grp: 8 (over y_hi, x), blk: 32 (over y_lo, z, core).
Axes of the slice: x: 4, y: 4 (y_hi: 2, y_lo: 2; y = y_hi * 2 + y_lo), z: 8, core: 2. Of those that a mesh axis runs over, the one named last changes fastest.
Arguments:
- features: bfloat16 [65536, 1536], P(('grp', 'blk')), may hold values from -2 to 2
- queries: bfloat16 [65536, 768], P(('grp', 'blk')), may hold values from -6 to 6
- key_vectors: bfloat16 [65536, 768], P(('grp', 'blk')), may hold values from -6 to 6
- values: bfloat16 [65536, 768], P(('grp', 'blk')), may hold values from -8 to 8
- record_lengths: int32 [128], replicated, may hold values from 1 to 1024, 65536 in all
- output_weight: bfloat16 [768, 1536], replicated, may hold values from -0.21875 to 0.21875
- norm_gain: float32 [1536], replicated, may hold values from 0.5 to 2
- norm_bias: float32 [1536], replicated, may hold values from -3 to 3
- depthwise_taps: float32 [31, 1536], replicated, may hold values from -1 to 1
- conv_gain: float32 [1536], replicated, may hold values from 0.5 to 2
- conv_bias: float32 [1536], replicated, may hold values from -3 to 3
- pointwise_weight: bfloat16 [1536, 1536], replicated, may hold values from -0.15625 to 0.15625
Outputs:
- block_out: bfloat16 [65536, 1536], P(('grp', 'blk'))
Inputs may be any that keep to these rules, and one draw needn't show every extreme that they name: `record_lengths`: recording lengths in frames, summing to 65536; the longest is exactly 1024.
All inputs are finite; a program needn't handle non-finite values.
Results may differ from a plain program's by a relative error of at most 0.013.
Values may be sent and summed in bfloat16 or wider, within the bound.
No kernel may reach another device: no remote copies, remote signals or barrier semaphores. Data moves between devices by JAX's collectives and lax.ppermute only.
A program may use at most 128 MiB of HBM per device.

v0:
```python
import jax
import jax.numpy as jnp
from jax import lax
from jax.sharding import PartitionSpec as P
from jax.experimental import pallas as pl
from jax.experimental.pallas import tpu as pltpu

HEADS = 12
HD = 64
REACH = 4


def shifted_2(block, axis, distance):
    devices = range(lax.axis_size(axis))
    route = [(i - distance, i) for i in devices if i - distance in devices]
    return lax.ppermute(block, axis, route)


def padded(block, sides, width):
    for axis, dim in sides:
        count = lax.axis_size(axis)
        forward = [(i, i + 1) for i in range(count - 1)]
        backward = [(target, source) for source, target in forward]
        low = lax.ppermute(
            lax.slice_in_dim(block, block.shape[dim] - width, None, axis=dim), axis, forward
        )
        high = lax.ppermute(lax.slice_in_dim(block, 0, width, axis=dim), axis, backward)
        block = jnp.concatenate([low, block, high], axis=dim)
    return block


def segment_of(positions, starts):
    return jnp.sum((starts[None, :] <= positions[:, None]).astype(jnp.int32), axis=1) - 1


def from_before(moving):
    return shifted_2(moving, ("grp", "blk"), 1)


def from_after(moving):
    return shifted_2(moving, ("grp", "blk"), -1)


NBLK = 2 * REACH + 1


def attend_kernel(recq_ref, reck_ref, q_ref, *refs):
    k_refs = refs[:NBLK]
    v_refs = refs[NBLK : 2 * NBLK]
    out_ref = refs[2 * NBLK]
    s_scr = refs[2 * NBLK + 1]
    rec_q = recq_ref[...]
    for hh in range(2):
        cols = slice(hh * HD, (hh + 1) * HD)
        q_h = q_ref[:, cols]
        top = None
        for j in range(NBLK):
            s = lax.dot_general(
                q_h, k_refs[j][:, cols], (((1,), (1,)), ((), ())),
                preferred_element_type=jnp.float32,
            ) * (HD ** (-0.5))
            s = jnp.where(rec_q == reck_ref[j : j + 1, :], s, -1e30)
            s_scr[j] = s
            row = jnp.max(s, axis=1, keepdims=True)
            top = row if top is None else jnp.maximum(top, row)
        total = None
        acc = None
        for j in range(NBLK):
            p = jnp.exp(s_scr[j] - top)
            part = jnp.sum(p, axis=1, keepdims=True)
            prod = jnp.dot(p.astype(jnp.bfloat16), v_refs[j][:, cols],
                           preferred_element_type=jnp.float32)
            total = part if total is None else total + part
            acc = prod if acc is None else acc + prod
        out_ref[:, cols] = (acc / total).astype(out_ref.dtype)


def attend(rec_q, rec_k, query, keys, vals):
    frames, width = query.shape
    pair = 2 * HD
    tile = pl.BlockSpec((frames, pair), lambda g: (0, g))
    return pl.pallas_call(
        attend_kernel,
        grid=(width // pair,),
        in_specs=[
            pl.BlockSpec(rec_q.shape, lambda g: (0, 0)),
            pl.BlockSpec(rec_k.shape, lambda g: (0, 0)),
            tile,
        ]
        + [tile] * (2 * NBLK),
        out_specs=tile,
        out_shape=jax.ShapeDtypeStruct((frames, width), jnp.bfloat16),
        scratch_shapes=[pltpu.VMEM((NBLK, frames, frames), jnp.float32)],
    )(rec_q, rec_k, query, *keys, *vals)


def shards(
    features,
    queries,
    key_vectors,
    values,
    record_lengths,
    output_weight,
    norm_gain,
    norm_bias,
    depthwise_taps,
    conv_gain,
    conv_bias,
    pointwise_weight,
):
    frames = features.shape[0]
    per_group = lax.axis_size("blk")
    nblocks = lax.axis_size("grp") * per_group
    block_here = lax.axis_index("grp") * per_group + lax.axis_index("blk")
    rec_ends = jnp.cumsum(record_lengths)
    starts = rec_ends - record_lengths
    offsets = jnp.arange(frames, dtype=jnp.int32)
    own_rec = segment_of(block_here * frames + offsets, starts)

    key_blocks = block_here + jnp.arange(-REACH, REACH + 1, dtype=jnp.int32)
    key_pos = (key_blocks[:, None] * frames + offsets[None, :]).reshape(-1)
    key_inside = ((key_blocks >= 0) & (key_blocks < nblocks))[:, None]
    key_rec = jnp.where(key_inside, segment_of(key_pos, starts).reshape(NBLK, frames), -1)
    rows = -(-NBLK // 8) * 8
    key_rec = jnp.pad(key_rec, ((0, rows - NBLK), (0, 0)), constant_values=-1)

    before_k, before_v, after_k, after_v = [], [], [], []
    moving = (key_vectors, values)
    for distance in range(1, REACH + 1):
        moving = from_before(moving)
        before_k.append(moving[0])
        before_v.append(moving[1])
    moving = (key_vectors, values)
    for distance in range(1, REACH + 1):
        moving = from_after(moving)
        after_k.append(moving[0])
        after_v.append(moving[1])
    keys = before_k[::-1] + [key_vectors] + after_k
    vals = before_v[::-1] + [values] + after_v
    attended = attend(own_rec[:, None], key_rec, queries, keys, vals)
    projected = jnp.dot(attended, output_weight, preferred_element_type=jnp.float32)
    resid = lax.optimization_barrier(
        (features.astype(jnp.float32) + projected).astype(jnp.bfloat16)
    )
    resid32 = resid.astype(jnp.float32)
    center = jnp.mean(resid32, axis=1, keepdims=True)
    spread = jnp.mean((resid32 - center) ** 2, axis=1, keepdims=True)
    normed = ((resid32 - center) * lax.rsqrt(spread + 1e-05) * norm_gain + norm_bias).astype(
        jnp.bfloat16
    )
    rim_width = (depthwise_taps.shape[0] - 1) // 2
    extended = padded(normed, ((("grp", "blk"), 0),), rim_width)
    ext_positions = (
        block_here * frames - rim_width + jnp.arange(frames + 2 * rim_width, dtype=jnp.int32)
    )
    ext_inside = (ext_positions >= 0) & (ext_positions < nblocks * frames)
    ext_rec = jnp.where(ext_inside, segment_of(ext_positions, starts), -1)
    extended32 = lax.optimization_barrier(extended).astype(jnp.float32)
    summed = jnp.zeros((frames, normed.shape[1]), jnp.float32)
    for tap in range(depthwise_taps.shape[0]):
        same_rec = (ext_rec[tap : tap + frames] == own_rec)[:, None]
        summed = summed + jnp.where(
            same_rec, extended32[tap : tap + frames] * depthwise_taps[tap], 0.0
        )
    shifted = summed * conv_gain + conv_bias
    act = (shifted * jax.nn.sigmoid(shifted)).astype(jnp.bfloat16)
    return (resid32 + jnp.dot(act, pointwise_weight, preferred_element_type=jnp.float32)).astype(
        jnp.bfloat16
    )


def solution(mesh):
    in_specs = (
        P(("grp", "blk"), None),
        P(("grp", "blk"), None),
        P(("grp", "blk"), None),
        P(("grp", "blk"), None),
        P(),
        P(),
        P(),
        P(),
        P(),
        P(),
        P(),
        P(),
    )
    out_specs = P(("grp", "blk"), None)
    return jax.shard_map(shards, mesh=mesh, in_specs=in_specs, out_specs=out_specs, check_vma=False)
```

profile of v0, /device:TPU:16, one launch (start us, length us, event | category | flops | bytes accessed | tf_op | source)
XLA Modules:
  0.0 150.2 jit_solution(15676015015636718163)
XLA Ops:
  0.0 2.0 %collective-permute-start.8 = (bf16[256,768]{1,0:T(8,128)(2,1)}, bf16[256,768]{1,0:T(8,128)(2,1)S(1)}, u32[]{:S(2)}, u32[]{:S(2)}) collective-permute-start(bf16[256,768]{1,0:T(8,128)(2,1)} %refs_13_.1), channel_id=1, source_target_pairs={{0,1},{1,2},{2,3},{3,4},{4,5},{5,6},{6,7},{7,8},{8,9},{9,10},{10,1... | collective-permute-start | bytes 1179656 | tf_op jit(solution)/shard_map/ppermute | solution.py:16
  2.1 9.3 %collective-permute-start.12 = (bf16[256,768]{1,0:T(8,128)(2,1)}, bf16[256,768]{1,0:T(8,128)(2,1)S(1)}, u32[]{:S(2)}, u32[]{:S(2)}) collective-permute-start(bf16[256,768]{1,0:T(8,128)(2,1)} %refs_13_.1), channel_id=1, source_target_pairs={{1,0},{2,1},{3,2},{4,3},{5,4},{6,5},{7,6},{8,7},{9,8},{10,9},{11,1... | collective-permute-start | bytes 1179656 | tf_op jit(solution)/shard_map/ppermute | solution.py:16
  11.3 1.9 %collective-permute-start = (bf16[256,768]{1,0:T(8,128)(2,1)}, bf16[256,768]{1,0:T(8,128)(2,1)S(1)}, u32[]{:S(2)}, u32[]{:S(2)}) collective-permute-start(bf16[256,768]{1,0:T(8,128)(2,1)} %refs_4_.1), channel_id=1, source_target_pairs={{0,1},{1,2},{2,3},{3,4},{4,5},{5,6},{6,7},{7,8},{8,9},{9,10},{10,1... | collective-permute-start | bytes 1179656 | tf_op jit(solution)/shard_map/ppermute | solution.py:16
  13.3 7.9 %collective-permute-start.4 = (bf16[256,768]{1,0:T(8,128)(2,1)}, bf16[256,768]{1,0:T(8,128)(2,1)}, u32[]{:S(2)}, u32[]{:S(2)}) collective-permute-start(bf16[256,768]{1,0:T(8,128)(2,1)} %refs_4_.1), channel_id=1, source_target_pairs={{1,0},{2,1},{3,2},{4,3},{5,4},{6,5},{7,6},{8,7},{9,8},{10,9},{11,1... | collective-permute-start | bytes 1179656 | tf_op jit(solution)/shard_map/ppermute | solution.py:16
  22.6 1.6 %reduce-window.9 = s32[128,1]{1,0:T(8,128)} reduce-window(s32[128,1]{1,0:T(8,128)} %copy.16, s32[]{:T(128)} %constant.14.clone.1), window={size=128x1 pad=127_0x0_0}, to_apply=%region_0.0 | reduce-window | flops 16256 | bytes 1028 | tf_op jit(solution)/shard_map/reduce-window.4
  26.7 1.9 %collective-permute-start.9 = (bf16[256,768]{1,0:T(8,128)(2,1)S(1)}, bf16[256,768]{1,0:T(8,128)(2,1)}, u32[]{:S(2)}, u32[]{:S(2)}) collective-permute-start(bf16[256,768]{1,0:T(8,128)(2,1)S(1)} %collective-permute-done.8.refs_12_), channel_id=1, source_target_pairs={{0,1},{1,2},{2,3},{3,4},{4,5},{5,6},{6,7},{7,8},{8,9},{9,10},{10,1... | collective-permute-start | bytes 1179656 | tf_op jit(solution)/shard_map/ppermute | solution.py:16
  28.6 7.9 %collective-permute-start.13 = (bf16[256,768]{1,0:T(8,128)(2,1)S(1)}, bf16[256,768]{1,0:T(8,128)(2,1)}, u32[]{:S(2)}, u32[]{:S(2)}) collective-permute-start(bf16[256,768]{1,0:T(8,128)(2,1)S(1)} %collective-permute-done.12.refs_14_), channel_id=1, source_target_pairs={{1,0},{2,1},{3,2},{4,3},{5,4},{6,5},{7,6},{8,7},{9,8},{10,9},{11,1... | collective-permute-start | bytes 1179656 | tf_op jit(solution)/shard_map/ppermute | solution.py:16
  36.5 1.9 %collective-permute-start.1 = (bf16[256,768]{1,0:T(8,128)(2,1)S(1)}, bf16[256,768]{1,0:T(8,128)(2,1)}, u32[]{:S(2)}, u32[]{:S(2)}) collective-permute-start(bf16[256,768]{1,0:T(8,128)(2,1)S(1)} %collective-permute-done.refs_3_), channel_id=1, source_target_pairs={{0,1},{1,2},{2,3},{3,4},{4,5},{5,6},{6,7},{7,8},{8,9},{9,10},{10,1... | collective-permute-start | bytes 1179656 | tf_op jit(solution)/shard_map/ppermute | solution.py:16
  38.5 7.9 %collective-permute-start.5 = (bf16[256,768]{1,0:T(8,128)(2,1)}, bf16[256,768]{1,0:T(8,128)(2,1)}, u32[]{:S(2)}, u32[]{:S(2)}) collective-permute-start(bf16[256,768]{1,0:T(8,128)(2,1)} %collective-permute-done.4.refs_5_), channel_id=1, source_target_pairs={{1,0},{2,1},{3,2},{4,3},{5,4},{6,5},{7,6},{8,7},{9,8},{10,9},{11,1... | collective-permute-start | bytes 1179656 | tf_op jit(solution)/shard_map/ppermute | solution.py:16
  47.8 2.0 %convert_reduce_fusion.1 = s32[2304]{0:T(1024)S(1)} fusion(s32[128]{0:T(128)} %copy-done.24, s32[2304]{0:T(1024)S(1)} %add.217), kind=kLoop, calls=%fused_computation.107 | loop fusion | flops 882432 | bytes 18944 | tf_op jit(solution)/shard_map/reduce_sum | solution.py:33
  49.8 1.9 %collective-permute-start.10 = (bf16[256,768]{1,0:T(8,128)(2,1)}, bf16[256,768]{1,0:T(8,128)(2,1)}, u32[]{:S(2)}, u32[]{:S(2)}) collective-permute-start(bf16[256,768]{1,0:T(8,128)(2,1)} %collective-permute-done.9.refs_11_), channel_id=1, source_target_pairs={{0,1},{1,2},{2,3},{3,4},{4,5},{5,6},{6,7},{7,8},{8,9},{9,10},{10,1... | collective-permute-start | bytes 1179656 | tf_op jit(solution)/shard_map/ppermute | solution.py:16
  51.8 7.9 %collective-permute-start.14 = (bf16[256,768]{1,0:T(8,128)(2,1)}, bf16[256,768]{1,0:T(8,128)(2,1)}, u32[]{:S(2)}, u32[]{:S(2)}) collective-permute-start(bf16[256,768]{1,0:T(8,128)(2,1)} %collective-permute-done.13.refs_15_), channel_id=1, source_target_pairs={{1,0},{2,1},{3,2},{4,3},{5,4},{6,5},{7,6},{8,7},{9,8},{10,9},{11,1... | collective-permute-start | bytes 1179656 | tf_op jit(solution)/shard_map/ppermute | solution.py:16
  59.7 1.9 %collective-permute-start.2 = (bf16[256,768]{1,0:T(8,128)(2,1)}, bf16[256,768]{1,0:T(8,128)(2,1)}, u32[]{:S(2)}, u32[]{:S(2)}) collective-permute-start(bf16[256,768]{1,0:T(8,128)(2,1)} %collective-permute-done.1.refs_2_), channel_id=1, source_target_pairs={{0,1},{1,2},{2,3},{3,4},{4,5},{5,6},{6,7},{7,8},{8,9},{9,10},{10,1... | collective-permute-start | bytes 1179656 | tf_op jit(solution)/shard_map/ppermute | solution.py:16
  61.6 7.9 %collective-permute-start.6 = (bf16[256,768]{1,0:T(8,128)(2,1)}, bf16[256,768]{1,0:T(8,128)(2,1)}, u32[]{:S(2)}, u32[]{:S(2)}) collective-permute-start(bf16[256,768]{1,0:T(8,128)(2,1)} %collective-permute-done.5.refs_6_), channel_id=1, source_target_pairs={{1,0},{2,1},{3,2},{4,3},{5,4},{6,5},{7,6},{8,7},{9,8},{10,9},{11,1... | collective-permute-start | bytes 1179656 | tf_op jit(solution)/shard_map/ppermute | solution.py:16
  72.8 1.9 %collective-permute-start.11 = (bf16[256,768]{1,0:T(8,128)(2,1)}, bf16[256,768]{1,0:T(8,128)(2,1)}, u32[]{:S(2)}, u32[]{:S(2)}) collective-permute-start(bf16[256,768]{1,0:T(8,128)(2,1)} %collective-permute-done.10.refs_10_), channel_id=1, source_target_pairs={{0,1},{1,2},{2,3},{3,4},{4,5},{5,6},{6,7},{7,8},{8,9},{9,10},{10,1... | collective-permute-start | bytes 1179656 | tf_op jit(solution)/shard_map/ppermute | solution.py:16
  74.7 7.9 %collective-permute-start.15 = (bf16[256,768]{1,0:T(8,128)(2,1)}, bf16[256,768]{1,0:T(8,128)(2,1)}, u32[]{:S(2)}, u32[]{:S(2)}) collective-permute-start(bf16[256,768]{1,0:T(8,128)(2,1)} %collective-permute-done.14.refs_16_), channel_id=1, source_target_pairs={{1,0},{2,1},{3,2},{4,3},{5,4},{6,5},{7,6},{8,7},{9,8},{10,9},{11,1... | collective-permute-start | bytes 1179656 | tf_op jit(solution)/shard_map/ppermute | solution.py:16
  82.6 1.9 %collective-permute-start.3 = (bf16[256,768]{1,0:T(8,128)(2,1)}, bf16[256,768]{1,0:T(8,128)(2,1)}, u32[]{:S(2)}, u32[]{:S(2)}) collective-permute-start(bf16[256,768]{1,0:T(8,128)(2,1)} %collective-permute-done.2.refs_1_), channel_id=1, source_target_pairs={{0,1},{1,2},{2,3},{3,4},{4,5},{5,6},{6,7},{7,8},{8,9},{9,10},{10,1... | collective-permute-start | bytes 1179656 | tf_op jit(solution)/shard_map/ppermute | solution.py:16
  84.5 7.9 %collective-permute-start.7 = (bf16[256,768]{1,0:T(8,128)(2,1)}, bf16[256,768]{1,0:T(8,128)(2,1)}, u32[]{:S(2)}, u32[]{:S(2)}) collective-permute-start(bf16[256,768]{1,0:T(8,128)(2,1)} %collective-permute-done.6.refs_7_), channel_id=1, source_target_pairs={{1,0},{2,1},{3,2},{4,3},{5,4},{6,5},{7,6},{8,7},{9,8},{10,9},{11,1... | collective-permute-start | bytes 1179656 | tf_op jit(solution)/shard_map/ppermute | solution.py:16
  95.1 2.4 %slice_reduce_fusion.30 = (f32[1536]{0:T(1024)S(1)}, f32[1536]{0:T(1024)}, f32[1536]{0:T(1024)}, f32[1536]{0:T(1024)}, f32[1536]{0:T(1024)}, /*index=5*/f32[1536...) fusion(f32[31,1536]{1,0:T(8,128)} %param.20), kind=kLoop, calls=%fused_computation.143 | loop fusion | bytes 233472 | tf_op jit(solution)/shard_map/slice | solution.py:163
  98.9 20.2 %shard_map.118 = bf16[256,768]{1,0:T(8,128)(2,1)} custom-call(s32[256,1]{1,0:T(8,128)} %copy.17.recq_ref, s32[16,256]{1,0:T(8,128)} %pad.4.reck_ref, bf16[256,768]{1,0:T(8,128)(2,1)} %q_ref.1, bf16[256,768]{1,0:T(8,128)(2,1)} %collective-permute-done.3.refs_0_, bf16[256,768]{1,0:T(8,128)(2,1)} %collective-permute-done.2.refs_1_, ...), custom_call_target="tpu_custom_call" | custom-call | tf_op jit(solution)/shard_map/pallas_call | solution.py:82
  119.1 2.0 %fusion.1 = bf16[256,1536]{1,0:T(8,128)(2,1)S(1)} fusion(bf16[256,768]{1,0:T(8,128)(2,1)} %shard_map.118, bf16[768,1536]{1,0:T(8,128)(2,1)S(1)} %copy-done, bf16[256,1536]{1,0:T(8,128)(2,1)} %param.12), kind=kOutput, calls=%fused_computation.3 | convolution fusion | flops 605159424 | bytes 4325376 | tf_op jit(solution)/shard_map/dot_general | solution.py:141
  122.3 1.9 %collective-permute-start.16 = (bf16[15,1536]{1,0:T(8,128)(2,1)S(1)}, bf16[15,1536]{1,0:T(8,128)(2,1)S(1)}, u32[]{:S(2)}, u32[]{:S(2)}) collective-permute-start(bf16[15,1536]{1,0:T(8,128)(2,1)S(1)} %get-tuple-element.36), channel_id=1, source_target_pairs={{0,1},{1,2},{2,3},{3,4},{4,5},{5,6},{6,7},{7,8},{8,9},{9,10},{10,1... | collective-permute-start | bytes 138248 | tf_op jit(solution)/shard_map/ppermute | solution.py:24
  124.2 8.0 %collective-permute-start.17 = (bf16[15,1536]{1,0:T(8,128)(2,1)S(1)}, bf16[15,1536]{1,0:T(8,128)(2,1)S(1)}, u32[]{:S(2)}, u32[]{:S(2)}) collective-permute-start(bf16[15,1536]{1,0:T(8,128)(2,1)S(1)} %get-tuple-element.37), channel_id=1, source_target_pairs={{1,0},{2,1},{3,2},{4,3},{5,4},{6,5},{7,6},{8,7},{9,8},{10,9},{11,1... | collective-permute-start | bytes 138248 | tf_op jit(solution)/shard_map/ppermute | solution.py:27
  135.2 15.0 %fusion = bf16[256,1536]{1,0:T(8,128)(2,1)} fusion(bf16[1536,1536]{1,0:T(8,128)(2,1)} %param.23, bf16[256,1536]{1,0:T(8,128)(2,1)S(1)} %fusion.1, f32[286,1536]{1,0:T(8,128)S(1)} %convert_element_type.37, f32[1536]{0:T(1024)} %param.22, f32[1536]{0:T(1024)} %param.21, f32[1536]{0:T(1024)S(1)} %get-tuple-element.34, f32[1536]{0:T(1024)S(1)} %get-tuple-element.35, ...), kind=kOutput, calls=%fused_computation.2 | convolution fusion | flops 1248067584 | bytes 55330304 | tf_op jit(solution)/shard_map/dot_general | solution.py:167
  (141 shorter events, 16.3 us)
Async XLA Ops:
  0.0 119.1 %copy-start = (bf16[768,1536]{1,0:T(8,128)(2,1)S(1)}, bf16[768,1536]{1,0:T(8,128)(2,1)}, u32[]{:S(2)}) copy-start(bf16[768,1536]{1,0:T(8,128)(2,1)} %param.17) | copy-start | bytes 7077892
  0.0 26.7 %collective-permute-start.8 = (bf16[256,768]{1,0:T(8,128)(2,1)}, bf16[256,768]{1,0:T(8,128)(2,1)S(1)}, u32[]{:S(2)}, u32[]{:S(2)}) collective-permute-start(bf16[256,768]{1,0:T(8,128)(2,1)} %refs_13_.1), channel_id=1, source_target_pairs={{0,1},{1,2},{2,3},{3,4},{4,5},{5,6},{6,7},{7,8},{8,9},{9,10},{10,1... | collective-permute-start | bytes 1179656 | tf_op jit(solution)/shard_map/ppermute | solution.py:16
  2.1 26.6 %collective-permute-start.12 = (bf16[256,768]{1,0:T(8,128)(2,1)}, bf16[256,768]{1,0:T(8,128)(2,1)S(1)}, u32[]{:S(2)}, u32[]{:S(2)}) collective-permute-start(bf16[256,768]{1,0:T(8,128)(2,1)} %refs_13_.1), channel_id=1, source_target_pairs={{1,0},{2,1},{3,2},{4,3},{5,4},{6,5},{7,6},{8,7},{9,8},{10,9},{11,1... | collective-permute-start | bytes 1179656 | tf_op jit(solution)/shard_map/ppermute | solution.py:16
  11.3 25.2 %collective-permute-start = (bf16[256,768]{1,0:T(8,128)(2,1)}, bf16[256,768]{1,0:T(8,128)(2,1)S(1)}, u32[]{:S(2)}, u32[]{:S(2)}) collective-permute-start(bf16[256,768]{1,0:T(8,128)(2,1)} %refs_4_.1), channel_id=1, source_target_pairs={{0,1},{1,2},{2,3},{3,4},{4,5},{5,6},{6,7},{7,8},{8,9},{9,10},{10,1... | collective-permute-start | bytes 1179656 | tf_op jit(solution)/shard_map/ppermute | solution.py:16
  13.3 25.2 %collective-permute-start.4 = (bf16[256,768]{1,0:T(8,128)(2,1)}, bf16[256,768]{1,0:T(8,128)(2,1)}, u32[]{:S(2)}, u32[]{:S(2)}) collective-permute-start(bf16[256,768]{1,0:T(8,128)(2,1)} %refs_4_.1), channel_id=1, source_target_pairs={{1,0},{2,1},{3,2},{4,3},{5,4},{6,5},{7,6},{8,7},{9,8},{10,9},{11,1... | collective-permute-start | bytes 1179656 | tf_op jit(solution)/shard_map/ppermute | solution.py:16
  25.8 20.6 %copy-start.24 = (s32[128]{0:T(128)}, s32[128]{0:T(128)S(1)}, u32[]{:S(2)}) copy-start(s32[128]{0:T(128)S(1)} %sub.34) | copy-start | bytes 1540
  26.7 72.2 %copy-start.1 = (bf16[256,768]{1,0:T(8,128)(2,1)}, bf16[256,768]{1,0:T(8,128)(2,1)S(1)}, u32[]{:S(2)}) copy-start(bf16[256,768]{1,0:T(8,128)(2,1)S(1)} %collective-permute-done.8.refs_12_) | copy-start | bytes 1179652
  26.7 23.1 %collective-permute-start.9 = (bf16[256,768]{1,0:T(8,128)(2,1)S(1)}, bf16[256,768]{1,0:T(8,128)(2,1)}, u32[]{:S(2)}, u32[]{:S(2)}) collective-permute-start(bf16[256,768]{1,0:T(8,128)(2,1)S(1)} %collective-permute-done.8.refs_12_), channel_id=1, source_target_pairs={{0,1},{1,2},{2,3},{3,4},{4,5},{5,6},{6,7},{7,8},{8,9},{9,10},{10,1... | collective-permute-start | bytes 1179656 | tf_op jit(solution)/shard_map/ppermute | solution.py:16
  28.6 70.3 %copy-start.2 = (bf16[256,768]{1,0:T(8,128)(2,1)}, bf16[256,768]{1,0:T(8,128)(2,1)S(1)}, u32[]{:S(2)}) copy-start(bf16[256,768]{1,0:T(8,128)(2,1)S(1)} %collective-permute-done.12.refs_14_) | copy-start | bytes 1179652
  28.6 23.1 %collective-permute-start.13 = (bf16[256,768]{1,0:T(8,128)(2,1)S(1)}, bf16[256,768]{1,0:T(8,128)(2,1)}, u32[]{:S(2)}, u32[]{:S(2)}) collective-permute-start(bf16[256,768]{1,0:T(8,128)(2,1)S(1)} %collective-permute-done.12.refs_14_), channel_id=1, source_target_pairs={{1,0},{2,1},{3,2},{4,3},{5,4},{6,5},{7,6},{8,7},{9,8},{10,9},{11,1... | collective-permute-start | bytes 1179656 | tf_op jit(solution)/shard_map/ppermute | solution.py:16
  36.5 62.4 %copy-start.3 = (bf16[256,768]{1,0:T(8,128)(2,1)}, bf16[256,768]{1,0:T(8,128)(2,1)S(1)}, u32[]{:S(2)}) copy-start(bf16[256,768]{1,0:T(8,128)(2,1)S(1)} %collective-permute-done.refs_3_) | copy-start | bytes 1179652
  36.5 23.1 %collective-permute-start.1 = (bf16[256,768]{1,0:T(8,128)(2,1)S(1)}, bf16[256,768]{1,0:T(8,128)(2,1)}, u32[]{:S(2)}, u32[]{:S(2)}) collective-permute-start(bf16[256,768]{1,0:T(8,128)(2,1)S(1)} %collective-permute-done.refs_3_), channel_id=1, source_target_pairs={{0,1},{1,2},{2,3},{3,4},{4,5},{5,6},{6,7},{7,8},{8,9},{9,10},{10,1... | collective-permute-start | bytes 1179656 | tf_op jit(solution)/shard_map/ppermute | solution.py:16
  38.5 23.1 %collective-permute-start.5 = (bf16[256,768]{1,0:T(8,128)(2,1)}, bf16[256,768]{1,0:T(8,128)(2,1)}, u32[]{:S(2)}, u32[]{:S(2)}) collective-permute-start(bf16[256,768]{1,0:T(8,128)(2,1)} %collective-permute-done.4.refs_5_), channel_id=1, source_target_pairs={{1,0},{2,1},{3,2},{4,3},{5,4},{6,5},{7,6},{8,7},{9,8},{10,9},{11,1... | collective-permute-start | bytes 1179656 | tf_op jit(solution)/shard_map/ppermute | solution.py:16
  49.8 22.9 %collective-permute-start.10 = (bf16[256,768]{1,0:T(8,128)(2,1)}, bf16[256,768]{1,0:T(8,128)(2,1)}, u32[]{:S(2)}, u32[]{:S(2)}) collective-permute-start(bf16[256,768]{1,0:T(8,128)(2,1)} %collective-permute-done.9.refs_11_), channel_id=1, source_target_pairs={{0,1},{1,2},{2,3},{3,4},{4,5},{5,6},{6,7},{7,8},{8,9},{9,10},{10,1... | collective-permute-start | bytes 1179656 | tf_op jit(solution)/shard_map/ppermute | solution.py:16
  51.8 22.9 %collective-permute-start.14 = (bf16[256,768]{1,0:T(8,128)(2,1)}, bf16[256,768]{1,0:T(8,128)(2,1)}, u32[]{:S(2)}, u32[]{:S(2)}) collective-permute-start(bf16[256,768]{1,0:T(8,128)(2,1)} %collective-permute-done.13.refs_15_), channel_id=1, source_target_pairs={{1,0},{2,1},{3,2},{4,3},{5,4},{6,5},{7,6},{8,7},{9,8},{10,9},{11,1... | collective-permute-start | bytes 1179656 | tf_op jit(solution)/shard_map/ppermute | solution.py:16
  59.7 22.9 %collective-permute-start.2 = (bf16[256,768]{1,0:T(8,128)(2,1)}, bf16[256,768]{1,0:T(8,128)(2,1)}, u32[]{:S(2)}, u32[]{:S(2)}) collective-permute-start(bf16[256,768]{1,0:T(8,128)(2,1)} %collective-permute-done.1.refs_2_), channel_id=1, source_target_pairs={{0,1},{1,2},{2,3},{3,4},{4,5},{5,6},{6,7},{7,8},{8,9},{9,10},{10,1... | collective-permute-start | bytes 1179656 | tf_op jit(solution)/shard_map/ppermute | solution.py:16
  61.6 22.9 %collective-permute-start.6 = (bf16[256,768]{1,0:T(8,128)(2,1)}, bf16[256,768]{1,0:T(8,128)(2,1)}, u32[]{:S(2)}, u32[]{:S(2)}) collective-permute-start(bf16[256,768]{1,0:T(8,128)(2,1)} %collective-permute-done.5.refs_6_), channel_id=1, source_target_pairs={{1,0},{2,1},{3,2},{4,3},{5,4},{6,5},{7,6},{8,7},{9,8},{10,9},{11,1... | collective-permute-start | bytes 1179656 | tf_op jit(solution)/shard_map/ppermute | solution.py:16
  72.8 26.1 %collective-permute-start.11 = (bf16[256,768]{1,0:T(8,128)(2,1)}, bf16[256,768]{1,0:T(8,128)(2,1)}, u32[]{:S(2)}, u32[]{:S(2)}) collective-permute-start(bf16[256,768]{1,0:T(8,128)(2,1)} %collective-permute-done.10.refs_10_), channel_id=1, source_target_pairs={{0,1},{1,2},{2,3},{3,4},{4,5},{5,6},{6,7},{7,8},{8,9},{9,10},{10,1... | collective-permute-start | bytes 1179656 | tf_op jit(solution)/shard_map/ppermute | solution.py:16
  74.7 24.2 %collective-permute-start.15 = (bf16[256,768]{1,0:T(8,128)(2,1)}, bf16[256,768]{1,0:T(8,128)(2,1)}, u32[]{:S(2)}, u32[]{:S(2)}) collective-permute-start(bf16[256,768]{1,0:T(8,128)(2,1)} %collective-permute-done.14.refs_16_), channel_id=1, source_target_pairs={{1,0},{2,1},{3,2},{4,3},{5,4},{6,5},{7,6},{8,7},{9,8},{10,9},{11,1... | collective-permute-start | bytes 1179656 | tf_op jit(solution)/shard_map/ppermute | solution.py:16
  82.6 16.3 %collective-permute-start.3 = (bf16[256,768]{1,0:T(8,128)(2,1)}, bf16[256,768]{1,0:T(8,128)(2,1)}, u32[]{:S(2)}, u32[]{:S(2)}) collective-permute-start(bf16[256,768]{1,0:T(8,128)(2,1)} %collective-permute-done.2.refs_1_), channel_id=1, source_target_pairs={{0,1},{1,2},{2,3},{3,4},{4,5},{5,6},{6,7},{7,8},{8,9},{9,10},{10,1... | collective-permute-start | bytes 1179656 | tf_op jit(solution)/shard_map/ppermute | solution.py:16
  84.5 14.4 %collective-permute-start.7 = (bf16[256,768]{1,0:T(8,128)(2,1)}, bf16[256,768]{1,0:T(8,128)(2,1)}, u32[]{:S(2)}, u32[]{:S(2)}) collective-permute-start(bf16[256,768]{1,0:T(8,128)(2,1)} %collective-permute-done.6.refs_7_), channel_id=1, source_target_pairs={{1,0},{2,1},{3,2},{4,3},{5,4},{6,5},{7,6},{8,7},{9,8},{10,9},{11,1... | collective-permute-start | bytes 1179656 | tf_op jit(solution)/shard_map/ppermute | solution.py:16
  122.3 11.4 %collective-permute-start.16 = (bf16[15,1536]{1,0:T(8,128)(2,1)S(1)}, bf16[15,1536]{1,0:T(8,128)(2,1)S(1)}, u32[]{:S(2)}, u32[]{:S(2)}) collective-permute-start(bf16[15,1536]{1,0:T(8,128)(2,1)S(1)} %get-tuple-element.36), channel_id=1, source_target_pairs={{0,1},{1,2},{2,3},{3,4},{4,5},{5,6},{6,7},{7,8},{8,9},{9,10},{10,1... | collective-permute-start | bytes 138248 | tf_op jit(solution)/shard_map/ppermute | solution.py:24
  124.2 9.6 %collective-permute-start.17 = (bf16[15,1536]{1,0:T(8,128)(2,1)S(1)}, bf16[15,1536]{1,0:T(8,128)(2,1)S(1)}, u32[]{:S(2)}, u32[]{:S(2)}) collective-permute-start(bf16[15,1536]{1,0:T(8,128)(2,1)S(1)} %get-tuple-element.37), channel_id=1, source_target_pairs={{1,0},{2,1},{3,2},{4,3},{5,4},{6,5},{7,6},{8,7},{9,8},{10,9},{11,1... | collective-permute-start | bytes 138248 | tf_op jit(solution)/shard_map/ppermute | solution.py:27
  134.2 0.8 copy-start.23
  (41 other events, 31.1 us)
where the time goes:
time: 151 us; the launch traced here: 150 us
  starting transfers between devices  89.8 us (59%)
  Pallas kernels  20.2 us (13%)
  matrix products  17 us (11%)
  other arithmetic  12.8 us (8%)
  local copies, waits for them, and re-layouts  9.3 us (6%)
    ppermute x16, starting transfers between devices, shifted_2(): return lax.ppermute(block, axis, route)  79.8 us
    pallas_call x1, Pallas kernels, attend(): pl.pallas_call(attend_kernel, grid=(width // pair,), in_specs=[pl.BlockSp...  20.2 us
    dot_general x1, matrix products, shards(): jnp.dot(act, pointwise_weight, preferred_element_type=jnp.float32)  15 us
    ppermute x1, starting transfers between devices, padded(): lax.ppermute(lax.slice_in_dim(block, 0, width, axis=dim), axis, backward)  8.04 us
    slice x2, local copies, waits for them, and re-layouts, shards(): depthwise_taps[tap]  3.8 us
  transfers between devices with their start and end apart: 18, of which 1 were waited for; matrix products, arithmetic and copies ran while one was open for 13% of the time, Pallas kernels for 0%

commit v1 on v0

--- a/solution.py
+++ b/solution.py
@@ -44,54 +44,126 @@
 NBLK = 2 * REACH + 1
 
 
-def attend_kernel(recq_ref, reck_ref, q_ref, *refs):
+def attend_kernel(flags_ref, recq_ref, reck_ref, q_ref, *refs):
     k_refs = refs[:NBLK]
     v_refs = refs[NBLK : 2 * NBLK]
     out_ref = refs[2 * NBLK]
-    s_scr = refs[2 * NBLK + 1]
+    s_scr, m_scr, l_scr, acc_scr = refs[2 * NBLK + 1 :]
     rec_q = recq_ref[...]
+    others = [j for j in range(NBLK) if j != REACH]
     for hh in range(2):
         cols = slice(hh * HD, (hh + 1) * HD)
         q_h = q_ref[:, cols]
-        top = None
-        for j in range(NBLK):
+
+        def scores(j):
             s = lax.dot_general(
                 q_h, k_refs[j][:, cols], (((1,), (1,)), ((), ())),
                 preferred_element_type=jnp.float32,
             ) * (HD ** (-0.5))
-            s = jnp.where(rec_q == reck_ref[j : j + 1, :], s, -1e30)
-            s_scr[j] = s
-            row = jnp.max(s, axis=1, keepdims=True)
-            top = row if top is None else jnp.maximum(top, row)
-        total = None
-        acc = None
-        for j in range(NBLK):
+            return jnp.where(rec_q == reck_ref[j : j + 1, :], s, -1e30)
+
+        s = scores(REACH)
+        s_scr[REACH] = s
+        m_scr[...] = jnp.max(s, axis=1, keepdims=True)
+        for j in others:
+            @pl.when(flags_ref[j] != 0)
+            def _(j=j):
+                s = scores(j)
+                s_scr[j] = s
+                m_scr[...] = jnp.maximum(m_scr[...], jnp.max(s, axis=1, keepdims=True))
+
+        top = m_scr[...]
+
+        def weigh(j):
             p = jnp.exp(s_scr[j] - top)
             part = jnp.sum(p, axis=1, keepdims=True)
             prod = jnp.dot(p.astype(jnp.bfloat16), v_refs[j][:, cols],
                            preferred_element_type=jnp.float32)
-            total = part if total is None else total + part
-            acc = prod if acc is None else acc + prod
-        out_ref[:, cols] = (acc / total).astype(out_ref.dtype)
-
-
-def attend(rec_q, rec_k, query, keys, vals):
+            return part, prod
+
+        part, prod = weigh(REACH)
+        l_scr[...] = part
+        acc_scr[...] = prod
+        for j in others:
+            @pl.when(flags_ref[j] != 0)
+            def _(j=j):
+                part, prod = weigh(j)
+                l_scr[...] += part
+                acc_scr[...] += prod
+
+        out_ref[:, cols] = (acc_scr[...] / l_scr[...]).astype(out_ref.dtype)
+
+
+def attend(flags, rec_q, rec_k, query, kvs):
     frames, width = query.shape
     pair = 2 * HD
-    tile = pl.BlockSpec((frames, pair), lambda g: (0, g))
+    steps = width // pair
+    q_tile = pl.BlockSpec((frames, pair), lambda g, f: (0, g))
+    k_tile = pl.BlockSpec((frames, pair), lambda g, f: (0, g))
+    v_tile = pl.BlockSpec((frames, pair), lambda g, f: (0, g + steps))
+    grid_spec = pltpu.PrefetchScalarGridSpec(
+        num_scalar_prefetch=1,
+        grid=(steps,),
+        in_specs=[
+            pl.BlockSpec(rec_q.shape, lambda g, f: (0, 0)),
+            pl.BlockSpec(rec_k.shape, lambda g, f: (0, 0)),
+            q_tile,
+        ]
+        + [k_tile] * NBLK
+        + [v_tile] * NBLK,
+        out_specs=q_tile,
+        scratch_shapes=[
+            pltpu.VMEM((NBLK, frames, frames), jnp.float32),
+            pltpu.VMEM((frames, 1), jnp.float32),
+            pltpu.VMEM((frames, 1), jnp.float32),
+            pltpu.VMEM((frames, HD), jnp.float32),
+        ],
+    )
     return pl.pallas_call(
         attend_kernel,
-        grid=(width // pair,),
+        grid_spec=grid_spec,
+        out_shape=jax.ShapeDtypeStruct((frames, width), jnp.bfloat16),
+    )(flags, rec_q, rec_k, query, *kvs, *kvs)
+
+
+CT = 128
+RT = 128
+
+
+def conv_kernel(extrec_ref, ownrec_ref, ext_ref, taps_ref, gain_ref, bias_ref, out_ref, x_scr):
+    x_scr[...] = ext_ref[...].astype(jnp.float32)
+    frames = out_ref.shape[0]
+    ntaps = taps_ref.shape[0]
+    for r0 in range(0, frames, RT):
+        own = ownrec_ref[r0 : r0 + RT, :]
+        acc = jnp.zeros((RT, out_ref.shape[1]), jnp.float32)
+        for j in range(ntaps):
+            same = extrec_ref[r0 + j : r0 + j + RT, :] == own
+            acc = acc + jnp.where(same, x_scr[r0 + j : r0 + j + RT, :] * taps_ref[j : j + 1, :], 0.0)
+        y = acc * gain_ref[...] + bias_ref[...]
+        out_ref[r0 : r0 + RT, :] = (y / (1.0 + jnp.exp(-y))).astype(out_ref.dtype)
+
+
+def depthwise(ext_rec, own_rec, ext, taps, gain, bias):
+    rows, width = ext.shape
+    frames = own_rec.shape[0]
+    ntaps = taps.shape[0]
+    col = lambda c: (0, c)
+    return pl.pallas_call(
+        conv_kernel,
+        grid=(width // CT,),
         in_specs=[
-            pl.BlockSpec(rec_q.shape, lambda g: (0, 0)),
-            pl.BlockSpec(rec_k.shape, lambda g: (0, 0)),
-            tile,
-        ]
-        + [tile] * (2 * NBLK),
-        out_specs=tile,
+            pl.BlockSpec(ext_rec.shape, lambda c: (0, 0)),
+            pl.BlockSpec(own_rec.shape, lambda c: (0, 0)),
+            pl.BlockSpec((rows, CT), col),
+            pl.BlockSpec((ntaps, CT), col),
+            pl.BlockSpec((1, CT), col),
+            pl.BlockSpec((1, CT), col),
+        ],
+        out_specs=pl.BlockSpec((frames, CT), col),
         out_shape=jax.ShapeDtypeStruct((frames, width), jnp.bfloat16),
-        scratch_shapes=[pltpu.VMEM((NBLK, frames, frames), jnp.float32)],
-    )(rec_q, rec_k, query, *keys, *vals)
+        scratch_shapes=[pltpu.VMEM((rows, CT), jnp.float32)],
+    )(ext_rec, own_rec, ext, taps, gain, bias)
 
 
 def shards(
@@ -124,20 +196,21 @@
     rows = -(-NBLK // 8) * 8
     key_rec = jnp.pad(key_rec, ((0, rows - NBLK), (0, 0)), constant_values=-1)
 
-    before_k, before_v, after_k, after_v = [], [], [], []
-    moving = (key_vectors, values)
+    own_kv = jnp.concatenate([key_vectors, values], axis=1)
+    before, after = [], []
+    moving = own_kv
     for distance in range(1, REACH + 1):
         moving = from_before(moving)
-        before_k.append(moving[0])
-        before_v.append(moving[1])
-    moving = (key_vectors, values)
+        before.append(moving)
+    moving = own_kv
     for distance in range(1, REACH + 1):
         moving = from_after(moving)
-        after_k.append(moving[0])
-        after_v.append(moving[1])
-    keys = before_k[::-1] + [key_vectors] + after_k
-    vals = before_v[::-1] + [values] + after_v
-    attended = attend(own_rec[:, None], key_rec, queries, keys, vals)
+        after.append(moving)
+    kvs = before[::-1] + [own_kv] + after
+    first_rec = key_rec[:NBLK, 0]
+    last_rec = key_rec[:NBLK, frames - 1]
+    flags = (key_inside[:, 0] & (first_rec <= own_rec[frames - 1]) & (last_rec >= own_rec[0]))
+    attended = attend(flags.astype(jnp.int32), own_rec[:, None], key_rec, queries, kvs)
     projected = jnp.dot(attended, output_weight, preferred_element_type=jnp.float32)
     resid = lax.optimization_barrier(
         (features.astype(jnp.float32) + projected).astype(jnp.bfloat16)
@@ -155,15 +228,13 @@
     )
     ext_inside = (ext_positions >= 0) & (ext_positions < nblocks * frames)
     ext_rec = jnp.where(ext_inside, segment_of(ext_positions, starts), -1)
-    extended32 = lax.optimization_barrier(extended).astype(jnp.float32)
-    summed = jnp.zeros((frames, normed.shape[1]), jnp.float32)
-    for tap in range(depthwise_taps.shape[0]):
-        same_rec = (ext_rec[tap : tap + frames] == own_rec)[:, None]
-        summed = summed + jnp.where(
-            same_rec, extended32[tap : tap + frames] * depthwise_taps[tap], 0.0
-        )
-    shifted = summed * conv_gain + conv_bias
-    act = (shifted * jax.nn.sigmoid(shifted)).astype(jnp.bfloat16)
+    rows = -(-(frames + 2 * rim_width) // 16) * 16
+    ext = jnp.pad(extended, ((0, rows - extended.shape[0]), (0, 0)))
+    ext_rec = jnp.pad(ext_rec, (0, rows - ext_rec.shape[0]), constant_values=-1)
+    act = depthwise(
+        ext_rec[:, None], own_rec[:, None], ext, depthwise_taps,
+        conv_gain[None, :], conv_bias[None, :],
+    )
     return (resid32 + jnp.dot(act, pointwise_weight, preferred_element_type=jnp.float32)).astype(
         jnp.bfloat16
     )

time: 151 us -> 169 us (1.12)
  the two profiles are of different devices: /device:TPU:16 before, /device:TPU:4 now
where the time goes in v1:
time: 169 us
  starting transfers between devices  68.4 us (40%)
  Pallas kernels  52.9 us (31%)
  waiting for transfers between devices  27.3 us (16%)
  matrix products  6.88 us (4%)
  local copies, waits for them, and re-layouts  6.47 us (4%)
  other arithmetic  6.29 us (4%)
    pallas_call x1, Pallas kernels, attend(): pl.pallas_call(attend_kernel, grid_spec=grid_spec, out_shape=jax.ShapeDty...  36.2 us
    ppermute x8, starting transfers between devices, shifted_2(): return lax.ppermute(block, axis, route)  35.8 us
    ppermute x1, starting transfers between devices, padded(): lax.ppermute(lax.slice_in_dim(block, 0, width, axis=dim), axis, backward)  30.7 us
    ppermute x8, waiting for transfers between devices, shifted_2(): return lax.ppermute(block, axis, route)  27.3 us
    pallas_call x1, Pallas kernels, depthwise(): pl.pallas_call(conv_kernel, grid=(width // CT,), in_specs=[pl.BlockSpec(e...  16.7 us
    dot_general x1, matrix products, shards(): jnp.dot(act, pointwise_weight, preferred_element_type=jnp.float32)  4.85 us
  transfers between devices with their start and end apart: 10, of which 5 were waited for; matrix products, arithmetic and copies ran while one was open for 5% of the time, Pallas kernels for 0%

profile of v1, /device:TPU:4, one launch (start us, length us, event | category | flops | bytes accessed | tf_op | source)
XLA Modules:
  0.0 168.6 jit_solution(8384679615105336765)
XLA Ops:
  0.0 1.2 constant_dynamic-update-slice_fusion.1
  1.2 1.0 constant_dynamic-update-slice_fusion.refs_4_.refs_13_
  2.2 1.9 %collective-permute-start = (bf16[256,1536]{1,0:T(8,128)(2,1)S(1)}, bf16[256,1536]{1,0:T(8,128)(2,1)}, u32[]{:S(2)}, u32[]{:S(2)}) collective-permute-start(bf16[256,1536]{1,0:T(8,128)(2,1)S(1)} %constant_dynamic-update-slice_fusion.refs_4_.refs_13_), channel_id=1, source_target_pairs={{0,1},{1,2},{2,3},{3,4},{4,5},{5,6},{6,7},{7,8},{8,9},{9,10},{10,1... | collective-permute-start | bytes 2359304 | tf_op jit(solution)/shard_map/ppermute | solution.py:16
  4.2 8.2 %collective-permute-start.4 = (bf16[256,1536]{1,0:T(8,128)(2,1)S(1)}, bf16[256,1536]{1,0:T(8,128)(2,1)}, u32[]{:S(2)}, u32[]{:S(2)}) collective-permute-start(bf16[256,1536]{1,0:T(8,128)(2,1)S(1)} %constant_dynamic-update-slice_fusion.refs_4_.refs_13_), channel_id=1, source_target_pairs={{1,0},{2,1},{3,2},{4,3},{5,4},{6,5},{7,6},{8,7},{9,8},{10,9},{11,1... | collective-permute-start | bytes 2359304 | tf_op jit(solution)/shard_map/ppermute | solution.py:16
  12.4 7.8 %collective-permute-done.refs_3_.refs_12_ = bf16[256,1536]{1,0:T(8,128)(2,1)} collective-permute-done((bf16[256,1536]{1,0:T(8,128)(2,1)S(1)}, bf16[256,1536]{1,0:T(8,128)(2,1)}, u32[]{:S(2)}, u32[]{:S(2)}) %collective-permute-start) | collective-permute-done | bytes 786464 | tf_op jit(solution)/shard_map/ppermute | solution.py:16
  20.2 1.9 %collective-permute-start.1 = (bf16[256,1536]{1,0:T(8,128)(2,1)}, bf16[256,1536]{1,0:T(8,128)(2,1)}, u32[]{:S(2)}, u32[]{:S(2)}) collective-permute-start(bf16[256,1536]{1,0:T(8,128)(2,1)} %collective-permute-done.refs_3_.refs_12_), channel_id=1, source_target_pairs={{0,1},{1,2},{2,3},{3,4},{4,5},{5,6},{6,7},{7,8},{8,9},{9,10},{10,1... | collective-permute-start | bytes 2359304 | tf_op jit(solution)/shard_map/ppermute | solution.py:16
  22.1 6.7 %collective-permute-start.5 = (bf16[256,1536]{1,0:T(8,128)(2,1)}, bf16[256,1536]{1,0:T(8,128)(2,1)}, u32[]{:S(2)}, u32[]{:S(2)}) collective-permute-start(bf16[256,1536]{1,0:T(8,128)(2,1)} %collective-permute-done.4.refs_5_.refs_14_), channel_id=1, source_target_pairs={{1,0},{2,1},{3,2},{4,3},{5,4},{6,5},{7,6},{8,7},{9,8},{10,9},{11,1... | collective-permute-start | bytes 2359304 | tf_op jit(solution)/shard_map/ppermute | solution.py:16
  29.3 1.5 convert_reduce_fusion.1
  30.8 6.1 %collective-permute-done.1.refs_2_.refs_11_ = bf16[256,1536]{1,0:T(8,128)(2,1)} collective-permute-done((bf16[256,1536]{1,0:T(8,128)(2,1)}, bf16[256,1536]{1,0:T(8,128)(2,1)}, u32[]{:S(2)}, u32[]{:S(2)}) %collective-permute-start.1) | collective-permute-done | bytes 786464 | tf_op jit(solution)/shard_map/ppermute | solution.py:16
  36.8 1.9 %collective-permute-start.2 = (bf16[256,1536]{1,0:T(8,128)(2,1)}, bf16[256,1536]{1,0:T(8,128)(2,1)}, u32[]{:S(2)}, u32[]{:S(2)}) collective-permute-start(bf16[256,1536]{1,0:T(8,128)(2,1)} %collective-permute-done.1.refs_2_.refs_11_), channel_id=1, source_target_pairs={{0,1},{1,2},{2,3},{3,4},{4,5},{5,6},{6,7},{7,8},{8,9},{9,10},{10,1... | collective-permute-start | bytes 2359304 | tf_op jit(solution)/shard_map/ppermute | solution.py:16
  38.7 6.7 %collective-permute-start.6 = (bf16[256,1536]{1,0:T(8,128)(2,1)}, bf16[256,1536]{1,0:T(8,128)(2,1)}, u32[]{:S(2)}, u32[]{:S(2)}) collective-permute-start(bf16[256,1536]{1,0:T(8,128)(2,1)} %collective-permute-done.5.refs_6_.refs_15_), channel_id=1, source_target_pairs={{1,0},{2,1},{3,2},{4,3},{5,4},{6,5},{7,6},{8,7},{9,8},{10,9},{11,1... | collective-permute-start | bytes 2359304 | tf_op jit(solution)/shard_map/ppermute | solution.py:16
  45.7 7.7 %collective-permute-done.2.refs_1_.refs_10_ = bf16[256,1536]{1,0:T(8,128)(2,1)} collective-permute-done((bf16[256,1536]{1,0:T(8,128)(2,1)}, bf16[256,1536]{1,0:T(8,128)(2,1)}, u32[]{:S(2)}, u32[]{:S(2)}) %collective-permute-start.2) | collective-permute-done | bytes 786464 | tf_op jit(solution)/shard_map/ppermute | solution.py:16
  53.4 1.9 %collective-permute-start.3 = (bf16[256,1536]{1,0:T(8,128)(2,1)}, bf16[256,1536]{1,0:T(8,128)(2,1)}, u32[]{:S(2)}, u32[]{:S(2)}) collective-permute-start(bf16[256,1536]{1,0:T(8,128)(2,1)} %collective-permute-done.2.refs_1_.refs_10_), channel_id=1, source_target_pairs={{0,1},{1,2},{2,3},{3,4},{4,5},{5,6},{6,7},{7,8},{8,9},{9,10},{10,1... | collective-permute-start | bytes 2359304 | tf_op jit(solution)/shard_map/ppermute | solution.py:16
  55.4 6.7 %collective-permute-start.7 = (bf16[256,1536]{1,0:T(8,128)(2,1)}, bf16[256,1536]{1,0:T(8,128)(2,1)}, u32[]{:S(2)}, u32[]{:S(2)}) collective-permute-start(bf16[256,1536]{1,0:T(8,128)(2,1)} %collective-permute-done.6.refs_7_.refs_16_), channel_id=1, source_target_pairs={{1,0},{2,1},{3,2},{4,3},{5,4},{6,5},{7,6},{8,7},{9,8},{10,9},{11,1... | collective-permute-start | bytes 2359304 | tf_op jit(solution)/shard_map/ppermute | solution.py:16
  64.1 1.4 fusion.13
  66.2 3.9 %collective-permute-done.3.refs_0_.refs_9_ = bf16[256,1536]{1,0:T(8,128)(2,1)} collective-permute-done((bf16[256,1536]{1,0:T(8,128)(2,1)}, bf16[256,1536]{1,0:T(8,128)(2,1)}, u32[]{:S(2)}, u32[]{:S(2)}) %collective-permute-start.3) | collective-permute-done | bytes 786464 | tf_op jit(solution)/shard_map/ppermute | solution.py:16
  70.1 1.8 %collective-permute-done.7.refs_8_.refs_17_ = bf16[256,1536]{1,0:T(8,128)(2,1)} collective-permute-done((bf16[256,1536]{1,0:T(8,128)(2,1)}, bf16[256,1536]{1,0:T(8,128)(2,1)}, u32[]{:S(2)}, u32[]{:S(2)}) %collective-permute-start.7) | collective-permute-done | bytes 786464 | tf_op jit(solution)/shard_map/ppermute | solution.py:16
  71.8 36.2 %shard_map.118 = bf16[256,768]{1,0:T(8,128)(2,1)} custom-call(s32[9]{0:T(128)} %and_convert_fusion.flags_ref, s32[256,1]{1,0:T(8,128)} %copy.19.recq_ref.ownrec_ref, s32[16,256]{1,0:T(8,128)} %pad.12.reck_ref, bf16[256,768]{1,0:T(8,128)(2,1)} %q_ref.1, bf16[256,1536]{1,0:T(8,128)(2,1)} %collective-permute-done.3.refs_0_.refs_9_, ...), custom_call_target="tpu_custom_call" | custom-call | tf_op jit(solution)/shard_map/pallas_call | solution.py:122
  108.0 2.0 %fusion.1 = bf16[256,1536]{1,0:T(8,128)(2,1)S(1)} fusion(bf16[256,768]{1,0:T(8,128)(2,1)} %shard_map.118, bf16[768,1536]{1,0:T(8,128)(2,1)S(1)} %copy-done, bf16[256,1536]{1,0:T(8,128)(2,1)} %param.12), kind=kOutput, calls=%fused_computation.3 | convolution fusion | flops 605159424 | bytes 4325376 | tf_op jit(solution)/shard_map/dot_general | solution.py:214
  111.2 1.9 %collective-permute-start.8 = (bf16[15,1536]{1,0:T(8,128)(2,1)S(1)}, bf16[15,1536]{1,0:T(8,128)(2,1)S(1)}, u32[]{:S(2)}, u32[]{:S(2)}) collective-permute-start(bf16[15,1536]{1,0:T(8,128)(2,1)S(1)} %get-tuple-element.7), channel_id=1, source_target_pairs={{0,1},{1,2},{2,3},{3,4},{4,5},{5,6},{6,7},{7,8},{8,9},{9,10},{10,1... | collective-permute-start | bytes 138248 | tf_op jit(solution)/shard_map/ppermute | solution.py:24
  113.1 30.7 %collective-permute-start.9 = (bf16[15,1536]{1,0:T(8,128)(2,1)S(1)}, bf16[15,1536]{1,0:T(8,128)(2,1)S(1)}, u32[]{:S(2)}, u32[]{:S(2)}) collective-permute-start(bf16[15,1536]{1,0:T(8,128)(2,1)S(1)} %get-tuple-element.8), channel_id=1, source_target_pairs={{1,0},{2,1},{3,2},{4,3},{5,4},{6,5},{7,6},{8,7},{9,8},{10,9},{11,1... | collective-permute-start | bytes 138248 | tf_op jit(solution)/shard_map/ppermute | solution.py:27
  145.9 1.1 fusion.12.ext_ref
  147.0 16.7 %shard_map.119 = bf16[256,1536]{1,0:T(8,128)(2,1)} custom-call(s32[288,1]{1,0:T(8,128)} %broadcast_in_dim.21.extrec_ref, s32[256,1]{1,0:T(8,128)} %copy.19.recq_ref.ownrec_ref, bf16[288,1536]{1,0:T(8,128)(2,1)} %fusion.12.ext_ref, f32[31,1536]{1,0:T(8,128)} %taps_ref.1, f32[1,1536]{1,0:T(1,128)} %broadcast_in_dim.19.gain_ref, ...), custom_call_target="tpu_custom_call" | custom-call | tf_op jit(solution)/shard_map/pallas_call | solution.py:152
  163.7 4.8 %fusion = bf16[256,1536]{1,0:T(8,128)(2,1)} fusion(bf16[256,1536]{1,0:T(8,128)(2,1)} %shard_map.119, bf16[1536,1536]{1,0:T(8,128)(2,1)} %param.23, bf16[256,1536]{1,0:T(8,128)(2,1)S(1)} %fusion.1), kind=kOutput, calls=%fused_computation.2 | convolution fusion | flops 1209139200 | bytes 7077888 | tf_op jit(solution)/shard_map/dot_general | solution.py:238
  (50 shorter events, 6.6 us)
Async XLA Ops:
  0.0 108.0 %copy-start = (bf16[768,1536]{1,0:T(8,128)(2,1)S(1)}, bf16[768,1536]{1,0:T(8,128)(2,1)}, u32[]{:S(2)}) copy-start(bf16[768,1536]{1,0:T(8,128)(2,1)} %param.17) | copy-start | bytes 7077892
  0.0 28.9 %copy-start.6 = (s32[128]{0:T(128)S(1)}, s32[128]{0:T(128)}, u32[]{:S(2)}) copy-start(s32[128]{0:T(128)} %param.16) | copy-start | bytes 1540
  2.2 69.6 %copy-start.1 = (bf16[256,1536]{1,0:T(8,128)(2,1)}, bf16[256,1536]{1,0:T(8,128)(2,1)S(1)}, u32[]{:S(2)}) copy-start(bf16[256,1536]{1,0:T(8,128)(2,1)S(1)} %constant_dynamic-update-slice_fusion.refs_4_.refs_13_) | copy-start | bytes 2359300
  2.2 18.0 %collective-permute-start = (bf16[256,1536]{1,0:T(8,128)(2,1)S(1)}, bf16[256,1536]{1,0:T(8,128)(2,1)}, u32[]{:S(2)}, u32[]{:S(2)}) collective-permute-start(bf16[256,1536]{1,0:T(8,128)(2,1)S(1)} %constant_dynamic-update-slice_fusion.refs_4_.refs_13_), channel_id=1, source_target_pairs={{0,1},{1,2},{2,3},{3,4},{4,5},{5,6},{6,7},{7,8},{8,9},{9,10},{10,1... | collective-permute-start | bytes 2359304 | tf_op jit(solution)/shard_map/ppermute | solution.py:16
  4.2 18.0 %collective-permute-start.4 = (bf16[256,1536]{1,0:T(8,128)(2,1)S(1)}, bf16[256,1536]{1,0:T(8,128)(2,1)}, u32[]{:S(2)}, u32[]{:S(2)}) collective-permute-start(bf16[256,1536]{1,0:T(8,128)(2,1)S(1)} %constant_dynamic-update-slice_fusion.refs_4_.refs_13_), channel_id=1, source_target_pairs={{1,0},{2,1},{3,2},{4,3},{5,4},{6,5},{7,6},{8,7},{9,8},{10,9},{11,1... | collective-permute-start | bytes 2359304 | tf_op jit(solution)/shard_map/ppermute | solution.py:16
  20.2 16.6 %collective-permute-start.1 = (bf16[256,1536]{1,0:T(8,128)(2,1)}, bf16[256,1536]{1,0:T(8,128)(2,1)}, u32[]{:S(2)}, u32[]{:S(2)}) collective-permute-start(bf16[256,1536]{1,0:T(8,128)(2,1)} %collective-permute-done.refs_3_.refs_12_), channel_id=1, source_target_pairs={{0,1},{1,2},{2,3},{3,4},{4,5},{5,6},{6,7},{7,8},{8,9},{9,10},{10,1... | collective-permute-start | bytes 2359304 | tf_op jit(solution)/shard_map/ppermute | solution.py:16
  22.1 16.6 %collective-permute-start.5 = (bf16[256,1536]{1,0:T(8,128)(2,1)}, bf16[256,1536]{1,0:T(8,128)(2,1)}, u32[]{:S(2)}, u32[]{:S(2)}) collective-permute-start(bf16[256,1536]{1,0:T(8,128)(2,1)} %collective-permute-done.4.refs_5_.refs_14_), channel_id=1, source_target_pairs={{1,0},{2,1},{3,2},{4,3},{5,4},{6,5},{7,6},{8,7},{9,8},{10,9},{11,1... | collective-permute-start | bytes 2359304 | tf_op jit(solution)/shard_map/ppermute | solution.py:16
  36.8 16.6 %collective-permute-start.2 = (bf16[256,1536]{1,0:T(8,128)(2,1)}, bf16[256,1536]{1,0:T(8,128)(2,1)}, u32[]{:S(2)}, u32[]{:S(2)}) collective-permute-start(bf16[256,1536]{1,0:T(8,128)(2,1)} %collective-permute-done.1.refs_2_.refs_11_), channel_id=1, source_target_pairs={{0,1},{1,2},{2,3},{3,4},{4,5},{5,6},{6,7},{7,8},{8,9},{9,10},{10,1... | collective-permute-start | bytes 2359304 | tf_op jit(solution)/shard_map/ppermute | solution.py:16
  38.7 16.6 %collective-permute-start.6 = (bf16[256,1536]{1,0:T(8,128)(2,1)}, bf16[256,1536]{1,0:T(8,128)(2,1)}, u32[]{:S(2)}, u32[]{:S(2)}) collective-permute-start(bf16[256,1536]{1,0:T(8,128)(2,1)} %collective-permute-done.5.refs_6_.refs_15_), channel_id=1, source_target_pairs={{1,0},{2,1},{3,2},{4,3},{5,4},{6,5},{7,6},{8,7},{9,8},{10,9},{11,1... | collective-permute-start | bytes 2359304 | tf_op jit(solution)/shard_map/ppermute | solution.py:16
  53.4 16.6 %collective-permute-start.3 = (bf16[256,1536]{1,0:T(8,128)(2,1)}, bf16[256,1536]{1,0:T(8,128)(2,1)}, u32[]{:S(2)}, u32[]{:S(2)}) collective-permute-start(bf16[256,1536]{1,0:T(8,128)(2,1)} %collective-permute-done.2.refs_1_.refs_10_), channel_id=1, source_target_pairs={{0,1},{1,2},{2,3},{3,4},{4,5},{5,6},{6,7},{7,8},{8,9},{9,10},{10,1... | collective-permute-start | bytes 2359304 | tf_op jit(solution)/shard_map/ppermute | solution.py:16
  55.4 16.5 %collective-permute-start.7 = (bf16[256,1536]{1,0:T(8,128)(2,1)}, bf16[256,1536]{1,0:T(8,128)(2,1)}, u32[]{:S(2)}, u32[]{:S(2)}) collective-permute-start(bf16[256,1536]{1,0:T(8,128)(2,1)} %collective-permute-done.6.refs_7_.refs_16_), channel_id=1, source_target_pairs={{1,0},{2,1},{3,2},{4,3},{5,4},{6,5},{7,6},{8,7},{9,8},{10,9},{11,1... | collective-permute-start | bytes 2359304 | tf_op jit(solution)/shard_map/ppermute | solution.py:16
  110.1 0.7 copy-start.2
  110.1 0.7 copy-start.3
  110.1 34.6 %copy-start.4 = (f32[1536]{0:T(1024)S(1)}, f32[1536]{0:T(1024)}, u32[]{:S(2)}) copy-start(f32[1536]{0:T(1024)} %param.21) | copy-start | bytes 18436
  110.3 35.0 %copy-start.5 = (f32[1536]{0:T(1024)S(1)}, f32[1536]{0:T(1024)}, u32[]{:S(2)}) copy-start(f32[1536]{0:T(1024)} %param.22) | copy-start | bytes 18436
  111.2 34.7 %collective-permute-start.8 = (bf16[15,1536]{1,0:T(8,128)(2,1)S(1)}, bf16[15,1536]{1,0:T(8,128)(2,1)S(1)}, u32[]{:S(2)}, u32[]{:S(2)}) collective-permute-start(bf16[15,1536]{1,0:T(8,128)(2,1)S(1)} %get-tuple-element.7), channel_id=1, source_target_pairs={{0,1},{1,2},{2,3},{3,4},{4,5},{5,6},{6,7},{7,8},{8,9},{9,10},{10,1... | collective-permute-start | bytes 138248 | tf_op jit(solution)/shard_map/ppermute | solution.py:24
  113.1 32.7 %collective-permute-start.9 = (bf16[15,1536]{1,0:T(8,128)(2,1)S(1)}, bf16[15,1536]{1,0:T(8,128)(2,1)S(1)}, u32[]{:S(2)}, u32[]{:S(2)}) collective-permute-start(bf16[15,1536]{1,0:T(8,128)(2,1)S(1)} %get-tuple-element.8), channel_id=1, source_target_pairs={{1,0},{2,1},{3,2},{4,3},{5,4},{6,5},{7,6},{8,7},{9,8},{10,9},{11,1... | collective-permute-start | bytes 138248 | tf_op jit(solution)/shard_map/ppermute | solution.py:27

commit v2 on v0

--- a/solution.py
+++ b/solution.py
@@ -163,7 +163,7 @@
             same_rec, extended32[tap : tap + frames] * depthwise_taps[tap], 0.0
         )
     shifted = summed * conv_gain + conv_bias
-    act = (shifted * jax.nn.sigmoid(shifted)).astype(jnp.bfloat16)
+    act = lax.optimization_barrier((shifted * jax.nn.sigmoid(shifted)).astype(jnp.bfloat16))
     return (resid32 + jnp.dot(act, pointwise_weight, preferred_element_type=jnp.float32)).astype(
         jnp.bfloat16
     )

time: 151 us -> 151 us (level)
  matrix products: 17 us -> 6.64 us
  other arithmetic: 12.8 us -> 22.6 us
    dot_general x1, matrix products: 15 us -> 4.6 us  [shards(): jnp.dot(act, pointwise_weight, preferred_element_type=jnp.float32)]
    convert_element_type x0 -> x1, other arithmetic: none -> 9.8 us  [shards(): (shifted * jax.nn.sigmoid(shifted)).astype(jnp.bfloat16)]
  transfers between devices with their start and end apart: 18 -> 18, of which waited for: 1 -> 1; matrix products, arithmetic and copies ran while one was open for 13% -> 14% of each run, Pallas kernels for 0% -> 0%
where the time goes in v2:
time: 151 us; the launch traced here: 150 us
  starting transfers between devices  89.6 us (59%)
  other arithmetic  22.6 us (15%)
  Pallas kernels  20.1 us (13%)
  local copies, waits for them, and re-layouts  9.62 us (6%)
  matrix products  6.64 us (4%)
    ppermute x16, starting transfers between devices, shifted_2(): return lax.ppermute(block, axis, route)  79.8 us
    pallas_call x1, Pallas kernels, attend(): pl.pallas_call(attend_kernel, grid=(width // pair,), in_specs=[pl.BlockSp...  20.1 us
    convert_element_type x1, other arithmetic, shards(): (shifted * jax.nn.sigmoid(shifted)).astype(jnp.bfloat16)  9.8 us
    ppermute x1, starting transfers between devices, padded(): lax.ppermute(lax.slice_in_dim(block, 0, width, axis=dim), axis, backward)  7.86 us
    dot_general x1, matrix products, shards(): jnp.dot(act, pointwise_weight, preferred_element_type=jnp.float32)  4.6 us
    slice x2, local copies, waits for them, and re-layouts, shards(): depthwise_taps[tap]  4.09 us
  transfers between devices with their start and end apart: 18, of which 1 were waited for; matrix products, arithmetic and copies ran while one was open for 14% of the time, Pallas kernels for 0%

profile of v2, /device:TPU:16, one launch (start us, length us, event | category | flops | bytes accessed | tf_op | source)
XLA Modules:
  0.0 149.7 jit_solution(15456652583403095901)
XLA Ops:
  0.0 2.0 %collective-permute-start.8 = (bf16[256,768]{1,0:T(8,128)(2,1)}, bf16[256,768]{1,0:T(8,128)(2,1)S(1)}, u32[]{:S(2)}, u32[]{:S(2)}) collective-permute-start(bf16[256,768]{1,0:T(8,128)(2,1)} %refs_13_.1), channel_id=1, source_target_pairs={{0,1},{1,2},{2,3},{3,4},{4,5},{5,6},{6,7},{7,8},{8,9},{9,10},{10,1... | collective-permute-start | bytes 1179656 | tf_op jit(solution)/shard_map/ppermute | solution.py:16
  2.1 9.3 %collective-permute-start.12 = (bf16[256,768]{1,0:T(8,128)(2,1)}, bf16[256,768]{1,0:T(8,128)(2,1)S(1)}, u32[]{:S(2)}, u32[]{:S(2)}) collective-permute-start(bf16[256,768]{1,0:T(8,128)(2,1)} %refs_13_.1), channel_id=1, source_target_pairs={{1,0},{2,1},{3,2},{4,3},{5,4},{6,5},{7,6},{8,7},{9,8},{10,9},{11,1... | collective-permute-start | bytes 1179656 | tf_op jit(solution)/shard_map/ppermute | solution.py:16
  11.3 1.9 %collective-permute-start = (bf16[256,768]{1,0:T(8,128)(2,1)}, bf16[256,768]{1,0:T(8,128)(2,1)S(1)}, u32[]{:S(2)}, u32[]{:S(2)}) collective-permute-start(bf16[256,768]{1,0:T(8,128)(2,1)} %refs_4_.1), channel_id=1, source_target_pairs={{0,1},{1,2},{2,3},{3,4},{4,5},{5,6},{6,7},{7,8},{8,9},{9,10},{10,1... | collective-permute-start | bytes 1179656 | tf_op jit(solution)/shard_map/ppermute | solution.py:16
  13.3 7.9 %collective-permute-start.4 = (bf16[256,768]{1,0:T(8,128)(2,1)}, bf16[256,768]{1,0:T(8,128)(2,1)}, u32[]{:S(2)}, u32[]{:S(2)}) collective-permute-start(bf16[256,768]{1,0:T(8,128)(2,1)} %refs_4_.1), channel_id=1, source_target_pairs={{1,0},{2,1},{3,2},{4,3},{5,4},{6,5},{7,6},{8,7},{9,8},{10,9},{11,1... | collective-permute-start | bytes 1179656 | tf_op jit(solution)/shard_map/ppermute | solution.py:16
  26.7 1.9 %collective-permute-start.9 = (bf16[256,768]{1,0:T(8,128)(2,1)S(1)}, bf16[256,768]{1,0:T(8,128)(2,1)}, u32[]{:S(2)}, u32[]{:S(2)}) collective-permute-start(bf16[256,768]{1,0:T(8,128)(2,1)S(1)} %collective-permute-done.8.refs_12_), channel_id=1, source_target_pairs={{0,1},{1,2},{2,3},{3,4},{4,5},{5,6},{6,7},{7,8},{8,9},{9,10},{10,1... | collective-permute-start | bytes 1179656 | tf_op jit(solution)/shard_map/ppermute | solution.py:16
  28.6 7.9 %collective-permute-start.13 = (bf16[256,768]{1,0:T(8,128)(2,1)S(1)}, bf16[256,768]{1,0:T(8,128)(2,1)}, u32[]{:S(2)}, u32[]{:S(2)}) collective-permute-start(bf16[256,768]{1,0:T(8,128)(2,1)S(1)} %collective-permute-done.12.refs_14_), channel_id=1, source_target_pairs={{1,0},{2,1},{3,2},{4,3},{5,4},{6,5},{7,6},{8,7},{9,8},{10,9},{11,1... | collective-permute-start | bytes 1179656 | tf_op jit(solution)/shard_map/ppermute | solution.py:16
  36.5 1.9 %collective-permute-start.1 = (bf16[256,768]{1,0:T(8,128)(2,1)S(1)}, bf16[256,768]{1,0:T(8,128)(2,1)}, u32[]{:S(2)}, u32[]{:S(2)}) collective-permute-start(bf16[256,768]{1,0:T(8,128)(2,1)S(1)} %collective-permute-done.refs_3_), channel_id=1, source_target_pairs={{0,1},{1,2},{2,3},{3,4},{4,5},{5,6},{6,7},{7,8},{8,9},{9,10},{10,1... | collective-permute-start | bytes 1179656 | tf_op jit(solution)/shard_map/ppermute | solution.py:16
  38.5 7.9 %collective-permute-start.5 = (bf16[256,768]{1,0:T(8,128)(2,1)}, bf16[256,768]{1,0:T(8,128)(2,1)}, u32[]{:S(2)}, u32[]{:S(2)}) collective-permute-start(bf16[256,768]{1,0:T(8,128)(2,1)} %collective-permute-done.4.refs_5_), channel_id=1, source_target_pairs={{1,0},{2,1},{3,2},{4,3},{5,4},{6,5},{7,6},{8,7},{9,8},{10,9},{11,1... | collective-permute-start | bytes 1179656 | tf_op jit(solution)/shard_map/ppermute | solution.py:16
  47.8 2.0 %convert_reduce_fusion.1 = s32[2304]{0:T(1024)S(1)} fusion(s32[128]{0:T(128)} %copy-done.26, s32[2304]{0:T(1024)S(1)} %add.217), kind=kLoop, calls=%fused_computation.107 | loop fusion | flops 882432 | bytes 18944 | tf_op jit(solution)/shard_map/reduce_sum | solution.py:33
  49.8 1.9 %collective-permute-start.10 = (bf16[256,768]{1,0:T(8,128)(2,1)}, bf16[256,768]{1,0:T(8,128)(2,1)}, u32[]{:S(2)}, u32[]{:S(2)}) collective-permute-start(bf16[256,768]{1,0:T(8,128)(2,1)} %collective-permute-done.9.refs_11_), channel_id=1, source_target_pairs={{0,1},{1,2},{2,3},{3,4},{4,5},{5,6},{6,7},{7,8},{8,9},{9,10},{10,1... | collective-permute-start | bytes 1179656 | tf_op jit(solution)/shard_map/ppermute | solution.py:16
  51.8 7.9 %collective-permute-start.14 = (bf16[256,768]{1,0:T(8,128)(2,1)}, bf16[256,768]{1,0:T(8,128)(2,1)}, u32[]{:S(2)}, u32[]{:S(2)}) collective-permute-start(bf16[256,768]{1,0:T(8,128)(2,1)} %collective-permute-done.13.refs_15_), channel_id=1, source_target_pairs={{1,0},{2,1},{3,2},{4,3},{5,4},{6,5},{7,6},{8,7},{9,8},{10,9},{11,1... | collective-permute-start | bytes 1179656 | tf_op jit(solution)/shard_map/ppermute | solution.py:16
  59.7 1.9 %collective-permute-start.2 = (bf16[256,768]{1,0:T(8,128)(2,1)}, bf16[256,768]{1,0:T(8,128)(2,1)}, u32[]{:S(2)}, u32[]{:S(2)}) collective-permute-start(bf16[256,768]{1,0:T(8,128)(2,1)} %collective-permute-done.1.refs_2_), channel_id=1, source_target_pairs={{0,1},{1,2},{2,3},{3,4},{4,5},{5,6},{6,7},{7,8},{8,9},{9,10},{10,1... | collective-permute-start | bytes 1179656 | tf_op jit(solution)/shard_map/ppermute | solution.py:16
  61.6 7.9 %collective-permute-start.6 = (bf16[256,768]{1,0:T(8,128)(2,1)}, bf16[256,768]{1,0:T(8,128)(2,1)}, u32[]{:S(2)}, u32[]{:S(2)}) collective-permute-start(bf16[256,768]{1,0:T(8,128)(2,1)} %collective-permute-done.5.refs_6_), channel_id=1, source_target_pairs={{1,0},{2,1},{3,2},{4,3},{5,4},{6,5},{7,6},{8,7},{9,8},{10,9},{11,1... | collective-permute-start | bytes 1179656 | tf_op jit(solution)/shard_map/ppermute | solution.py:16
  72.8 1.9 %collective-permute-start.11 = (bf16[256,768]{1,0:T(8,128)(2,1)}, bf16[256,768]{1,0:T(8,128)(2,1)}, u32[]{:S(2)}, u32[]{:S(2)}) collective-permute-start(bf16[256,768]{1,0:T(8,128)(2,1)} %collective-permute-done.10.refs_10_), channel_id=1, source_target_pairs={{0,1},{1,2},{2,3},{3,4},{4,5},{5,6},{6,7},{7,8},{8,9},{9,10},{10,1... | collective-permute-start | bytes 1179656 | tf_op jit(solution)/shard_map/ppermute | solution.py:16
  74.7 7.9 %collective-permute-start.15 = (bf16[256,768]{1,0:T(8,128)(2,1)}, bf16[256,768]{1,0:T(8,128)(2,1)}, u32[]{:S(2)}, u32[]{:S(2)}) collective-permute-start(bf16[256,768]{1,0:T(8,128)(2,1)} %collective-permute-done.14.refs_16_), channel_id=1, source_target_pairs={{1,0},{2,1},{3,2},{4,3},{5,4},{6,5},{7,6},{8,7},{9,8},{10,9},{11,1... | collective-permute-start | bytes 1179656 | tf_op jit(solution)/shard_map/ppermute | solution.py:16
  82.6 1.9 %collective-permute-start.3 = (bf16[256,768]{1,0:T(8,128)(2,1)}, bf16[256,768]{1,0:T(8,128)(2,1)}, u32[]{:S(2)}, u32[]{:S(2)}) collective-permute-start(bf16[256,768]{1,0:T(8,128)(2,1)} %collective-permute-done.2.refs_1_), channel_id=1, source_target_pairs={{0,1},{1,2},{2,3},{3,4},{4,5},{5,6},{6,7},{7,8},{8,9},{9,10},{10,1... | collective-permute-start | bytes 1179656 | tf_op jit(solution)/shard_map/ppermute | solution.py:16
  84.5 7.9 %collective-permute-start.7 = (bf16[256,768]{1,0:T(8,128)(2,1)}, bf16[256,768]{1,0:T(8,128)(2,1)}, u32[]{:S(2)}, u32[]{:S(2)}) collective-permute-start(bf16[256,768]{1,0:T(8,128)(2,1)} %collective-permute-done.6.refs_7_), channel_id=1, source_target_pairs={{1,0},{2,1},{3,2},{4,3},{5,4},{6,5},{7,6},{8,7},{9,8},{10,9},{11,1... | collective-permute-start | bytes 1179656 | tf_op jit(solution)/shard_map/ppermute | solution.py:16
  95.1 2.6 %slice_reduce_fusion.30 = (f32[1536]{0:T(1024)S(1)}, f32[1536]{0:T(1024)}, f32[1536]{0:T(1024)}, f32[1536]{0:T(1024)}, f32[1536]{0:T(1024)}, /*index=5*/f32[1536...) fusion(f32[31,1536]{1,0:T(8,128)} %param.20), kind=kLoop, calls=%fused_computation.143 | loop fusion | bytes 233472 | tf_op jit(solution)/shard_map/slice | solution.py:163
  99.1 20.1 %shard_map.118 = bf16[256,768]{1,0:T(8,128)(2,1)} custom-call(s32[256,1]{1,0:T(8,128)} %copy.17.recq_ref, s32[16,256]{1,0:T(8,128)} %pad.4.reck_ref, bf16[256,768]{1,0:T(8,128)(2,1)} %q_ref.1, bf16[256,768]{1,0:T(8,128)(2,1)} %collective-permute-done.3.refs_0_, bf16[256,768]{1,0:T(8,128)(2,1)} %collective-permute-done.2.refs_1_, ...), custom_call_target="tpu_custom_call" | custom-call | tf_op jit(solution)/shard_map/pallas_call | solution.py:82
  119.2 2.0 %fusion.1 = bf16[256,1536]{1,0:T(8,128)(2,1)S(1)} fusion(bf16[256,768]{1,0:T(8,128)(2,1)} %shard_map.118, bf16[768,1536]{1,0:T(8,128)(2,1)S(1)} %copy-done, bf16[256,1536]{1,0:T(8,128)(2,1)} %param.12), kind=kOutput, calls=%fused_computation.3 | convolution fusion | flops 605159424 | bytes 4325376 | tf_op jit(solution)/shard_map/dot_general | solution.py:141
  122.4 1.9 %collective-permute-start.16 = (bf16[15,1536]{1,0:T(8,128)(2,1)S(1)}, bf16[15,1536]{1,0:T(8,128)(2,1)S(1)}, u32[]{:S(2)}, u32[]{:S(2)}) collective-permute-start(bf16[15,1536]{1,0:T(8,128)(2,1)S(1)} %get-tuple-element.36), channel_id=1, source_target_pairs={{0,1},{1,2},{2,3},{3,4},{4,5},{5,6},{6,7},{7,8},{8,9},{9,10},{10,1... | collective-permute-start | bytes 138248 | tf_op jit(solution)/shard_map/ppermute | solution.py:24
  124.3 7.9 %collective-permute-start.17 = (bf16[15,1536]{1,0:T(8,128)(2,1)S(1)}, bf16[15,1536]{1,0:T(8,128)(2,1)S(1)}, u32[]{:S(2)}, u32[]{:S(2)}) collective-permute-start(bf16[15,1536]{1,0:T(8,128)(2,1)S(1)} %get-tuple-element.37), channel_id=1, source_target_pairs={{1,0},{2,1},{3,2},{4,3},{5,4},{6,5},{7,6},{8,7},{9,8},{10,9},{11,1... | collective-permute-start | bytes 138248 | tf_op jit(solution)/shard_map/ppermute | solution.py:27
  135.3 9.8 %multiply_convert_fusion = bf16[256,1536]{1,0:T(8,128)(2,1)S(1)} fusion(f32[286,1536]{1,0:T(8,128)S(1)} %convert_element_type.37, f32[1536]{0:T(1024)S(1)} %copy-done.24, f32[1536]{0:T(1024)S(1)} %copy-done.25, f32[1536]{0:T(1024)S(1)} %get-tuple-element.34, f32[1536]{0:T(1024)S(1)} %get-tuple-element.35, f32[1536]{0:T(1024)S(1)} %copy-done.4, ...), kind=kLoop, calls=%fused_computation.106 | loop fusion | flops 38928384 | bytes 49755904 | tf_op jit(solution)/shard_map/convert_element_type | solution.py:166
  145.1 4.6 %fusion = bf16[256,1536]{1,0:T(8,128)(2,1)} fusion(bf16[256,1536]{1,0:T(8,128)(2,1)S(1)} %multiply_convert_fusion, bf16[1536,1536]{1,0:T(8,128)(2,1)} %param.23, bf16[256,1536]{1,0:T(8,128)(2,1)S(1)} %fusion.1), kind=kOutput, calls=%fused_computation.2 | convolution fusion | flops 1209139200 | bytes 7077888 | tf_op jit(solution)/shard_map/dot_general | solution.py:167
  (142 shorter events, 18.1 us)
Async XLA Ops:
  0.0 119.2 %copy-start = (bf16[768,1536]{1,0:T(8,128)(2,1)S(1)}, bf16[768,1536]{1,0:T(8,128)(2,1)}, u32[]{:S(2)}) copy-start(bf16[768,1536]{1,0:T(8,128)(2,1)} %param.17) | copy-start | bytes 7077892
  0.0 26.7 %collective-permute-start.8 = (bf16[256,768]{1,0:T(8,128)(2,1)}, bf16[256,768]{1,0:T(8,128)(2,1)S(1)}, u32[]{:S(2)}, u32[]{:S(2)}) collective-permute-start(bf16[256,768]{1,0:T(8,128)(2,1)} %refs_13_.1), channel_id=1, source_target_pairs={{0,1},{1,2},{2,3},{3,4},{4,5},{5,6},{6,7},{7,8},{8,9},{9,10},{10,1... | collective-permute-start | bytes 1179656 | tf_op jit(solution)/shard_map/ppermute | solution.py:16
  2.1 26.6 %collective-permute-start.12 = (bf16[256,768]{1,0:T(8,128)(2,1)}, bf16[256,768]{1,0:T(8,128)(2,1)S(1)}, u32[]{:S(2)}, u32[]{:S(2)}) collective-permute-start(bf16[256,768]{1,0:T(8,128)(2,1)} %refs_13_.1), channel_id=1, source_target_pairs={{1,0},{2,1},{3,2},{4,3},{5,4},{6,5},{7,6},{8,7},{9,8},{10,9},{11,1... | collective-permute-start | bytes 1179656 | tf_op jit(solution)/shard_map/ppermute | solution.py:16
  11.3 25.2 %collective-permute-start = (bf16[256,768]{1,0:T(8,128)(2,1)}, bf16[256,768]{1,0:T(8,128)(2,1)S(1)}, u32[]{:S(2)}, u32[]{:S(2)}) collective-permute-start(bf16[256,768]{1,0:T(8,128)(2,1)} %refs_4_.1), channel_id=1, source_target_pairs={{0,1},{1,2},{2,3},{3,4},{4,5},{5,6},{6,7},{7,8},{8,9},{9,10},{10,1... | collective-permute-start | bytes 1179656 | tf_op jit(solution)/shard_map/ppermute | solution.py:16
  13.3 25.2 %collective-permute-start.4 = (bf16[256,768]{1,0:T(8,128)(2,1)}, bf16[256,768]{1,0:T(8,128)(2,1)}, u32[]{:S(2)}, u32[]{:S(2)}) collective-permute-start(bf16[256,768]{1,0:T(8,128)(2,1)} %refs_4_.1), channel_id=1, source_target_pairs={{1,0},{2,1},{3,2},{4,3},{5,4},{6,5},{7,6},{8,7},{9,8},{10,9},{11,1... | collective-permute-start | bytes 1179656 | tf_op jit(solution)/shard_map/ppermute | solution.py:16
  25.8 20.6 %copy-start.26 = (s32[128]{0:T(128)}, s32[128]{0:T(128)S(1)}, u32[]{:S(2)}) copy-start(s32[128]{0:T(128)S(1)} %sub.34) | copy-start | bytes 1540
  26.7 72.4 %copy-start.1 = (bf16[256,768]{1,0:T(8,128)(2,1)}, bf16[256,768]{1,0:T(8,128)(2,1)S(1)}, u32[]{:S(2)}) copy-start(bf16[256,768]{1,0:T(8,128)(2,1)S(1)} %collective-permute-done.8.refs_12_) | copy-start | bytes 1179652
  26.7 23.1 %collective-permute-start.9 = (bf16[256,768]{1,0:T(8,128)(2,1)S(1)}, bf16[256,768]{1,0:T(8,128)(2,1)}, u32[]{:S(2)}, u32[]{:S(2)}) collective-permute-start(bf16[256,768]{1,0:T(8,128)(2,1)S(1)} %collective-permute-done.8.refs_12_), channel_id=1, source_target_pairs={{0,1},{1,2},{2,3},{3,4},{4,5},{5,6},{6,7},{7,8},{8,9},{9,10},{10,1... | collective-permute-start | bytes 1179656 | tf_op jit(solution)/shard_map/ppermute | solution.py:16
  28.6 70.4 %copy-start.2 = (bf16[256,768]{1,0:T(8,128)(2,1)}, bf16[256,768]{1,0:T(8,128)(2,1)S(1)}, u32[]{:S(2)}) copy-start(bf16[256,768]{1,0:T(8,128)(2,1)S(1)} %collective-permute-done.12.refs_14_) | copy-start | bytes 1179652
  28.6 23.1 %collective-permute-start.13 = (bf16[256,768]{1,0:T(8,128)(2,1)S(1)}, bf16[256,768]{1,0:T(8,128)(2,1)}, u32[]{:S(2)}, u32[]{:S(2)}) collective-permute-start(bf16[256,768]{1,0:T(8,128)(2,1)S(1)} %collective-permute-done.12.refs_14_), channel_id=1, source_target_pairs={{1,0},{2,1},{3,2},{4,3},{5,4},{6,5},{7,6},{8,7},{9,8},{10,9},{11,1... | collective-permute-start | bytes 1179656 | tf_op jit(solution)/shard_map/ppermute | solution.py:16
  36.5 62.6 %copy-start.3 = (bf16[256,768]{1,0:T(8,128)(2,1)}, bf16[256,768]{1,0:T(8,128)(2,1)S(1)}, u32[]{:S(2)}) copy-start(bf16[256,768]{1,0:T(8,128)(2,1)S(1)} %collective-permute-done.refs_3_) | copy-start | bytes 1179652
  36.5 23.1 %collective-permute-start.1 = (bf16[256,768]{1,0:T(8,128)(2,1)S(1)}, bf16[256,768]{1,0:T(8,128)(2,1)}, u32[]{:S(2)}, u32[]{:S(2)}) collective-permute-start(bf16[256,768]{1,0:T(8,128)(2,1)S(1)} %collective-permute-done.refs_3_), channel_id=1, source_target_pairs={{0,1},{1,2},{2,3},{3,4},{4,5},{5,6},{6,7},{7,8},{8,9},{9,10},{10,1... | collective-permute-start | bytes 1179656 | tf_op jit(solution)/shard_map/ppermute | solution.py:16
  38.5 23.1 %collective-permute-start.5 = (bf16[256,768]{1,0:T(8,128)(2,1)}, bf16[256,768]{1,0:T(8,128)(2,1)}, u32[]{:S(2)}, u32[]{:S(2)}) collective-permute-start(bf16[256,768]{1,0:T(8,128)(2,1)} %collective-permute-done.4.refs_5_), channel_id=1, source_target_pairs={{1,0},{2,1},{3,2},{4,3},{5,4},{6,5},{7,6},{8,7},{9,8},{10,9},{11,1... | collective-permute-start | bytes 1179656 | tf_op jit(solution)/shard_map/ppermute | solution.py:16
  49.8 22.9 %collective-permute-start.10 = (bf16[256,768]{1,0:T(8,128)(2,1)}, bf16[256,768]{1,0:T(8,128)(2,1)}, u32[]{:S(2)}, u32[]{:S(2)}) collective-permute-start(bf16[256,768]{1,0:T(8,128)(2,1)} %collective-permute-done.9.refs_11_), channel_id=1, source_target_pairs={{0,1},{1,2},{2,3},{3,4},{4,5},{5,6},{6,7},{7,8},{8,9},{9,10},{10,1... | collective-permute-start | bytes 1179656 | tf_op jit(solution)/shard_map/ppermute | solution.py:16
  51.8 22.9 %collective-permute-start.14 = (bf16[256,768]{1,0:T(8,128)(2,1)}, bf16[256,768]{1,0:T(8,128)(2,1)}, u32[]{:S(2)}, u32[]{:S(2)}) collective-permute-start(bf16[256,768]{1,0:T(8,128)(2,1)} %collective-permute-done.13.refs_15_), channel_id=1, source_target_pairs={{1,0},{2,1},{3,2},{4,3},{5,4},{6,5},{7,6},{8,7},{9,8},{10,9},{11,1... | collective-permute-start | bytes 1179656 | tf_op jit(solution)/shard_map/ppermute | solution.py:16
  59.7 22.9 %collective-permute-start.2 = (bf16[256,768]{1,0:T(8,128)(2,1)}, bf16[256,768]{1,0:T(8,128)(2,1)}, u32[]{:S(2)}, u32[]{:S(2)}) collective-permute-start(bf16[256,768]{1,0:T(8,128)(2,1)} %collective-permute-done.1.refs_2_), channel_id=1, source_target_pairs={{0,1},{1,2},{2,3},{3,4},{4,5},{5,6},{6,7},{7,8},{8,9},{9,10},{10,1... | collective-permute-start | bytes 1179656 | tf_op jit(solution)/shard_map/ppermute | solution.py:16
  61.6 22.9 %collective-permute-start.6 = (bf16[256,768]{1,0:T(8,128)(2,1)}, bf16[256,768]{1,0:T(8,128)(2,1)}, u32[]{:S(2)}, u32[]{:S(2)}) collective-permute-start(bf16[256,768]{1,0:T(8,128)(2,1)} %collective-permute-done.5.refs_6_), channel_id=1, source_target_pairs={{1,0},{2,1},{3,2},{4,3},{5,4},{6,5},{7,6},{8,7},{9,8},{10,9},{11,1... | collective-permute-start | bytes 1179656 | tf_op jit(solution)/shard_map/ppermute | solution.py:16
  72.8 26.2 %collective-permute-start.11 = (bf16[256,768]{1,0:T(8,128)(2,1)}, bf16[256,768]{1,0:T(8,128)(2,1)}, u32[]{:S(2)}, u32[]{:S(2)}) collective-permute-start(bf16[256,768]{1,0:T(8,128)(2,1)} %collective-permute-done.10.refs_10_), channel_id=1, source_target_pairs={{0,1},{1,2},{2,3},{3,4},{4,5},{5,6},{6,7},{7,8},{8,9},{9,10},{10,1... | collective-permute-start | bytes 1179656 | tf_op jit(solution)/shard_map/ppermute | solution.py:16
  74.7 24.3 %collective-permute-start.15 = (bf16[256,768]{1,0:T(8,128)(2,1)}, bf16[256,768]{1,0:T(8,128)(2,1)}, u32[]{:S(2)}, u32[]{:S(2)}) collective-permute-start(bf16[256,768]{1,0:T(8,128)(2,1)} %collective-permute-done.14.refs_16_), channel_id=1, source_target_pairs={{1,0},{2,1},{3,2},{4,3},{5,4},{6,5},{7,6},{8,7},{9,8},{10,9},{11,1... | collective-permute-start | bytes 1179656 | tf_op jit(solution)/shard_map/ppermute | solution.py:16
  82.6 16.5 %collective-permute-start.3 = (bf16[256,768]{1,0:T(8,128)(2,1)}, bf16[256,768]{1,0:T(8,128)(2,1)}, u32[]{:S(2)}, u32[]{:S(2)}) collective-permute-start(bf16[256,768]{1,0:T(8,128)(2,1)} %collective-permute-done.2.refs_1_), channel_id=1, source_target_pairs={{0,1},{1,2},{2,3},{3,4},{4,5},{5,6},{6,7},{7,8},{8,9},{9,10},{10,1... | collective-permute-start | bytes 1179656 | tf_op jit(solution)/shard_map/ppermute | solution.py:16
  84.5 14.5 %collective-permute-start.7 = (bf16[256,768]{1,0:T(8,128)(2,1)}, bf16[256,768]{1,0:T(8,128)(2,1)}, u32[]{:S(2)}, u32[]{:S(2)}) collective-permute-start(bf16[256,768]{1,0:T(8,128)(2,1)} %collective-permute-done.6.refs_7_), channel_id=1, source_target_pairs={{1,0},{2,1},{3,2},{4,3},{5,4},{6,5},{7,6},{8,7},{9,8},{10,9},{11,1... | collective-permute-start | bytes 1179656 | tf_op jit(solution)/shard_map/ppermute | solution.py:16
  122.4 11.3 %collective-permute-start.16 = (bf16[15,1536]{1,0:T(8,128)(2,1)S(1)}, bf16[15,1536]{1,0:T(8,128)(2,1)S(1)}, u32[]{:S(2)}, u32[]{:S(2)}) collective-permute-start(bf16[15,1536]{1,0:T(8,128)(2,1)S(1)} %get-tuple-element.36), channel_id=1, source_target_pairs={{0,1},{1,2},{2,3},{3,4},{4,5},{5,6},{6,7},{7,8},{8,9},{9,10},{10,1... | collective-permute-start | bytes 138248 | tf_op jit(solution)/shard_map/ppermute | solution.py:24
  124.3 9.6 %collective-permute-start.17 = (bf16[15,1536]{1,0:T(8,128)(2,1)S(1)}, bf16[15,1536]{1,0:T(8,128)(2,1)S(1)}, u32[]{:S(2)}, u32[]{:S(2)}) collective-permute-start(bf16[15,1536]{1,0:T(8,128)(2,1)S(1)} %get-tuple-element.37), channel_id=1, source_target_pairs={{1,0},{2,1},{3,2},{4,3},{5,4},{6,5},{7,6},{8,7},{9,8},{10,9},{11,1... | collective-permute-start | bytes 138248 | tf_op jit(solution)/shard_map/ppermute | solution.py:27
  134.3 0.8 copy-start.25
  (41 other events, 31.4 us)

commit v3 on v2

--- a/solution.py
+++ b/solution.py
@@ -117,26 +117,34 @@
     offsets = jnp.arange(frames, dtype=jnp.int32)
     own_rec = segment_of(block_here * frames + offsets, starts)
 
-    key_blocks = block_here + jnp.arange(-REACH, REACH + 1, dtype=jnp.int32)
+    def hop(pair, distance):
+        return tuple(shifted_2(x, ("grp", "blk"), distance) for x in pair)
+
+    own_pair = (key_vectors, values)
+    from_m2 = hop(own_pair, 2)
+    from_p2 = hop(own_pair, -2)
+    from_m4 = hop(from_m2, 2)
+    from_p4 = hop(from_p2, -2)
+    parity = block_here % 2
+    partner = block_here + 1 - 2 * parity
+    far = tuple(lax.select(parity == 0, p4, m4) for m4, p4 in zip(from_m4, from_p4))
+    swap = [(i, i ^ 1) for i in range(nblocks)]
+    got = [
+        tuple(lax.ppermute(x, ("grp", "blk"), swap) for x in pair)
+        for pair in (own_pair, from_m2, from_p2, far)
+    ]
+    pairs = [own_pair, from_m2, from_p2, from_m4, from_p4] + got
+    key_blocks = jnp.stack([
+        block_here, block_here - 2, block_here + 2, block_here - 4, block_here + 4,
+        partner, partner - 2, partner + 2, partner - 4 + 8 * parity,
+    ]).astype(jnp.int32)
     key_pos = (key_blocks[:, None] * frames + offsets[None, :]).reshape(-1)
     key_inside = ((key_blocks >= 0) & (key_blocks < nblocks))[:, None]
     key_rec = jnp.where(key_inside, segment_of(key_pos, starts).reshape(NBLK, frames), -1)
     rows = -(-NBLK // 8) * 8
     key_rec = jnp.pad(key_rec, ((0, rows - NBLK), (0, 0)), constant_values=-1)
-
-    before_k, before_v, after_k, after_v = [], [], [], []
-    moving = (key_vectors, values)
-    for distance in range(1, REACH + 1):
-        moving = from_before(moving)
-        before_k.append(moving[0])
-        before_v.append(moving[1])
-    moving = (key_vectors, values)
-    for distance in range(1, REACH + 1):
-        moving = from_after(moving)
-        after_k.append(moving[0])
-        after_v.append(moving[1])
-    keys = before_k[::-1] + [key_vectors] + after_k
-    vals = before_v[::-1] + [values] + after_v
+    keys = [p[0] for p in pairs]
+    vals = [p[1] for p in pairs]
     attended = attend(own_rec[:, None], key_rec, queries, keys, vals)
     projected = jnp.dot(attended, output_weight, preferred_element_type=jnp.float32)
     resid = lax.optimization_barrier(

time: 151 us -> 115 us (0.76)
  starting transfers between devices: 89.6 us -> 54 us
  waiting for transfers between devices: 0.23 us -> 6.5 us
  other arithmetic: 22.6 us -> 17.7 us
    ppermute x16 -> x8, starting transfers between devices: 79.8 us -> 42.1 us  [shifted_2(): return lax.ppermute(block, axis, route)]
    ppermute x16 -> x8, waiting for transfers between devices: 0.04 us -> 6.34 us  [shifted_2(): return lax.ppermute(block, axis, route)]
    another operation x2, other arithmetic: 2.54 us -> 0.27 us
    select_n x0 -> x2, other arithmetic: none -> 1.61 us  [shards(): lax.select(parity == 0, p4, m4)]
  transfers between devices with their start and end apart: 18 -> 18, of which waited for: 1 -> 3; matrix products, arithmetic and copies ran while one was open for 14% -> 12% of each run, Pallas kernels for 0% -> 0%
where the time goes in v3:
time: 115 us; the launch traced here: 114 us
  starting transfers between devices  54 us (47%)
  Pallas kernels  20.2 us (18%)
  other arithmetic  17.7 us (15%)
  local copies, waits for them, and re-layouts  8.2 us (7%)
  matrix products  6.64 us (6%)
  waiting for transfers between devices  6.5 us (6%)
    ppermute x8, starting transfers between devices, shifted_2(): return lax.ppermute(block, axis, route)  42.1 us
    pallas_call x1, Pallas kernels, attend(): pl.pallas_call(attend_kernel, grid=(width // pair,), in_specs=[pl.BlockSp...  20.2 us
    convert_element_type x1, other arithmetic, shards(): (shifted * jax.nn.sigmoid(shifted)).astype(jnp.bfloat16)  9.78 us
    ppermute x1, starting transfers between devices, padded(): lax.ppermute(lax.slice_in_dim(block, 0, width, axis=dim), axis, backward)  8.35 us
    ppermute x8, waiting for transfers between devices, shifted_2(): return lax.ppermute(block, axis, route)  6.34 us
    dot_general x1, matrix products, shards(): jnp.dot(act, pointwise_weight, preferred_element_type=jnp.float32)  4.6 us
    slice x2, local copies, waits for them, and re-layouts, shards(): depthwise_taps[tap]  3.8 us
  transfers between devices with their start and end apart: 18, of which 3 were waited for; matrix products, arithmetic and copies ran while one was open for 12% of the time, Pallas kernels for 0%

profile of v3, /device:TPU:16, one launch (start us, length us, event | category | flops | bytes accessed | tf_op | source)
XLA Modules:
  0.0 114.1 jit_solution(2893063515095549166)
XLA Ops:
  0.0 3.9 %collective-permute-start.8 = (bf16[256,768]{1,0:T(8,128)(2,1)}, bf16[256,768]{1,0:T(8,128)(2,1)}, u32[]{:S(2)}, u32[]{:S(2)}) collective-permute-start(bf16[256,768]{1,0:T(8,128)(2,1)} %refs_9_.1), channel_id=1, source_target_pairs={{0,2},{1,3},{2,4},{3,5},{4,6},{5,7},{6,8},{7,9},{8,10},{9,11},{10,... | collective-permute-start | bytes 1179656 | tf_op jit(solution)/shard_map/ppermute | solution.py:16
  4.0 7.9 %collective-permute-start.9 = (bf16[256,768]{1,0:T(8,128)(2,1)}, bf16[256,768]{1,0:T(8,128)(2,1)}, u32[]{:S(2)}, u32[]{:S(2)}) collective-permute-start(bf16[256,768]{1,0:T(8,128)(2,1)} %refs_9_.1), channel_id=1, source_target_pairs={{2,0},{3,1},{4,2},{5,3},{6,4},{7,5},{8,6},{9,7},{10,8},{11,9},{12,... | collective-permute-start | bytes 1179656 | tf_op jit(solution)/shard_map/ppermute | solution.py:16
  11.9 1.9 %collective-permute-start = (bf16[256,768]{1,0:T(8,128)(2,1)}, bf16[256,768]{1,0:T(8,128)(2,1)}, u32[]{:S(2)}, u32[]{:S(2)}) collective-permute-start(bf16[256,768]{1,0:T(8,128)(2,1)} %refs_0_.1), channel_id=1, source_target_pairs={{0,2},{1,3},{2,4},{3,5},{4,6},{5,7},{6,8},{7,9},{8,10},{9,11},{10,... | collective-permute-start | bytes 1179656 | tf_op jit(solution)/shard_map/ppermute | solution.py:16
  13.8 8.1 %collective-permute-start.1 = (bf16[256,768]{1,0:T(8,128)(2,1)}, bf16[256,768]{1,0:T(8,128)(2,1)}, u32[]{:S(2)}, u32[]{:S(2)}) collective-permute-start(bf16[256,768]{1,0:T(8,128)(2,1)} %refs_0_.1), channel_id=1, source_target_pairs={{2,0},{3,1},{4,2},{5,3},{6,4},{7,5},{8,6},{9,7},{10,8},{11,9},{12,... | collective-permute-start | bytes 1179656 | tf_op jit(solution)/shard_map/ppermute | solution.py:16
  22.3 0.8 copy.16
  24.0 1.4 %convert_reduce_fusion.1 = s32[2304]{0:T(1024)S(1)} fusion(s32[128]{0:T(128)S(1)} %sub.49, s32[2304]{0:T(1024)S(1)} %add.220), kind=kLoop, calls=%fused_computation.107 | loop fusion | flops 882432 | bytes 18944 | tf_op jit(solution)/shard_map/reduce_sum | solution.py:33
  26.4 1.9 %collective-permute-start.10 = (bf16[256,768]{1,0:T(8,128)(2,1)}, bf16[256,768]{1,0:T(8,128)(2,1)S(1)}, u32[]{:S(2)}, u32[]{:S(2)}) collective-permute-start(bf16[256,768]{1,0:T(8,128)(2,1)} %collective-permute-done.8.refs_10_), channel_id=1, source_target_pairs={{0,2},{1,3},{2,4},{3,5},{4,6},{5,7},{6,8},{7,9},{8,10},{9,11},{10,... | collective-permute-start | bytes 1179656 | tf_op jit(solution)/shard_map/ppermute | solution.py:16
  28.3 8.1 %collective-permute-start.11 = (bf16[256,768]{1,0:T(8,128)(2,1)}, bf16[256,768]{1,0:T(8,128)(2,1)S(1)}, u32[]{:S(2)}, u32[]{:S(2)}) collective-permute-start(bf16[256,768]{1,0:T(8,128)(2,1)} %collective-permute-done.9.refs_11_), channel_id=1, source_target_pairs={{2,0},{3,1},{4,2},{5,3},{6,4},{7,5},{8,6},{9,7},{10,8},{11,9},{12,... | collective-permute-start | bytes 1179656 | tf_op jit(solution)/shard_map/ppermute | solution.py:16
  36.7 1.9 %collective-permute-start.2 = (bf16[256,768]{1,0:T(8,128)(2,1)}, bf16[256,768]{1,0:T(8,128)(2,1)S(1)}, u32[]{:S(2)}, u32[]{:S(2)}) collective-permute-start(bf16[256,768]{1,0:T(8,128)(2,1)} %collective-permute-done.refs_1_), channel_id=1, source_target_pairs={{0,2},{1,3},{2,4},{3,5},{4,6},{5,7},{6,8},{7,9},{8,10},{9,11},{10,... | collective-permute-start | bytes 1179656 | tf_op jit(solution)/shard_map/ppermute | solution.py:16
  38.6 8.1 %collective-permute-start.3 = (bf16[256,768]{1,0:T(8,128)(2,1)}, bf16[256,768]{1,0:T(8,128)(2,1)S(1)}, u32[]{:S(2)}, u32[]{:S(2)}) collective-permute-start(bf16[256,768]{1,0:T(8,128)(2,1)} %collective-permute-done.1.refs_2_), channel_id=1, source_target_pairs={{2,0},{3,1},{4,2},{5,3},{6,4},{7,5},{8,6},{9,7},{10,8},{11,9},{12,... | collective-permute-start | bytes 1179656 | tf_op jit(solution)/shard_map/ppermute | solution.py:16
  48.1 0.8 broadcast_select_fusion
  48.9 5.0 %collective-permute-done.2.refs_3_ = bf16[256,768]{1,0:T(8,128)(2,1)S(1)} collective-permute-done((bf16[256,768]{1,0:T(8,128)(2,1)}, bf16[256,768]{1,0:T(8,128)(2,1)S(1)}, u32[]{:S(2)}, u32[]{:S(2)}) %collective-permute-start.2) | collective-permute-done | bytes 393248 | tf_op jit(solution)/shard_map/ppermute | solution.py:16
  53.9 1.3 %collective-permute-done.3.refs_4_ = bf16[256,768]{1,0:T(8,128)(2,1)S(1)} collective-permute-done((bf16[256,768]{1,0:T(8,128)(2,1)}, bf16[256,768]{1,0:T(8,128)(2,1)S(1)}, u32[]{:S(2)}, u32[]{:S(2)}) %collective-permute-start.3) | collective-permute-done | bytes 393248 | tf_op jit(solution)/shard_map/ppermute | solution.py:16
  56.0 0.8 broadcast_select_fusion.1
  57.4 0.8 copy.17.recq_ref
  58.2 1.3 %pad.4.reck_ref = s32[16,256]{1,0:T(8,128)} pad(s32[9,256]{1,0:T(8,128)} %broadcast_select_fusion.2, s32[]{:T(128)} %constant.55.clone.1), padding=0_7x0_0 | pad | bytes 25604 | tf_op jit(solution)/shard_map/jit(_pad)/pad | solution.py:145
  59.5 2.4 %slice_reduce_fusion.30 = (f32[1536]{0:T(1024)S(1)}, f32[1536]{0:T(1024)}, f32[1536]{0:T(1024)}, f32[1536]{0:T(1024)}, f32[1536]{0:T(1024)}, /*index=5*/f32[1536...) fusion(f32[31,1536]{1,0:T(8,128)} %param.20), kind=kLoop, calls=%fused_computation.145 | loop fusion | bytes 233472 | tf_op jit(solution)/shard_map/slice | solution.py:171
  62.7 20.2 %shard_map.118 = bf16[256,768]{1,0:T(8,128)(2,1)} custom-call(s32[256,1]{1,0:T(8,128)} %copy.17.recq_ref, s32[16,256]{1,0:T(8,128)} %pad.4.reck_ref, bf16[256,768]{1,0:T(8,128)(2,1)} %q_ref.1, bf16[256,768]{1,0:T(8,128)(2,1)} %refs_0_.1, bf16[256,768]{1,0:T(8,128)(2,1)} %collective-permute-done.refs_1_, bf16[256,768]{1,0:T(8,128)(2,1)} %collective-permute-done.1.refs_2_, ...), custom_call_target="tpu_custom_call" | custom-call | tf_op jit(solution)/shard_map/pallas_call | solution.py:82
  82.9 2.0 %fusion.1 = bf16[256,1536]{1,0:T(8,128)(2,1)S(1)} fusion(bf16[256,768]{1,0:T(8,128)(2,1)} %shard_map.118, bf16[768,1536]{1,0:T(8,128)(2,1)S(1)} %copy-done, bf16[256,1536]{1,0:T(8,128)(2,1)} %param.12), kind=kOutput, calls=%fused_computation.3 | convolution fusion | flops 605159424 | bytes 4325376 | tf_op jit(solution)/shard_map/dot_general | solution.py:149
  86.1 2.3 %collective-permute-start.16 = (bf16[15,1536]{1,0:T(8,128)(2,1)S(1)}, bf16[15,1536]{1,0:T(8,128)(2,1)S(1)}, u32[]{:S(2)}, u32[]{:S(2)}) collective-permute-start(bf16[15,1536]{1,0:T(8,128)(2,1)S(1)} %get-tuple-element.36), channel_id=1, source_target_pairs={{0,1},{1,2},{2,3},{3,4},{4,5},{5,6},{6,7},{7,8},{8,9},{9,10},{10,1... | collective-permute-start | bytes 138248 | tf_op jit(solution)/shard_map/ppermute | solution.py:24
  88.4 8.3 %collective-permute-start.17 = (bf16[15,1536]{1,0:T(8,128)(2,1)S(1)}, bf16[15,1536]{1,0:T(8,128)(2,1)S(1)}, u32[]{:S(2)}, u32[]{:S(2)}) collective-permute-start(bf16[15,1536]{1,0:T(8,128)(2,1)S(1)} %get-tuple-element.37), channel_id=1, source_target_pairs={{1,0},{2,1},{3,2},{4,3},{5,4},{6,5},{7,6},{8,7},{9,8},{10,9},{11,1... | collective-permute-start | bytes 138248 | tf_op jit(solution)/shard_map/ppermute | solution.py:27
  96.7 1.4 %slice_reduce_fusion.29 = (f32[1536]{0:T(1024)S(1)}, f32[1536]{0:T(1024)S(1)}, f32[1536]{0:T(1024)S(1)}, f32[1536]{0:T(1024)S(1)}, f32[1536]{0:T(1024)S(1)}, /*i...) fusion(f32[31,1536]{1,0:T(8,128)} %param.20), kind=kLoop, calls=%fused_computation.144 | loop fusion | bytes 147456 | tf_op jit(solution)/shard_map/slice | solution.py:171
  99.7 9.8 %multiply_convert_fusion = bf16[256,1536]{1,0:T(8,128)(2,1)S(1)} fusion(f32[286,1536]{1,0:T(8,128)S(1)} %convert_element_type.37, f32[1536]{0:T(1024)S(1)} %copy-done.25, f32[1536]{0:T(1024)S(1)} %copy-done.26, f32[1536]{0:T(1024)S(1)} %get-tuple-element.34, f32[1536]{0:T(1024)S(1)} %get-tuple-element.35, f32[1536]{0:T(1024)S(1)} %copy-done.5, ...), kind=kLoop, calls=%fused_computation.106 | loop fusion | flops 38928384 | bytes 49755904 | tf_op jit(solution)/shard_map/convert_element_type | solution.py:174
  109.5 4.6 %fusion = bf16[256,1536]{1,0:T(8,128)(2,1)} fusion(bf16[256,1536]{1,0:T(8,128)(2,1)S(1)} %multiply_convert_fusion, bf16[1536,1536]{1,0:T(8,128)(2,1)} %param.23, bf16[256,1536]{1,0:T(8,128)(2,1)S(1)} %fusion.1), kind=kOutput, calls=%fused_computation.2 | convolution fusion | flops 1209139200 | bytes 7077888 | tf_op jit(solution)/shard_map/dot_general | solution.py:175
  (145 shorter events, 7.8 us)
Async XLA Ops:
  0.0 82.9 %copy-start = (bf16[768,1536]{1,0:T(8,128)(2,1)S(1)}, bf16[768,1536]{1,0:T(8,128)(2,1)}, u32[]{:S(2)}) copy-start(bf16[768,1536]{1,0:T(8,128)(2,1)} %param.17) | copy-start | bytes 7077892
  0.0 26.4 %collective-permute-start.8 = (bf16[256,768]{1,0:T(8,128)(2,1)}, bf16[256,768]{1,0:T(8,128)(2,1)}, u32[]{:S(2)}, u32[]{:S(2)}) collective-permute-start(bf16[256,768]{1,0:T(8,128)(2,1)} %refs_9_.1), channel_id=1, source_target_pairs={{0,2},{1,3},{2,4},{3,5},{4,6},{5,7},{6,8},{7,9},{8,10},{9,11},{10,... | collective-permute-start | bytes 1179656 | tf_op jit(solution)/shard_map/ppermute | solution.py:16
  4.0 24.4 %collective-permute-start.9 = (bf16[256,768]{1,0:T(8,128)(2,1)}, bf16[256,768]{1,0:T(8,128)(2,1)}, u32[]{:S(2)}, u32[]{:S(2)}) collective-permute-start(bf16[256,768]{1,0:T(8,128)(2,1)} %refs_9_.1), channel_id=1, source_target_pairs={{2,0},{3,1},{4,2},{5,3},{6,4},{7,5},{8,6},{9,7},{10,8},{11,9},{12,... | collective-permute-start | bytes 1179656 | tf_op jit(solution)/shard_map/ppermute | solution.py:16
  11.9 24.8 %collective-permute-start = (bf16[256,768]{1,0:T(8,128)(2,1)}, bf16[256,768]{1,0:T(8,128)(2,1)}, u32[]{:S(2)}, u32[]{:S(2)}) collective-permute-start(bf16[256,768]{1,0:T(8,128)(2,1)} %refs_0_.1), channel_id=1, source_target_pairs={{0,2},{1,3},{2,4},{3,5},{4,6},{5,7},{6,8},{7,9},{8,10},{9,11},{10,... | collective-permute-start | bytes 1179656 | tf_op jit(solution)/shard_map/ppermute | solution.py:16
  13.8 24.8 %collective-permute-start.1 = (bf16[256,768]{1,0:T(8,128)(2,1)}, bf16[256,768]{1,0:T(8,128)(2,1)}, u32[]{:S(2)}, u32[]{:S(2)}) collective-permute-start(bf16[256,768]{1,0:T(8,128)(2,1)} %refs_0_.1), channel_id=1, source_target_pairs={{2,0},{3,1},{4,2},{5,3},{6,4},{7,5},{8,6},{9,7},{10,8},{11,9},{12,... | collective-permute-start | bytes 1179656 | tf_op jit(solution)/shard_map/ppermute | solution.py:16
  22.0 34.8 %collective-permute-start.12 = (bf16[256,768]{1,0:T(8,128)(2,1)}, bf16[256,768]{1,0:T(8,128)(2,1)}, u32[]{:S(2)}, u32[]{:S(2)}) collective-permute-start(bf16[256,768]{1,0:T(8,128)(2,1)} %refs_9_.1), channel_id=1, source_target_pairs={{0,1},{1,0},{2,3},{3,2},{4,5},{5,4},{6,7},{7,6},{8,9},{9,8},{10,11... | collective-permute-start | bytes 1179656 | tf_op jit(solution)/shard_map/ppermute | solution.py:133
  26.4 21.1 %collective-permute-start.10 = (bf16[256,768]{1,0:T(8,128)(2,1)}, bf16[256,768]{1,0:T(8,128)(2,1)S(1)}, u32[]{:S(2)}, u32[]{:S(2)}) collective-permute-start(bf16[256,768]{1,0:T(8,128)(2,1)} %collective-permute-done.8.refs_10_), channel_id=1, source_target_pairs={{0,2},{1,3},{2,4},{3,5},{4,6},{5,7},{6,8},{7,9},{8,10},{9,11},{10,... | collective-permute-start | bytes 1179656 | tf_op jit(solution)/shard_map/ppermute | solution.py:16
  28.3 19.3 %collective-permute-start.11 = (bf16[256,768]{1,0:T(8,128)(2,1)}, bf16[256,768]{1,0:T(8,128)(2,1)S(1)}, u32[]{:S(2)}, u32[]{:S(2)}) collective-permute-start(bf16[256,768]{1,0:T(8,128)(2,1)} %collective-permute-done.9.refs_11_), channel_id=1, source_target_pairs={{2,0},{3,1},{4,2},{5,3},{6,4},{7,5},{8,6},{9,7},{10,8},{11,9},{12,... | collective-permute-start | bytes 1179656 | tf_op jit(solution)/shard_map/ppermute | solution.py:16
  36.7 17.2 %collective-permute-start.2 = (bf16[256,768]{1,0:T(8,128)(2,1)}, bf16[256,768]{1,0:T(8,128)(2,1)S(1)}, u32[]{:S(2)}, u32[]{:S(2)}) collective-permute-start(bf16[256,768]{1,0:T(8,128)(2,1)} %collective-permute-done.refs_1_), channel_id=1, source_target_pairs={{0,2},{1,3},{2,4},{3,5},{4,6},{5,7},{6,8},{7,9},{8,10},{9,11},{10,... | collective-permute-start | bytes 1179656 | tf_op jit(solution)/shard_map/ppermute | solution.py:16
  38.6 16.6 %collective-permute-start.3 = (bf16[256,768]{1,0:T(8,128)(2,1)}, bf16[256,768]{1,0:T(8,128)(2,1)S(1)}, u32[]{:S(2)}, u32[]{:S(2)}) collective-permute-start(bf16[256,768]{1,0:T(8,128)(2,1)} %collective-permute-done.1.refs_2_), channel_id=1, source_target_pairs={{2,0},{3,1},{4,2},{5,3},{6,4},{7,5},{8,6},{9,7},{10,8},{11,9},{12,... | collective-permute-start | bytes 1179656 | tf_op jit(solution)/shard_map/ppermute | solution.py:16
  47.5 15.2 %copy-start.1 = (bf16[256,768]{1,0:T(8,128)(2,1)}, bf16[256,768]{1,0:T(8,128)(2,1)S(1)}, u32[]{:S(2)}) copy-start(bf16[256,768]{1,0:T(8,128)(2,1)S(1)} %collective-permute-done.10.refs_12_) | copy-start | bytes 1179652
  47.5 9.3 %collective-permute-start.4 = (bf16[256,768]{1,0:T(8,128)(2,1)}, bf16[256,768]{1,0:T(8,128)(2,1)}, u32[]{:S(2)}, u32[]{:S(2)}) collective-permute-start(bf16[256,768]{1,0:T(8,128)(2,1)} %refs_0_.1), channel_id=1, source_target_pairs={{0,1},{1,0},{2,3},{3,2},{4,5},{5,4},{6,7},{7,6},{8,9},{9,8},{10,11... | collective-permute-start | bytes 1179656 | tf_op jit(solution)/shard_map/ppermute | solution.py:133
  47.6 15.1 %copy-start.2 = (bf16[256,768]{1,0:T(8,128)(2,1)}, bf16[256,768]{1,0:T(8,128)(2,1)S(1)}, u32[]{:S(2)}) copy-start(bf16[256,768]{1,0:T(8,128)(2,1)S(1)} %collective-permute-done.11.refs_13_) | copy-start | bytes 1179652
  47.6 9.7 %collective-permute-start.13 = (bf16[256,768]{1,0:T(8,128)(2,1)}, bf16[256,768]{1,0:T(8,128)(2,1)}, u32[]{:S(2)}, u32[]{:S(2)}) collective-permute-start(bf16[256,768]{1,0:T(8,128)(2,1)} %collective-permute-done.8.refs_10_), channel_id=1, source_target_pairs={{0,1},{1,0},{2,3},{3,2},{4,5},{5,4},{6,7},{7,6},{8,9},{9,8},{10,11... | collective-permute-start | bytes 1179656 | tf_op jit(solution)/shard_map/ppermute | solution.py:133
  53.9 8.8 %copy-start.3 = (bf16[256,768]{1,0:T(8,128)(2,1)}, bf16[256,768]{1,0:T(8,128)(2,1)S(1)}, u32[]{:S(2)}) copy-start(bf16[256,768]{1,0:T(8,128)(2,1)S(1)} %collective-permute-done.2.refs_3_) | copy-start | bytes 1179652
  53.9 8.7 %collective-permute-start.14 = (bf16[256,768]{1,0:T(8,128)(2,1)}, bf16[256,768]{1,0:T(8,128)(2,1)}, u32[]{:S(2)}, u32[]{:S(2)}) collective-permute-start(bf16[256,768]{1,0:T(8,128)(2,1)} %collective-permute-done.9.refs_11_), channel_id=1, source_target_pairs={{0,1},{1,0},{2,3},{3,2},{4,5},{5,4},{6,7},{7,6},{8,9},{9,8},{10,11... | collective-permute-start | bytes 1179656 | tf_op jit(solution)/shard_map/ppermute | solution.py:133
  55.2 7.4 %collective-permute-start.5 = (bf16[256,768]{1,0:T(8,128)(2,1)}, bf16[256,768]{1,0:T(8,128)(2,1)}, u32[]{:S(2)}, u32[]{:S(2)}) collective-permute-start(bf16[256,768]{1,0:T(8,128)(2,1)} %collective-permute-done.refs_1_), channel_id=1, source_target_pairs={{0,1},{1,0},{2,3},{3,2},{4,5},{5,4},{6,7},{7,6},{8,9},{9,8},{10,11... | collective-permute-start | bytes 1179656 | tf_op jit(solution)/shard_map/ppermute | solution.py:133
  56.8 5.9 %collective-permute-start.6 = (bf16[256,768]{1,0:T(8,128)(2,1)}, bf16[256,768]{1,0:T(8,128)(2,1)}, u32[]{:S(2)}, u32[]{:S(2)}) collective-permute-start(bf16[256,768]{1,0:T(8,128)(2,1)} %collective-permute-done.1.refs_2_), channel_id=1, source_target_pairs={{0,1},{1,0},{2,3},{3,2},{4,5},{5,4},{6,7},{7,6},{8,9},{9,8},{10,11... | collective-permute-start | bytes 1179656 | tf_op jit(solution)/shard_map/ppermute | solution.py:133
  56.8 5.9 %collective-permute-start.15 = (bf16[256,768]{1,0:T(8,128)(2,1)}, bf16[256,768]{1,0:T(8,128)(2,1)}, u32[]{:S(2)}, u32[]{:S(2)}) collective-permute-start(bf16[256,768]{1,0:T(8,128)(2,1)} %broadcast_select_fusion), channel_id=1, source_target_pairs={{0,1},{1,0},{2,3},{3,2},{4,5},{5,4},{6,7},{7,6},{8,9},{9,8},{10,11... | collective-permute-start | bytes 1179656 | tf_op jit(solution)/shard_map/ppermute | solution.py:133
  57.3 5.4 %collective-permute-start.7 = (bf16[256,768]{1,0:T(8,128)(2,1)}, bf16[256,768]{1,0:T(8,128)(2,1)}, u32[]{:S(2)}, u32[]{:S(2)}) collective-permute-start(bf16[256,768]{1,0:T(8,128)(2,1)} %broadcast_select_fusion.1), channel_id=1, source_target_pairs={{0,1},{1,0},{2,3},{3,2},{4,5},{5,4},{6,7},{7,6},{8,9},{9,8},{10,11... | collective-permute-start | bytes 1179656 | tf_op jit(solution)/shard_map/ppermute | solution.py:133
  86.1 12.0 %collective-permute-start.16 = (bf16[15,1536]{1,0:T(8,128)(2,1)S(1)}, bf16[15,1536]{1,0:T(8,128)(2,1)S(1)}, u32[]{:S(2)}, u32[]{:S(2)}) collective-permute-start(bf16[15,1536]{1,0:T(8,128)(2,1)S(1)} %get-tuple-element.36), channel_id=1, source_target_pairs={{0,1},{1,2},{2,3},{3,4},{4,5},{5,6},{6,7},{7,8},{8,9},{9,10},{10,1... | collective-permute-start | bytes 138248 | tf_op jit(solution)/shard_map/ppermute | solution.py:24
  88.4 9.9 %collective-permute-start.17 = (bf16[15,1536]{1,0:T(8,128)(2,1)S(1)}, bf16[15,1536]{1,0:T(8,128)(2,1)S(1)}, u32[]{:S(2)}, u32[]{:S(2)}) collective-permute-start(bf16[15,1536]{1,0:T(8,128)(2,1)S(1)} %get-tuple-element.37), channel_id=1, source_target_pairs={{1,0},{2,1},{3,2},{4,3},{5,4},{6,5},{7,6},{8,7},{9,8},{10,9},{11,1... | collective-permute-start | bytes 138248 | tf_op jit(solution)/shard_map/ppermute | solution.py:27
  98.7 0.8 copy-start.25
  98.7 0.8 copy-start.26
  (41 other events, 31.3 us)

commit v4 on v3

--- a/solution.py
+++ b/solution.py
@@ -1,3 +1,5 @@
+import functools
+
 import jax
 import jax.numpy as jnp
 from jax import lax
@@ -44,54 +46,69 @@
 NBLK = 2 * REACH + 1
 
 
-def attend_kernel(recq_ref, reck_ref, q_ref, *refs):
-    k_refs = refs[:NBLK]
-    v_refs = refs[NBLK : 2 * NBLK]
-    out_ref = refs[2 * NBLK]
-    s_scr = refs[2 * NBLK + 1]
+def absorb_kernel(nblk, final, recq_ref, reck_ref, q_ref, m_ref, l_ref, acc_ref, *refs):
+    k_refs = refs[:nblk]
+    v_refs = refs[nblk : 2 * nblk]
+    m_out, l_out, acc_out, s_scr = refs[2 * nblk :]
     rec_q = recq_ref[...]
     for hh in range(2):
         cols = slice(hh * HD, (hh + 1) * HD)
         q_h = q_ref[:, cols]
-        top = None
-        for j in range(NBLK):
+        m_old = m_ref[0, :, hh : hh + 1]
+        top = m_old
+        for j in range(nblk):
             s = lax.dot_general(
                 q_h, k_refs[j][:, cols], (((1,), (1,)), ((), ())),
                 preferred_element_type=jnp.float32,
             ) * (HD ** (-0.5))
             s = jnp.where(rec_q == reck_ref[j : j + 1, :], s, -1e30)
             s_scr[j] = s
-            row = jnp.max(s, axis=1, keepdims=True)
-            top = row if top is None else jnp.maximum(top, row)
-        total = None
-        acc = None
-        for j in range(NBLK):
+            top = jnp.maximum(top, jnp.max(s, axis=1, keepdims=True))
+        alpha = jnp.exp(m_old - top)
+        total = l_ref[0, :, hh : hh + 1] * alpha
+        acc = acc_ref[:, cols] * alpha
+        for j in range(nblk):
             p = jnp.exp(s_scr[j] - top)
-            part = jnp.sum(p, axis=1, keepdims=True)
-            prod = jnp.dot(p.astype(jnp.bfloat16), v_refs[j][:, cols],
-                           preferred_element_type=jnp.float32)
-            total = part if total is None else total + part
-            acc = prod if acc is None else acc + prod
-        out_ref[:, cols] = (acc / total).astype(out_ref.dtype)
-
-
-def attend(rec_q, rec_k, query, keys, vals):
+            total = total + jnp.sum(p, axis=1, keepdims=True)
+            acc = acc + jnp.dot(p.astype(jnp.bfloat16), v_refs[j][:, cols],
+                                preferred_element_type=jnp.float32)
+        if final:
+            acc_out[:, cols] = (acc / total).astype(acc_out.dtype)
+        else:
+            acc_out[:, cols] = acc
+            m_out[0, :, hh : hh + 1] = top
+            l_out[0, :, hh : hh + 1] = total
+
+
+def absorb(state, rec_q, key_rec, query, keys, vals, final):
+    m, l, acc = state
+    nblk = len(keys)
     frames, width = query.shape
     pair = 2 * HD
+    steps = width // pair
+    rows = -(-nblk // 8) * 8
+    rec_k = jnp.pad(key_rec, ((0, rows - nblk), (0, 0)), constant_values=-1)
     tile = pl.BlockSpec((frames, pair), lambda g: (0, g))
-    return pl.pallas_call(
-        attend_kernel,
-        grid=(width // pair,),
+    stat = pl.BlockSpec((1, frames, 2), lambda g: (g, 0, 0))
+    out_dtype = jnp.bfloat16 if final else jnp.float32
+    out = pl.pallas_call(
+        functools.partial(absorb_kernel, nblk, final),
+        grid=(steps,),
         in_specs=[
             pl.BlockSpec(rec_q.shape, lambda g: (0, 0)),
             pl.BlockSpec(rec_k.shape, lambda g: (0, 0)),
-            tile,
+            tile, stat, stat, tile,
         ]
-        + [tile] * (2 * NBLK),
-        out_specs=tile,
-        out_shape=jax.ShapeDtypeStruct((frames, width), jnp.bfloat16),
-        scratch_shapes=[pltpu.VMEM((NBLK, frames, frames), jnp.float32)],
-    )(rec_q, rec_k, query, *keys, *vals)
+        + [tile] * (2 * nblk),
+        out_specs=[stat, stat, tile],
+        out_shape=[
+            jax.ShapeDtypeStruct(m.shape, jnp.float32),
+            jax.ShapeDtypeStruct(l.shape, jnp.float32),
+            jax.ShapeDtypeStruct((frames, width), out_dtype),
+        ],
+        scratch_shapes=[pltpu.VMEM((nblk, frames, frames), jnp.float32)],
+    )(rec_q, rec_k, query, m, l, acc, *keys, *vals)
+    return tuple(out)
 
 
 def shards(
@@ -133,19 +150,34 @@
         tuple(lax.ppermute(x, ("grp", "blk"), swap) for x in pair)
         for pair in (own_pair, from_m2, from_p2, far)
     ]
-    pairs = [own_pair, from_m2, from_p2, from_m4, from_p4] + got
-    key_blocks = jnp.stack([
-        block_here, block_here - 2, block_here + 2, block_here - 4, block_here + 4,
-        partner, partner - 2, partner + 2, partner - 4 + 8 * parity,
-    ]).astype(jnp.int32)
-    key_pos = (key_blocks[:, None] * frames + offsets[None, :]).reshape(-1)
-    key_inside = ((key_blocks >= 0) & (key_blocks < nblocks))[:, None]
-    key_rec = jnp.where(key_inside, segment_of(key_pos, starts).reshape(NBLK, frames), -1)
-    rows = -(-NBLK // 8) * 8
-    key_rec = jnp.pad(key_rec, ((0, rows - NBLK), (0, 0)), constant_values=-1)
-    keys = [p[0] for p in pairs]
-    vals = [p[1] for p in pairs]
-    attended = attend(own_rec[:, None], key_rec, queries, keys, vals)
+    def recs_of(blocks):
+        blocks = jnp.stack(blocks).astype(jnp.int32)
+        pos = (blocks[:, None] * frames + offsets[None, :]).reshape(-1)
+        inside = ((blocks >= 0) & (blocks < nblocks))[:, None]
+        return jnp.where(inside, segment_of(pos, starts).reshape(blocks.shape[0], frames), -1)
+
+    stages = [
+        ([own_pair], [block_here]),
+        (
+            [from_m2, from_p2] + got[:3],
+            [block_here - 2, block_here + 2, partner, partner - 2, partner + 2],
+        ),
+        ([from_m4, from_p4, got[3]], [block_here - 4, block_here + 4, partner - 4 + 8 * parity]),
+    ]
+    steps = queries.shape[1] // (2 * HD)
+    state = (
+        jnp.full((steps, frames, 2), -1e30, jnp.float32),
+        jnp.zeros((steps, frames, 2), jnp.float32),
+        jnp.zeros(queries.shape, jnp.float32),
+    )
+    rec_q = own_rec[:, None]
+    for n, (stage_pairs, blocks) in enumerate(stages):
+        state = absorb(
+            state, rec_q, recs_of(blocks), queries,
+            [p[0] for p in stage_pairs], [p[1] for p in stage_pairs],
+            n == len(stages) - 1,
+        )
+    attended = state[2]
     projected = jnp.dot(attended, output_weight, preferred_element_type=jnp.float32)
     resid = lax.optimization_barrier(
         (features.astype(jnp.float32) + projected).astype(jnp.bfloat16)

time: 115 us -> 130 us (1.13)
  Pallas kernels: 20.2 us -> 35.5 us
  matrix products: 6.64 us -> 4.3 us
  local copies, waits for them, and re-layouts: 8.2 us -> 10.1 us
  waiting for transfers between devices: 6.5 us -> 7.83 us
    pallas_call x1 -> x3, Pallas kernels: 20.2 us -> 35.5 us  [absorb(): pl.pallas_call(functools.partial(absorb_kernel, nblk, final), grid=(steps...]
    slice x2, local copies, waits for them, and re-layouts: 3.8 us -> 0.52 us  [shards(): depthwise_taps[tap]]
    broadcast_in_dim x0 -> x3, local copies, waits for them, and re-layouts: none -> 2.81 us  [the longest x1 0.96 us: shards(): jnp.zeros(queries.shape, jnp.float32)]
    dot_general x1, matrix products: 4.6 us -> 2.27 us  [shards(): jnp.dot(act, pointwise_weight, preferred_element_type=jnp.float32)]
    ppermute x1, waiting for transfers between devices: 0.14 us -> 1.52 us  [padded(): lax.ppermute(lax.slice_in_dim(block, 0, width, axis=dim), axis, backward)]
  transfers between devices with their start and end apart: 18 -> 18, of which waited for: 3 -> 3; matrix products, arithmetic and copies ran while one was open for 12% -> 12% of each run, Pallas kernels for 0% -> 19%
where the time goes in v4:
time: 130 us
  starting transfers between devices  53.8 us (41%)
  Pallas kernels  35.5 us (27%)
  other arithmetic  17.5 us (13%)
  local copies, waits for them, and re-layouts  10.1 us (8%)
  waiting for transfers between devices  7.83 us (6%)
  matrix products  4.3 us (3%)
    ppermute x8, starting transfers between devices, shifted_2(): return lax.ppermute(block, axis, route)  42.1 us
    pallas_call x3, Pallas kernels, absorb(): pl.pallas_call(functools.partial(absorb_kernel, nblk, final), grid=(steps...  35.5 us
    convert_element_type x1, other arithmetic, shards(): (shifted * jax.nn.sigmoid(shifted)).astype(jnp.bfloat16)  9.37 us
    ppermute x1, starting transfers between devices, padded(): lax.ppermute(lax.slice_in_dim(block, 0, width, axis=dim), axis, backward)  8.12 us
    ppermute x8, waiting for transfers between devices, shifted_2(): return lax.ppermute(block, axis, route)  6.29 us
  transfers between devices with their start and end apart: 18, of which 3 were waited for; matrix products, arithmetic and copies ran while one was open for 12% of the time, Pallas kernels for 19%

profile of v4, /device:TPU:16, one launch (start us, length us, event | category | flops | bytes accessed | tf_op | source)
XLA Modules:
  0.0 129.6 jit_solution(4849948493464198228)
XLA Ops:
  0.0 3.9 %collective-permute-start = (bf16[256,768]{1,0:T(8,128)(2,1)}, bf16[256,768]{1,0:T(8,128)(2,1)}, u32[]{:S(2)}, u32[]{:S(2)}) collective-permute-start(bf16[256,768]{1,0:T(8,128)(2,1)} %refs_0_.1), channel_id=1, source_target_pairs={{0,2},{1,3},{2,4},{3,5},{4,6},{5,7},{6,8},{7,9},{8,10},{9,11},{10,... | collective-permute-start | bytes 1179656 | tf_op jit(solution)/shard_map/ppermute | solution.py:18
  4.0 7.9 %collective-permute-start.1 = (bf16[256,768]{1,0:T(8,128)(2,1)}, bf16[256,768]{1,0:T(8,128)(2,1)}, u32[]{:S(2)}, u32[]{:S(2)}) collective-permute-start(bf16[256,768]{1,0:T(8,128)(2,1)} %refs_0_.1), channel_id=1, source_target_pairs={{2,0},{3,1},{4,2},{5,3},{6,4},{7,5},{8,6},{9,7},{10,8},{11,9},{12,... | collective-permute-start | bytes 1179656 | tf_op jit(solution)/shard_map/ppermute | solution.py:18
  11.9 1.9 %collective-permute-start.5 = (bf16[256,768]{1,0:T(8,128)(2,1)}, bf16[256,768]{1,0:T(8,128)(2,1)}, u32[]{:S(2)}, u32[]{:S(2)}) collective-permute-start(bf16[256,768]{1,0:T(8,128)(2,1)} %refs_1_.1), channel_id=1, source_target_pairs={{0,2},{1,3},{2,4},{3,5},{4,6},{5,7},{6,8},{7,9},{8,10},{9,11},{10,... | collective-permute-start | bytes 1179656 | tf_op jit(solution)/shard_map/ppermute | solution.py:18
  13.8 8.1 %collective-permute-start.6 = (bf16[256,768]{1,0:T(8,128)(2,1)}, bf16[256,768]{1,0:T(8,128)(2,1)}, u32[]{:S(2)}, u32[]{:S(2)}) collective-permute-start(bf16[256,768]{1,0:T(8,128)(2,1)} %refs_1_.1), channel_id=1, source_target_pairs={{2,0},{3,1},{4,2},{5,3},{6,4},{7,5},{8,6},{9,7},{10,8},{11,9},{12,... | collective-permute-start | bytes 1179656 | tf_op jit(solution)/shard_map/ppermute | solution.py:18
  26.7 1.9 %collective-permute-start.10 = (bf16[256,768]{1,0:T(8,128)(2,1)}, bf16[256,768]{1,0:T(8,128)(2,1)S(1)}, u32[]{:S(2)}, u32[]{:S(2)}) collective-permute-start(bf16[256,768]{1,0:T(8,128)(2,1)} %collective-permute-done.refs_0_), channel_id=1, source_target_pairs={{0,2},{1,3},{2,4},{3,5},{4,6},{5,7},{6,8},{7,9},{8,10},{9,11},{10,... | collective-permute-start | bytes 1179656 | tf_op jit(solution)/shard_map/ppermute | solution.py:18
  28.6 8.1 %collective-permute-start.11 = (bf16[256,768]{1,0:T(8,128)(2,1)}, bf16[256,768]{1,0:T(8,128)(2,1)S(1)}, u32[]{:S(2)}, u32[]{:S(2)}) collective-permute-start(bf16[256,768]{1,0:T(8,128)(2,1)} %collective-permute-done.1.refs_1_), channel_id=1, source_target_pairs={{2,0},{3,1},{4,2},{5,3},{6,4},{7,5},{8,6},{9,7},{10,8},{11,9},{12,... | collective-permute-start | bytes 1179656 | tf_op jit(solution)/shard_map/ppermute | solution.py:18
  37.5 1.9 %collective-permute-start.13 = (bf16[256,768]{1,0:T(8,128)(2,1)}, bf16[256,768]{1,0:T(8,128)(2,1)S(1)}, u32[]{:S(2)}, u32[]{:S(2)}) collective-permute-start(bf16[256,768]{1,0:T(8,128)(2,1)} %collective-permute-done.5.refs_5_), channel_id=1, source_target_pairs={{0,2},{1,3},{2,4},{3,5},{4,6},{5,7},{6,8},{7,9},{8,10},{9,11},{10,... | collective-permute-start | bytes 1179656 | tf_op jit(solution)/shard_map/ppermute | solution.py:18
  39.4 8.1 %collective-permute-start.14 = (bf16[256,768]{1,0:T(8,128)(2,1)}, bf16[256,768]{1,0:T(8,128)(2,1)S(1)}, u32[]{:S(2)}, u32[]{:S(2)}) collective-permute-start(bf16[256,768]{1,0:T(8,128)(2,1)} %collective-permute-done.6.refs_6_), channel_id=1, source_target_pairs={{2,0},{3,1},{4,2},{5,3},{6,4},{7,5},{8,6},{9,7},{10,8},{11,9},{12,... | collective-permute-start | bytes 1179656 | tf_op jit(solution)/shard_map/ppermute | solution.py:18
  49.7 5.0 %collective-permute-done.13.refs_3_ = bf16[256,768]{1,0:T(8,128)(2,1)S(1)} collective-permute-done((bf16[256,768]{1,0:T(8,128)(2,1)}, bf16[256,768]{1,0:T(8,128)(2,1)S(1)}, u32[]{:S(2)}, u32[]{:S(2)}) %collective-permute-start.13) | collective-permute-done | bytes 393248 | tf_op jit(solution)/shard_map/ppermute | solution.py:18
  54.7 1.3 collective-permute-done.14.refs_4_
  58.9 1.5 %copy.21.recq_ref = s32[256,1]{1,0:T(8,128)} copy(s32[256,1]{0,1:T(1,128)} %bitcast.15) | data formatting | bytes 2048 | tf_op jit(solution)/shard_map/sub | solution.py:35
  61.0 1.3 pad.14.reck_ref
  62.9 0.9 broadcast_in_dim.289.m_ref
  63.8 0.9 broadcast_in_dim.290.l_ref
  64.7 1.0 broadcast_in_dim.291.acc_ref
  65.7 8.8 %shard_map.118 = (f32[6,256,2]{2,1,0:T(8,128)}, f32[6,256,2]{2,1,0:T(8,128)}, f32[256,768]{1,0:T(8,128)}) custom-call(s32[256,1]{1,0:T(8,128)} %copy.21.recq_ref, s32[8,256]{1,0:T(8,128)} %pad.14.reck_ref, bf16[256,768]{1,0:T(8,128)(2,1)} %q_ref.5, f32[6,256,2]{2,1,0:T(8,128)} %broadcast_in_dim.289.m_ref, f32[6,256,2]{2,1,0:T(8,128)} %broadcast_in_dim.290.l_ref, ...), custom_call_target="tpu_custom_call" | custom-call | tf_op jit(solution)/shard_map/pallas_call | solution.py:94
  75.0 16.4 %shard_map.119 = (f32[6,256,2]{2,1,0:T(8,128)}, f32[6,256,2]{2,1,0:T(8,128)}, f32[256,768]{1,0:T(8,128)}) custom-call(s32[256,1]{1,0:T(8,128)} %copy.21.recq_ref, s32[8,256]{1,0:T(8,128)} %pad.13.reck_ref, bf16[256,768]{1,0:T(8,128)(2,1)} %q_ref.5, f32[6,256,2]{2,1,0:T(8,128)} %get-tuple-element.12.m_ref, f32[6,256,2]{2,1,0:T(8,128)} %get-tuple-element.13.l_ref, ...), custom_call_target="tpu_custom_call" | custom-call | tf_op jit(solution)/shard_map/pallas_call | solution.py:94
  91.4 10.3 %shard_map.120 = (f32[6,256,2]{2,1,0:T(8,128)}, f32[6,256,2]{2,1,0:T(8,128)}, bf16[256,768]{1,0:T(8,128)(2,1)}) custom-call(s32[256,1]{1,0:T(8,128)} %copy.21.recq_ref, s32[8,256]{1,0:T(8,128)} %pad.12.reck_ref, bf16[256,768]{1,0:T(8,128)(2,1)} %q_ref.5, f32[6,256,2]{2,1,0:T(8,128)} %get-tuple-element.15.m_ref, f32[6,256,2]{2,1,0:T(8,128)} %get-tuple-element.16.l_ref, ...), custom_call_target="tpu_custom_call" | custom-call | tf_op jit(solution)/shard_map/pallas_call | solution.py:94
  101.7 2.0 %fusion.1 = bf16[256,1536]{1,0:T(8,128)(2,1)S(1)} fusion(bf16[256,768]{1,0:T(8,128)(2,1)} %get-tuple-element.18, bf16[768,1536]{1,0:T(8,128)(2,1)S(1)} %copy-done, bf16[256,1536]{1,0:T(8,128)(2,1)} %param.12), kind=kOutput, calls=%fused_computation.3 | convolution fusion | flops 605159424 | bytes 4325376 | tf_op jit(solution)/shard_map/dot_general | solution.py:181
  104.9 2.2 %collective-permute-start.16 = (bf16[15,1536]{1,0:T(8,128)(2,1)S(1)}, bf16[15,1536]{1,0:T(8,128)(2,1)S(1)}, u32[]{:S(2)}, u32[]{:S(2)}) collective-permute-start(bf16[15,1536]{1,0:T(8,128)(2,1)S(1)} %get-tuple-element.52), channel_id=1, source_target_pairs={{0,1},{1,2},{2,3},{3,4},{4,5},{5,6},{6,7},{7,8},{8,9},{9,10},{10,1... | collective-permute-start | bytes 138248 | tf_op jit(solution)/shard_map/ppermute | solution.py:26
  107.0 8.1 %collective-permute-start.17 = (bf16[15,1536]{1,0:T(8,128)(2,1)S(1)}, bf16[15,1536]{1,0:T(8,128)(2,1)S(1)}, u32[]{:S(2)}, u32[]{:S(2)}) collective-permute-start(bf16[15,1536]{1,0:T(8,128)(2,1)S(1)} %get-tuple-element.53), channel_id=1, source_target_pairs={{1,0},{2,1},{3,2},{4,3},{5,4},{6,5},{7,6},{8,7},{9,8},{10,9},{11,1... | collective-permute-start | bytes 138248 | tf_op jit(solution)/shard_map/ppermute | solution.py:29
  115.4 1.5 %collective-permute-done.17 = bf16[15,1536]{1,0:T(8,128)(2,1)S(1)} collective-permute-done((bf16[15,1536]{1,0:T(8,128)(2,1)S(1)}, bf16[15,1536]{1,0:T(8,128)(2,1)S(1)}, u32[]{:S(2)}, u32[]{:S(2)}) %collective-permute-start.17) | collective-permute-done | bytes 46112 | tf_op jit(solution)/shard_map/ppermute | solution.py:29
  117.9 9.4 %multiply_convert_fusion = bf16[256,1536]{1,0:T(8,128)(2,1)S(1)} fusion(f32[286,1536]{1,0:T(8,128)S(1)} %convert_element_type.42, f32[1536]{0:T(1024)S(1)} %copy-done.10, f32[1536]{0:T(1024)S(1)} %copy-done.11, f32[1536]{0:T(1024)S(1)} %get-tuple-element.48, f32[1536]{0:T(1024)S(1)} %get-tuple-element.49, f32[1536]{0:T(1024)S(1)} %get-tuple-element.20, ...), kind=kLoop, calls=%fused_computation.106 | loop fusion | flops 38928384 | bytes 49755904 | tf_op jit(solution)/shard_map/convert_element_type | solution.py:206
  127.3 2.3 %fusion = bf16[256,1536]{1,0:T(8,128)(2,1)} fusion(bf16[256,1536]{1,0:T(8,128)(2,1)S(1)} %multiply_convert_fusion, bf16[1536,1536]{1,0:T(8,128)(2,1)S(1)} %bitcast.19, bf16[256,1536]{1,0:T(8,128)(2,1)S(1)} %fusion.1), kind=kOutput, calls=%fused_computation.2 | convolution fusion | flops 1209139200 | bytes 7077888 | tf_op jit(solution)/shard_map/dot_general | solution.py:207
  (121 shorter events, 14.1 us)
Async XLA Ops:
  0.0 101.7 %copy-start = (bf16[768,1536]{1,0:T(8,128)(2,1)S(1)}, bf16[768,1536]{1,0:T(8,128)(2,1)}, u32[]{:S(2)}) copy-start(bf16[768,1536]{1,0:T(8,128)(2,1)} %param.17) | copy-start | bytes 7077892
  0.0 26.6 %collective-permute-start = (bf16[256,768]{1,0:T(8,128)(2,1)}, bf16[256,768]{1,0:T(8,128)(2,1)}, u32[]{:S(2)}, u32[]{:S(2)}) collective-permute-start(bf16[256,768]{1,0:T(8,128)(2,1)} %refs_0_.1), channel_id=1, source_target_pairs={{0,2},{1,3},{2,4},{3,5},{4,6},{5,7},{6,8},{7,9},{8,10},{9,11},{10,... | collective-permute-start | bytes 1179656 | tf_op jit(solution)/shard_map/ppermute | solution.py:18
  4.0 24.6 %collective-permute-start.1 = (bf16[256,768]{1,0:T(8,128)(2,1)}, bf16[256,768]{1,0:T(8,128)(2,1)}, u32[]{:S(2)}, u32[]{:S(2)}) collective-permute-start(bf16[256,768]{1,0:T(8,128)(2,1)} %refs_0_.1), channel_id=1, source_target_pairs={{2,0},{3,1},{4,2},{5,3},{6,4},{7,5},{8,6},{9,7},{10,8},{11,9},{12,... | collective-permute-start | bytes 1179656 | tf_op jit(solution)/shard_map/ppermute | solution.py:18
  11.9 25.6 %collective-permute-start.5 = (bf16[256,768]{1,0:T(8,128)(2,1)}, bf16[256,768]{1,0:T(8,128)(2,1)}, u32[]{:S(2)}, u32[]{:S(2)}) collective-permute-start(bf16[256,768]{1,0:T(8,128)(2,1)} %refs_1_.1), channel_id=1, source_target_pairs={{0,2},{1,3},{2,4},{3,5},{4,6},{5,7},{6,8},{7,9},{8,10},{9,11},{10,... | collective-permute-start | bytes 1179656 | tf_op jit(solution)/shard_map/ppermute | solution.py:18
  13.8 25.5 %collective-permute-start.6 = (bf16[256,768]{1,0:T(8,128)(2,1)}, bf16[256,768]{1,0:T(8,128)(2,1)}, u32[]{:S(2)}, u32[]{:S(2)}) collective-permute-start(bf16[256,768]{1,0:T(8,128)(2,1)} %refs_1_.1), channel_id=1, source_target_pairs={{2,0},{3,1},{4,2},{5,3},{6,4},{7,5},{8,6},{9,7},{10,8},{11,9},{12,... | collective-permute-start | bytes 1179656 | tf_op jit(solution)/shard_map/ppermute | solution.py:18
  22.0 35.6 %collective-permute-start.2 = (bf16[256,768]{1,0:T(8,128)(2,1)}, bf16[256,768]{1,0:T(8,128)(2,1)}, u32[]{:S(2)}, u32[]{:S(2)}) collective-permute-start(bf16[256,768]{1,0:T(8,128)(2,1)} %refs_0_.1), channel_id=1, source_target_pairs={{0,1},{1,0},{2,3},{3,2},{4,5},{5,4},{6,7},{7,6},{8,9},{9,8},{10,11... | collective-permute-start | bytes 1179656 | tf_op jit(solution)/shard_map/ppermute | solution.py:150
  26.6 31.7 %copy-start.6 = (s32[256]{0:T(256)}, s32[256]{0:T(256)S(1)}, u32[]{:S(2)}) copy-start(s32[256]{0:T(256)S(1)} %convert_reduce_fusion.4) | copy-start | bytes 3076
  26.7 21.7 %collective-permute-start.10 = (bf16[256,768]{1,0:T(8,128)(2,1)}, bf16[256,768]{1,0:T(8,128)(2,1)S(1)}, u32[]{:S(2)}, u32[]{:S(2)}) collective-permute-start(bf16[256,768]{1,0:T(8,128)(2,1)} %collective-permute-done.refs_0_), channel_id=1, source_target_pairs={{0,2},{1,3},{2,4},{3,5},{4,6},{5,7},{6,8},{7,9},{8,10},{9,11},{10,... | collective-permute-start | bytes 1179656 | tf_op jit(solution)/shard_map/ppermute | solution.py:18
  28.6 19.8 %collective-permute-start.11 = (bf16[256,768]{1,0:T(8,128)(2,1)}, bf16[256,768]{1,0:T(8,128)(2,1)S(1)}, u32[]{:S(2)}, u32[]{:S(2)}) collective-permute-start(bf16[256,768]{1,0:T(8,128)(2,1)} %collective-permute-done.1.refs_1_), channel_id=1, source_target_pairs={{2,0},{3,1},{4,2},{5,3},{6,4},{7,5},{8,6},{9,7},{10,8},{11,9},{12,... | collective-permute-start | bytes 1179656 | tf_op jit(solution)/shard_map/ppermute | solution.py:18
  37.5 17.2 %collective-permute-start.13 = (bf16[256,768]{1,0:T(8,128)(2,1)}, bf16[256,768]{1,0:T(8,128)(2,1)S(1)}, u32[]{:S(2)}, u32[]{:S(2)}) collective-permute-start(bf16[256,768]{1,0:T(8,128)(2,1)} %collective-permute-done.5.refs_5_), channel_id=1, source_target_pairs={{0,2},{1,3},{2,4},{3,5},{4,6},{5,7},{6,8},{7,9},{8,10},{9,11},{10,... | collective-permute-start | bytes 1179656 | tf_op jit(solution)/shard_map/ppermute | solution.py:18
  39.4 16.6 %collective-permute-start.14 = (bf16[256,768]{1,0:T(8,128)(2,1)}, bf16[256,768]{1,0:T(8,128)(2,1)S(1)}, u32[]{:S(2)}, u32[]{:S(2)}) collective-permute-start(bf16[256,768]{1,0:T(8,128)(2,1)} %collective-permute-done.6.refs_6_), channel_id=1, source_target_pairs={{2,0},{3,1},{4,2},{5,3},{6,4},{7,5},{8,6},{9,7},{10,8},{11,9},{12,... | collective-permute-start | bytes 1179656 | tf_op jit(solution)/shard_map/ppermute | solution.py:18
  48.3 15.5 %copy-start.1 = (bf16[256,768]{1,0:T(8,128)(2,1)}, bf16[256,768]{1,0:T(8,128)(2,1)S(1)}, u32[]{:S(2)}) copy-start(bf16[256,768]{1,0:T(8,128)(2,1)S(1)} %collective-permute-done.10.refs_0_) | copy-start | bytes 1179652
  48.3 9.3 %collective-permute-start.7 = (bf16[256,768]{1,0:T(8,128)(2,1)}, bf16[256,768]{1,0:T(8,128)(2,1)}, u32[]{:S(2)}, u32[]{:S(2)}) collective-permute-start(bf16[256,768]{1,0:T(8,128)(2,1)} %refs_1_.1), channel_id=1, source_target_pairs={{0,1},{1,0},{2,3},{3,2},{4,5},{5,4},{6,7},{7,6},{8,9},{9,8},{10,11... | collective-permute-start | bytes 1179656 | tf_op jit(solution)/shard_map/ppermute | solution.py:150
  48.4 15.4 %copy-start.2 = (bf16[256,768]{1,0:T(8,128)(2,1)}, bf16[256,768]{1,0:T(8,128)(2,1)S(1)}, u32[]{:S(2)}) copy-start(bf16[256,768]{1,0:T(8,128)(2,1)S(1)} %collective-permute-done.11.refs_1_) | copy-start | bytes 1179652
  48.4 9.7 %collective-permute-start.3 = (bf16[256,768]{1,0:T(8,128)(2,1)}, bf16[256,768]{1,0:T(8,128)(2,1)}, u32[]{:S(2)}, u32[]{:S(2)}) collective-permute-start(bf16[256,768]{1,0:T(8,128)(2,1)} %collective-permute-done.refs_0_), channel_id=1, source_target_pairs={{0,1},{1,0},{2,3},{3,2},{4,5},{5,4},{6,7},{7,6},{8,9},{9,8},{10,11... | collective-permute-start | bytes 1179656 | tf_op jit(solution)/shard_map/ppermute | solution.py:150
  54.7 11.0 %copy-start.3 = (bf16[256,768]{1,0:T(8,128)(2,1)}, bf16[256,768]{1,0:T(8,128)(2,1)S(1)}, u32[]{:S(2)}) copy-start(bf16[256,768]{1,0:T(8,128)(2,1)S(1)} %collective-permute-done.13.refs_3_) | copy-start | bytes 1179652
  54.7 20.3 %collective-permute-start.4 = (bf16[256,768]{1,0:T(8,128)(2,1)}, bf16[256,768]{1,0:T(8,128)(2,1)}, u32[]{:S(2)}, u32[]{:S(2)}) collective-permute-start(bf16[256,768]{1,0:T(8,128)(2,1)} %collective-permute-done.1.refs_1_), channel_id=1, source_target_pairs={{0,1},{1,0},{2,3},{3,2},{4,5},{5,4},{6,7},{7,6},{8,9},{9,8},{10,11... | collective-permute-start | bytes 1179656 | tf_op jit(solution)/shard_map/ppermute | solution.py:150
  56.0 19.0 %collective-permute-start.8 = (bf16[256,768]{1,0:T(8,128)(2,1)}, bf16[256,768]{1,0:T(8,128)(2,1)}, u32[]{:S(2)}, u32[]{:S(2)}) collective-permute-start(bf16[256,768]{1,0:T(8,128)(2,1)} %collective-permute-done.5.refs_5_), channel_id=1, source_target_pairs={{0,1},{1,0},{2,3},{3,2},{4,5},{5,4},{6,7},{7,6},{8,9},{9,8},{10,11... | collective-permute-start | bytes 1179656 | tf_op jit(solution)/shard_map/ppermute | solution.py:150
  57.6 17.4 %collective-permute-start.9 = (bf16[256,768]{1,0:T(8,128)(2,1)}, bf16[256,768]{1,0:T(8,128)(2,1)}, u32[]{:S(2)}, u32[]{:S(2)}) collective-permute-start(bf16[256,768]{1,0:T(8,128)(2,1)} %collective-permute-done.6.refs_6_), channel_id=1, source_target_pairs={{0,1},{1,0},{2,3},{3,2},{4,5},{5,4},{6,7},{7,6},{8,9},{9,8},{10,11... | collective-permute-start | bytes 1179656 | tf_op jit(solution)/shard_map/ppermute | solution.py:150
  57.6 33.9 %collective-permute-start.12 = (bf16[256,768]{1,0:T(8,128)(2,1)}, bf16[256,768]{1,0:T(8,128)(2,1)}, u32[]{:S(2)}, u32[]{:S(2)}) collective-permute-start(bf16[256,768]{1,0:T(8,128)(2,1)} %broadcast_select_fusion.1), channel_id=1, source_target_pairs={{0,1},{1,0},{2,3},{3,2},{4,5},{5,4},{6,7},{7,6},{8,9},{9,8},{10,11... | collective-permute-start | bytes 1179656 | tf_op jit(solution)/shard_map/ppermute | solution.py:150
  58.1 33.4 %collective-permute-start.15 = (bf16[256,768]{1,0:T(8,128)(2,1)}, bf16[256,768]{1,0:T(8,128)(2,1)}, u32[]{:S(2)}, u32[]{:S(2)}) collective-permute-start(bf16[256,768]{1,0:T(8,128)(2,1)} %broadcast_select_fusion), channel_id=1, source_target_pairs={{0,1},{1,0},{2,3},{3,2},{4,5},{5,4},{6,7},{7,6},{8,9},{9,8},{10,11... | collective-permute-start | bytes 1179656 | tf_op jit(solution)/shard_map/ppermute | solution.py:150
  104.9 10.5 %collective-permute-start.16 = (bf16[15,1536]{1,0:T(8,128)(2,1)S(1)}, bf16[15,1536]{1,0:T(8,128)(2,1)S(1)}, u32[]{:S(2)}, u32[]{:S(2)}) collective-permute-start(bf16[15,1536]{1,0:T(8,128)(2,1)S(1)} %get-tuple-element.52), channel_id=1, source_target_pairs={{0,1},{1,2},{2,3},{3,4},{4,5},{5,6},{6,7},{7,8},{8,9},{9,10},{10,1... | collective-permute-start | bytes 138248 | tf_op jit(solution)/shard_map/ppermute | solution.py:26
  107.0 9.9 %collective-permute-start.17 = (bf16[15,1536]{1,0:T(8,128)(2,1)S(1)}, bf16[15,1536]{1,0:T(8,128)(2,1)S(1)}, u32[]{:S(2)}, u32[]{:S(2)}) collective-permute-start(bf16[15,1536]{1,0:T(8,128)(2,1)S(1)} %get-tuple-element.53), channel_id=1, source_target_pairs={{1,0},{2,1},{3,2},{4,3},{5,4},{6,5},{7,6},{8,7},{9,8},{10,9},{11,1... | collective-permute-start | bytes 138248 | tf_op jit(solution)/shard_map/ppermute | solution.py:29
  117.3 10.1 %slice-start = ((s8[4718592]{0:T(1024)(128)(4,1)}), s8[4194304]{0:T(1024)(128)(4,1)S(1)}, s32[]{:S(2)}) async-start(s8[4718592]{0:T(1024)(128)(4,1)} %bitcast.18), calls=%async_computation | async-start | bytes 8388608
  (21 other events, 39.8 us)

commit v5 on v3

--- a/solution.py
+++ b/solution.py
@@ -44,34 +44,49 @@
 NBLK = 2 * REACH + 1
 
 
+def fold_lanes(x, op):
+    width = x.shape[1]
+    out = x[:, :128]
+    for c in range(128, width, 128):
+        out = op(out, x[:, c : c + 128])
+    return out
+
+
 def attend_kernel(recq_ref, reck_ref, q_ref, *refs):
     k_refs = refs[:NBLK]
     v_refs = refs[NBLK : 2 * NBLK]
     out_ref = refs[2 * NBLK]
-    s_scr = refs[2 * NBLK + 1]
-    rec_q = recq_ref[...]
+    s_scr, bias_scr = refs[2 * NBLK + 1 :]
+
+    @pl.when(pl.program_id(0) == 0)
+    def _():
+        rec_q = recq_ref[...]
+        for j in range(NBLK):
+            bias_scr[j] = jnp.where(rec_q == reck_ref[j : j + 1, :], 0.0, -1e30)
+
     for hh in range(2):
         cols = slice(hh * HD, (hh + 1) * HD)
         q_h = q_ref[:, cols]
-        top = None
+        wide_top = None
         for j in range(NBLK):
             s = lax.dot_general(
                 q_h, k_refs[j][:, cols], (((1,), (1,)), ((), ())),
                 preferred_element_type=jnp.float32,
-            ) * (HD ** (-0.5))
-            s = jnp.where(rec_q == reck_ref[j : j + 1, :], s, -1e30)
+            ) * (HD ** (-0.5)) + bias_scr[j]
             s_scr[j] = s
-            row = jnp.max(s, axis=1, keepdims=True)
-            top = row if top is None else jnp.maximum(top, row)
-        total = None
+            part = fold_lanes(s, jnp.maximum)
+            wide_top = part if wide_top is None else jnp.maximum(wide_top, part)
+        top = jnp.max(wide_top, axis=1, keepdims=True)
+        wide_total = None
         acc = None
         for j in range(NBLK):
             p = jnp.exp(s_scr[j] - top)
-            part = jnp.sum(p, axis=1, keepdims=True)
+            part = fold_lanes(p, jnp.add)
             prod = jnp.dot(p.astype(jnp.bfloat16), v_refs[j][:, cols],
                            preferred_element_type=jnp.float32)
-            total = part if total is None else total + part
+            wide_total = part if wide_total is None else wide_total + part
             acc = prod if acc is None else acc + prod
+        total = jnp.sum(wide_total, axis=1, keepdims=True)
         out_ref[:, cols] = (acc / total).astype(out_ref.dtype)
 
 
@@ -90,7 +105,7 @@
         + [tile] * (2 * NBLK),
         out_specs=tile,
         out_shape=jax.ShapeDtypeStruct((frames, width), jnp.bfloat16),
-        scratch_shapes=[pltpu.VMEM((NBLK, frames, frames), jnp.float32)],
+        scratch_shapes=[pltpu.VMEM((NBLK, frames, frames), jnp.float32)] * 2,
     )(rec_q, rec_k, query, *keys, *vals)
 
 

time: 115 us -> 111 us (0.965)
  Pallas kernels: 20.2 us -> 16.2 us
    pallas_call x1, Pallas kernels: 20.2 us -> 16.2 us  [attend(): pl.pallas_call(attend_kernel, grid=(width // pair,), in_specs=[pl.BlockSp...]
where the time goes in v5:
time: 111 us; the launch traced here: 110 us
  starting transfers between devices  54 us (49%)
  other arithmetic  17.7 us (16%)
  Pallas kernels  16.2 us (15%)
  local copies, waits for them, and re-layouts  8.2 us (7%)
  matrix products  6.64 us (6%)
  waiting for transfers between devices  6.5 us (6%)
    ppermute x8, starting transfers between devices, shifted_2(): return lax.ppermute(block, axis, route)  42.1 us
    pallas_call x1, Pallas kernels, attend(): pl.pallas_call(attend_kernel, grid=(width // pair,), in_specs=[pl.BlockSp...  16.2 us
    convert_element_type x1, other arithmetic, shards(): (shifted * jax.nn.sigmoid(shifted)).astype(jnp.bfloat16)  9.78 us
    ppermute x1, starting transfers between devices, padded(): lax.ppermute(lax.slice_in_dim(block, 0, width, axis=dim), axis, backward)  8.31 us
    ppermute x8, waiting for transfers between devices, shifted_2(): return lax.ppermute(block, axis, route)  6.34 us
    dot_general x1, matrix products, shards(): jnp.dot(act, pointwise_weight, preferred_element_type=jnp.float32)  4.6 us
    slice x2, local copies, waits for them, and re-layouts, shards(): depthwise_taps[tap]  3.8 us
    ppermute x1, starting transfers between devices, padded(): lax.ppermute(lax.slice_in_dim(block, block.shape[dim] - width, None, axis...  2.32 us
  transfers between devices with their start and end apart: 18, of which 3 were waited for; matrix products, arithmetic and copies ran while one was open for 12% of the time, Pallas kernels for 0%

profile of v5, /device:TPU:16, one launch (start us, length us, event | category | flops | bytes accessed | tf_op | source)
XLA Modules:
  0.0 110.1 jit_solution(6860640782920112472)
XLA Ops:
  0.0 3.9 %collective-permute-start.8 = (bf16[256,768]{1,0:T(8,128)(2,1)}, bf16[256,768]{1,0:T(8,128)(2,1)}, u32[]{:S(2)}, u32[]{:S(2)}) collective-permute-start(bf16[256,768]{1,0:T(8,128)(2,1)} %refs_9_.1), channel_id=1, source_target_pairs={{0,2},{1,3},{2,4},{3,5},{4,6},{5,7},{6,8},{7,9},{8,10},{9,11},{10,... | collective-permute-start | bytes 1179656 | tf_op jit(solution)/shard_map/ppermute | solution.py:16
  4.0 7.9 %collective-permute-start.9 = (bf16[256,768]{1,0:T(8,128)(2,1)}, bf16[256,768]{1,0:T(8,128)(2,1)}, u32[]{:S(2)}, u32[]{:S(2)}) collective-permute-start(bf16[256,768]{1,0:T(8,128)(2,1)} %refs_9_.1), channel_id=1, source_target_pairs={{2,0},{3,1},{4,2},{5,3},{6,4},{7,5},{8,6},{9,7},{10,8},{11,9},{12,... | collective-permute-start | bytes 1179656 | tf_op jit(solution)/shard_map/ppermute | solution.py:16
  11.9 1.9 %collective-permute-start = (bf16[256,768]{1,0:T(8,128)(2,1)}, bf16[256,768]{1,0:T(8,128)(2,1)}, u32[]{:S(2)}, u32[]{:S(2)}) collective-permute-start(bf16[256,768]{1,0:T(8,128)(2,1)} %refs_0_.1), channel_id=1, source_target_pairs={{0,2},{1,3},{2,4},{3,5},{4,6},{5,7},{6,8},{7,9},{8,10},{9,11},{10,... | collective-permute-start | bytes 1179656 | tf_op jit(solution)/shard_map/ppermute | solution.py:16
  13.8 8.1 %collective-permute-start.1 = (bf16[256,768]{1,0:T(8,128)(2,1)}, bf16[256,768]{1,0:T(8,128)(2,1)}, u32[]{:S(2)}, u32[]{:S(2)}) collective-permute-start(bf16[256,768]{1,0:T(8,128)(2,1)} %refs_0_.1), channel_id=1, source_target_pairs={{2,0},{3,1},{4,2},{5,3},{6,4},{7,5},{8,6},{9,7},{10,8},{11,9},{12,... | collective-permute-start | bytes 1179656 | tf_op jit(solution)/shard_map/ppermute | solution.py:16
  22.3 0.8 copy.16
  24.0 1.4 %convert_reduce_fusion.1 = s32[2304]{0:T(1024)S(1)} fusion(s32[128]{0:T(128)S(1)} %sub.49, s32[2304]{0:T(1024)S(1)} %add.220), kind=kLoop, calls=%fused_computation.107 | loop fusion | flops 882432 | bytes 18944 | tf_op jit(solution)/shard_map/reduce_sum | solution.py:33
  26.4 1.9 %collective-permute-start.10 = (bf16[256,768]{1,0:T(8,128)(2,1)}, bf16[256,768]{1,0:T(8,128)(2,1)S(1)}, u32[]{:S(2)}, u32[]{:S(2)}) collective-permute-start(bf16[256,768]{1,0:T(8,128)(2,1)} %collective-permute-done.8.refs_10_), channel_id=1, source_target_pairs={{0,2},{1,3},{2,4},{3,5},{4,6},{5,7},{6,8},{7,9},{8,10},{9,11},{10,... | collective-permute-start | bytes 1179656 | tf_op jit(solution)/shard_map/ppermute | solution.py:16
  28.3 8.1 %collective-permute-start.11 = (bf16[256,768]{1,0:T(8,128)(2,1)}, bf16[256,768]{1,0:T(8,128)(2,1)S(1)}, u32[]{:S(2)}, u32[]{:S(2)}) collective-permute-start(bf16[256,768]{1,0:T(8,128)(2,1)} %collective-permute-done.9.refs_11_), channel_id=1, source_target_pairs={{2,0},{3,1},{4,2},{5,3},{6,4},{7,5},{8,6},{9,7},{10,8},{11,9},{12,... | collective-permute-start | bytes 1179656 | tf_op jit(solution)/shard_map/ppermute | solution.py:16
  36.7 1.9 %collective-permute-start.2 = (bf16[256,768]{1,0:T(8,128)(2,1)}, bf16[256,768]{1,0:T(8,128)(2,1)S(1)}, u32[]{:S(2)}, u32[]{:S(2)}) collective-permute-start(bf16[256,768]{1,0:T(8,128)(2,1)} %collective-permute-done.refs_1_), channel_id=1, source_target_pairs={{0,2},{1,3},{2,4},{3,5},{4,6},{5,7},{6,8},{7,9},{8,10},{9,11},{10,... | collective-permute-start | bytes 1179656 | tf_op jit(solution)/shard_map/ppermute | solution.py:16
  38.6 8.1 %collective-permute-start.3 = (bf16[256,768]{1,0:T(8,128)(2,1)}, bf16[256,768]{1,0:T(8,128)(2,1)S(1)}, u32[]{:S(2)}, u32[]{:S(2)}) collective-permute-start(bf16[256,768]{1,0:T(8,128)(2,1)} %collective-permute-done.1.refs_2_), channel_id=1, source_target_pairs={{2,0},{3,1},{4,2},{5,3},{6,4},{7,5},{8,6},{9,7},{10,8},{11,9},{12,... | collective-permute-start | bytes 1179656 | tf_op jit(solution)/shard_map/ppermute | solution.py:16
  48.1 0.8 broadcast_select_fusion
  48.9 5.0 %collective-permute-done.2.refs_3_ = bf16[256,768]{1,0:T(8,128)(2,1)S(1)} collective-permute-done((bf16[256,768]{1,0:T(8,128)(2,1)}, bf16[256,768]{1,0:T(8,128)(2,1)S(1)}, u32[]{:S(2)}, u32[]{:S(2)}) %collective-permute-start.2) | collective-permute-done | bytes 393248 | tf_op jit(solution)/shard_map/ppermute | solution.py:16
  53.9 1.3 %collective-permute-done.3.refs_4_ = bf16[256,768]{1,0:T(8,128)(2,1)S(1)} collective-permute-done((bf16[256,768]{1,0:T(8,128)(2,1)}, bf16[256,768]{1,0:T(8,128)(2,1)S(1)}, u32[]{:S(2)}, u32[]{:S(2)}) %collective-permute-start.3) | collective-permute-done | bytes 393248 | tf_op jit(solution)/shard_map/ppermute | solution.py:16
  56.0 0.8 broadcast_select_fusion.1
  57.4 0.8 copy.17.recq_ref
  58.2 1.3 %pad.4.reck_ref = s32[16,256]{1,0:T(8,128)} pad(s32[9,256]{1,0:T(8,128)} %broadcast_select_fusion.2, s32[]{:T(128)} %constant.55.clone.1), padding=0_7x0_0 | pad | bytes 25604 | tf_op jit(solution)/shard_map/jit(_pad)/pad | solution.py:160
  59.5 2.4 %slice_reduce_fusion.30 = (f32[1536]{0:T(1024)S(1)}, f32[1536]{0:T(1024)}, f32[1536]{0:T(1024)}, f32[1536]{0:T(1024)}, f32[1536]{0:T(1024)}, /*index=5*/f32[1536...) fusion(f32[31,1536]{1,0:T(8,128)} %param.20), kind=kLoop, calls=%fused_computation.145 | loop fusion | bytes 233472 | tf_op jit(solution)/shard_map/slice | solution.py:186
  62.7 16.2 %shard_map.118 = bf16[256,768]{1,0:T(8,128)(2,1)} custom-call(s32[256,1]{1,0:T(8,128)} %copy.17.recq_ref, s32[16,256]{1,0:T(8,128)} %pad.4.reck_ref, bf16[256,768]{1,0:T(8,128)(2,1)} %q_ref.1, bf16[256,768]{1,0:T(8,128)(2,1)} %refs_0_.1, bf16[256,768]{1,0:T(8,128)(2,1)} %collective-permute-done.refs_1_, bf16[256,768]{1,0:T(8,128)(2,1)} %collective-permute-done.1.refs_2_, ...), custom_call_target="tpu_custom_call" | custom-call | tf_op jit(solution)/shard_map/pallas_call | solution.py:97
  79.0 2.0 %fusion.1 = bf16[256,1536]{1,0:T(8,128)(2,1)S(1)} fusion(bf16[256,768]{1,0:T(8,128)(2,1)} %shard_map.118, bf16[768,1536]{1,0:T(8,128)(2,1)S(1)} %copy-done, bf16[256,1536]{1,0:T(8,128)(2,1)} %param.12), kind=kOutput, calls=%fused_computation.3 | convolution fusion | flops 605159424 | bytes 4325376 | tf_op jit(solution)/shard_map/dot_general | solution.py:164
  82.1 2.3 %collective-permute-start.16 = (bf16[15,1536]{1,0:T(8,128)(2,1)S(1)}, bf16[15,1536]{1,0:T(8,128)(2,1)S(1)}, u32[]{:S(2)}, u32[]{:S(2)}) collective-permute-start(bf16[15,1536]{1,0:T(8,128)(2,1)S(1)} %get-tuple-element.36), channel_id=1, source_target_pairs={{0,1},{1,2},{2,3},{3,4},{4,5},{5,6},{6,7},{7,8},{8,9},{9,10},{10,1... | collective-permute-start | bytes 138248 | tf_op jit(solution)/shard_map/ppermute | solution.py:24
  84.4 8.3 %collective-permute-start.17 = (bf16[15,1536]{1,0:T(8,128)(2,1)S(1)}, bf16[15,1536]{1,0:T(8,128)(2,1)S(1)}, u32[]{:S(2)}, u32[]{:S(2)}) collective-permute-start(bf16[15,1536]{1,0:T(8,128)(2,1)S(1)} %get-tuple-element.37), channel_id=1, source_target_pairs={{1,0},{2,1},{3,2},{4,3},{5,4},{6,5},{7,6},{8,7},{9,8},{10,9},{11,1... | collective-permute-start | bytes 138248 | tf_op jit(solution)/shard_map/ppermute | solution.py:27
  92.8 1.4 %slice_reduce_fusion.29 = (f32[1536]{0:T(1024)S(1)}, f32[1536]{0:T(1024)S(1)}, f32[1536]{0:T(1024)S(1)}, f32[1536]{0:T(1024)S(1)}, f32[1536]{0:T(1024)S(1)}, /*i...) fusion(f32[31,1536]{1,0:T(8,128)} %param.20), kind=kLoop, calls=%fused_computation.144 | loop fusion | bytes 147456 | tf_op jit(solution)/shard_map/slice | solution.py:186
  95.7 9.8 %multiply_convert_fusion = bf16[256,1536]{1,0:T(8,128)(2,1)S(1)} fusion(f32[286,1536]{1,0:T(8,128)S(1)} %convert_element_type.37, f32[1536]{0:T(1024)S(1)} %copy-done.25, f32[1536]{0:T(1024)S(1)} %copy-done.26, f32[1536]{0:T(1024)S(1)} %get-tuple-element.34, f32[1536]{0:T(1024)S(1)} %get-tuple-element.35, f32[1536]{0:T(1024)S(1)} %copy-done.5, ...), kind=kLoop, calls=%fused_computation.106 | loop fusion | flops 38928384 | bytes 49755904 | tf_op jit(solution)/shard_map/convert_element_type | solution.py:189
  105.5 4.6 %fusion = bf16[256,1536]{1,0:T(8,128)(2,1)} fusion(bf16[256,1536]{1,0:T(8,128)(2,1)S(1)} %multiply_convert_fusion, bf16[1536,1536]{1,0:T(8,128)(2,1)} %param.23, bf16[256,1536]{1,0:T(8,128)(2,1)S(1)} %fusion.1), kind=kOutput, calls=%fused_computation.2 | convolution fusion | flops 1209139200 | bytes 7077888 | tf_op jit(solution)/shard_map/dot_general | solution.py:190
  (145 shorter events, 7.8 us)
Async XLA Ops:
  0.0 78.9 %copy-start = (bf16[768,1536]{1,0:T(8,128)(2,1)S(1)}, bf16[768,1536]{1,0:T(8,128)(2,1)}, u32[]{:S(2)}) copy-start(bf16[768,1536]{1,0:T(8,128)(2,1)} %param.17) | copy-start | bytes 7077892
  0.0 26.4 %collective-permute-start.8 = (bf16[256,768]{1,0:T(8,128)(2,1)}, bf16[256,768]{1,0:T(8,128)(2,1)}, u32[]{:S(2)}, u32[]{:S(2)}) collective-permute-start(bf16[256,768]{1,0:T(8,128)(2,1)} %refs_9_.1), channel_id=1, source_target_pairs={{0,2},{1,3},{2,4},{3,5},{4,6},{5,7},{6,8},{7,9},{8,10},{9,11},{10,... | collective-permute-start | bytes 1179656 | tf_op jit(solution)/shard_map/ppermute | solution.py:16
  4.0 24.4 %collective-permute-start.9 = (bf16[256,768]{1,0:T(8,128)(2,1)}, bf16[256,768]{1,0:T(8,128)(2,1)}, u32[]{:S(2)}, u32[]{:S(2)}) collective-permute-start(bf16[256,768]{1,0:T(8,128)(2,1)} %refs_9_.1), channel_id=1, source_target_pairs={{2,0},{3,1},{4,2},{5,3},{6,4},{7,5},{8,6},{9,7},{10,8},{11,9},{12,... | collective-permute-start | bytes 1179656 | tf_op jit(solution)/shard_map/ppermute | solution.py:16
  11.9 24.8 %collective-permute-start = (bf16[256,768]{1,0:T(8,128)(2,1)}, bf16[256,768]{1,0:T(8,128)(2,1)}, u32[]{:S(2)}, u32[]{:S(2)}) collective-permute-start(bf16[256,768]{1,0:T(8,128)(2,1)} %refs_0_.1), channel_id=1, source_target_pairs={{0,2},{1,3},{2,4},{3,5},{4,6},{5,7},{6,8},{7,9},{8,10},{9,11},{10,... | collective-permute-start | bytes 1179656 | tf_op jit(solution)/shard_map/ppermute | solution.py:16
  13.8 24.8 %collective-permute-start.1 = (bf16[256,768]{1,0:T(8,128)(2,1)}, bf16[256,768]{1,0:T(8,128)(2,1)}, u32[]{:S(2)}, u32[]{:S(2)}) collective-permute-start(bf16[256,768]{1,0:T(8,128)(2,1)} %refs_0_.1), channel_id=1, source_target_pairs={{2,0},{3,1},{4,2},{5,3},{6,4},{7,5},{8,6},{9,7},{10,8},{11,9},{12,... | collective-permute-start | bytes 1179656 | tf_op jit(solution)/shard_map/ppermute | solution.py:16
  22.0 34.8 %collective-permute-start.12 = (bf16[256,768]{1,0:T(8,128)(2,1)}, bf16[256,768]{1,0:T(8,128)(2,1)}, u32[]{:S(2)}, u32[]{:S(2)}) collective-permute-start(bf16[256,768]{1,0:T(8,128)(2,1)} %refs_9_.1), channel_id=1, source_target_pairs={{0,1},{1,0},{2,3},{3,2},{4,5},{5,4},{6,7},{7,6},{8,9},{9,8},{10,11... | collective-permute-start | bytes 1179656 | tf_op jit(solution)/shard_map/ppermute | solution.py:148
  26.4 21.1 %collective-permute-start.10 = (bf16[256,768]{1,0:T(8,128)(2,1)}, bf16[256,768]{1,0:T(8,128)(2,1)S(1)}, u32[]{:S(2)}, u32[]{:S(2)}) collective-permute-start(bf16[256,768]{1,0:T(8,128)(2,1)} %collective-permute-done.8.refs_10_), channel_id=1, source_target_pairs={{0,2},{1,3},{2,4},{3,5},{4,6},{5,7},{6,8},{7,9},{8,10},{9,11},{10,... | collective-permute-start | bytes 1179656 | tf_op jit(solution)/shard_map/ppermute | solution.py:16
  28.3 19.3 %collective-permute-start.11 = (bf16[256,768]{1,0:T(8,128)(2,1)}, bf16[256,768]{1,0:T(8,128)(2,1)S(1)}, u32[]{:S(2)}, u32[]{:S(2)}) collective-permute-start(bf16[256,768]{1,0:T(8,128)(2,1)} %collective-permute-done.9.refs_11_), channel_id=1, source_target_pairs={{2,0},{3,1},{4,2},{5,3},{6,4},{7,5},{8,6},{9,7},{10,8},{11,9},{12,... | collective-permute-start | bytes 1179656 | tf_op jit(solution)/shard_map/ppermute | solution.py:16
  36.7 17.2 %collective-permute-start.2 = (bf16[256,768]{1,0:T(8,128)(2,1)}, bf16[256,768]{1,0:T(8,128)(2,1)S(1)}, u32[]{:S(2)}, u32[]{:S(2)}) collective-permute-start(bf16[256,768]{1,0:T(8,128)(2,1)} %collective-permute-done.refs_1_), channel_id=1, source_target_pairs={{0,2},{1,3},{2,4},{3,5},{4,6},{5,7},{6,8},{7,9},{8,10},{9,11},{10,... | collective-permute-start | bytes 1179656 | tf_op jit(solution)/shard_map/ppermute | solution.py:16
  38.6 16.6 %collective-permute-start.3 = (bf16[256,768]{1,0:T(8,128)(2,1)}, bf16[256,768]{1,0:T(8,128)(2,1)S(1)}, u32[]{:S(2)}, u32[]{:S(2)}) collective-permute-start(bf16[256,768]{1,0:T(8,128)(2,1)} %collective-permute-done.1.refs_2_), channel_id=1, source_target_pairs={{2,0},{3,1},{4,2},{5,3},{6,4},{7,5},{8,6},{9,7},{10,8},{11,9},{12,... | collective-permute-start | bytes 1179656 | tf_op jit(solution)/shard_map/ppermute | solution.py:16
  47.5 15.2 %copy-start.1 = (bf16[256,768]{1,0:T(8,128)(2,1)}, bf16[256,768]{1,0:T(8,128)(2,1)S(1)}, u32[]{:S(2)}) copy-start(bf16[256,768]{1,0:T(8,128)(2,1)S(1)} %collective-permute-done.10.refs_12_) | copy-start | bytes 1179652
  47.5 9.3 %collective-permute-start.4 = (bf16[256,768]{1,0:T(8,128)(2,1)}, bf16[256,768]{1,0:T(8,128)(2,1)}, u32[]{:S(2)}, u32[]{:S(2)}) collective-permute-start(bf16[256,768]{1,0:T(8,128)(2,1)} %refs_0_.1), channel_id=1, source_target_pairs={{0,1},{1,0},{2,3},{3,2},{4,5},{5,4},{6,7},{7,6},{8,9},{9,8},{10,11... | collective-permute-start | bytes 1179656 | tf_op jit(solution)/shard_map/ppermute | solution.py:148
  47.6 15.1 %copy-start.2 = (bf16[256,768]{1,0:T(8,128)(2,1)}, bf16[256,768]{1,0:T(8,128)(2,1)S(1)}, u32[]{:S(2)}) copy-start(bf16[256,768]{1,0:T(8,128)(2,1)S(1)} %collective-permute-done.11.refs_13_) | copy-start | bytes 1179652
  47.6 9.7 %collective-permute-start.13 = (bf16[256,768]{1,0:T(8,128)(2,1)}, bf16[256,768]{1,0:T(8,128)(2,1)}, u32[]{:S(2)}, u32[]{:S(2)}) collective-permute-start(bf16[256,768]{1,0:T(8,128)(2,1)} %collective-permute-done.8.refs_10_), channel_id=1, source_target_pairs={{0,1},{1,0},{2,3},{3,2},{4,5},{5,4},{6,7},{7,6},{8,9},{9,8},{10,11... | collective-permute-start | bytes 1179656 | tf_op jit(solution)/shard_map/ppermute | solution.py:148
  53.9 8.8 %copy-start.3 = (bf16[256,768]{1,0:T(8,128)(2,1)}, bf16[256,768]{1,0:T(8,128)(2,1)S(1)}, u32[]{:S(2)}) copy-start(bf16[256,768]{1,0:T(8,128)(2,1)S(1)} %collective-permute-done.2.refs_3_) | copy-start | bytes 1179652
  53.9 8.7 %collective-permute-start.14 = (bf16[256,768]{1,0:T(8,128)(2,1)}, bf16[256,768]{1,0:T(8,128)(2,1)}, u32[]{:S(2)}, u32[]{:S(2)}) collective-permute-start(bf16[256,768]{1,0:T(8,128)(2,1)} %collective-permute-done.9.refs_11_), channel_id=1, source_target_pairs={{0,1},{1,0},{2,3},{3,2},{4,5},{5,4},{6,7},{7,6},{8,9},{9,8},{10,11... | collective-permute-start | bytes 1179656 | tf_op jit(solution)/shard_map/ppermute | solution.py:148
  55.2 7.4 %collective-permute-start.5 = (bf16[256,768]{1,0:T(8,128)(2,1)}, bf16[256,768]{1,0:T(8,128)(2,1)}, u32[]{:S(2)}, u32[]{:S(2)}) collective-permute-start(bf16[256,768]{1,0:T(8,128)(2,1)} %collective-permute-done.refs_1_), channel_id=1, source_target_pairs={{0,1},{1,0},{2,3},{3,2},{4,5},{5,4},{6,7},{7,6},{8,9},{9,8},{10,11... | collective-permute-start | bytes 1179656 | tf_op jit(solution)/shard_map/ppermute | solution.py:148
  56.8 5.9 %collective-permute-start.6 = (bf16[256,768]{1,0:T(8,128)(2,1)}, bf16[256,768]{1,0:T(8,128)(2,1)}, u32[]{:S(2)}, u32[]{:S(2)}) collective-permute-start(bf16[256,768]{1,0:T(8,128)(2,1)} %collective-permute-done.1.refs_2_), channel_id=1, source_target_pairs={{0,1},{1,0},{2,3},{3,2},{4,5},{5,4},{6,7},{7,6},{8,9},{9,8},{10,11... | collective-permute-start | bytes 1179656 | tf_op jit(solution)/shard_map/ppermute | solution.py:148
  56.8 5.9 %collective-permute-start.15 = (bf16[256,768]{1,0:T(8,128)(2,1)}, bf16[256,768]{1,0:T(8,128)(2,1)}, u32[]{:S(2)}, u32[]{:S(2)}) collective-permute-start(bf16[256,768]{1,0:T(8,128)(2,1)} %broadcast_select_fusion), channel_id=1, source_target_pairs={{0,1},{1,0},{2,3},{3,2},{4,5},{5,4},{6,7},{7,6},{8,9},{9,8},{10,11... | collective-permute-start | bytes 1179656 | tf_op jit(solution)/shard_map/ppermute | solution.py:148
  57.3 5.4 %collective-permute-start.7 = (bf16[256,768]{1,0:T(8,128)(2,1)}, bf16[256,768]{1,0:T(8,128)(2,1)}, u32[]{:S(2)}, u32[]{:S(2)}) collective-permute-start(bf16[256,768]{1,0:T(8,128)(2,1)} %broadcast_select_fusion.1), channel_id=1, source_target_pairs={{0,1},{1,0},{2,3},{3,2},{4,5},{5,4},{6,7},{7,6},{8,9},{9,8},{10,11... | collective-permute-start | bytes 1179656 | tf_op jit(solution)/shard_map/ppermute | solution.py:148
  82.1 12.0 %collective-permute-start.16 = (bf16[15,1536]{1,0:T(8,128)(2,1)S(1)}, bf16[15,1536]{1,0:T(8,128)(2,1)S(1)}, u32[]{:S(2)}, u32[]{:S(2)}) collective-permute-start(bf16[15,1536]{1,0:T(8,128)(2,1)S(1)} %get-tuple-element.36), channel_id=1, source_target_pairs={{0,1},{1,2},{2,3},{3,4},{4,5},{5,6},{6,7},{7,8},{8,9},{9,10},{10,1... | collective-permute-start | bytes 138248 | tf_op jit(solution)/shard_map/ppermute | solution.py:24
  84.4 9.9 %collective-permute-start.17 = (bf16[15,1536]{1,0:T(8,128)(2,1)S(1)}, bf16[15,1536]{1,0:T(8,128)(2,1)S(1)}, u32[]{:S(2)}, u32[]{:S(2)}) collective-permute-start(bf16[15,1536]{1,0:T(8,128)(2,1)S(1)} %get-tuple-element.37), channel_id=1, source_target_pairs={{1,0},{2,1},{3,2},{4,3},{5,4},{6,5},{7,6},{8,7},{9,8},{10,9},{11,1... | collective-permute-start | bytes 138248 | tf_op jit(solution)/shard_map/ppermute | solution.py:27
  94.7 0.8 copy-start.25
  94.7 0.8 copy-start.26
  (41 other events, 31.3 us)

commit v6 on v5

--- a/solution.py
+++ b/solution.py
@@ -172,7 +172,19 @@
         jnp.bfloat16
     )
     rim_width = (depthwise_taps.shape[0] - 1) // 2
-    extended = padded(normed, ((("grp", "blk"), 0),), rim_width)
+    head_rows = normed[:rim_width]
+    tail_rows = normed[frames - rim_width :]
+    cross = [(i, i + 1) for i in range(1, nblocks - 1, 2)]
+    cross = cross + [(j, i) for i, j in cross]
+    over_link = lax.ppermute(
+        lax.select(parity == 0, head_rows, tail_rows), ("grp", "blk"), cross
+    )
+    on_chip = lax.ppermute(
+        lax.select(parity == 0, tail_rows, head_rows), ("grp", "blk"), swap
+    )
+    low = lax.select(parity == 0, over_link, on_chip)
+    high = lax.select(parity == 0, on_chip, over_link)
+    extended = jnp.concatenate([low, normed, high], axis=0)
     ext_positions = (
         block_here * frames - rim_width + jnp.arange(frames + 2 * rim_width, dtype=jnp.int32)
     )

time: 111 us -> 110 us (level)
  starting transfers between devices: 54 us -> 52.2 us
    ppermute x2, starting transfers between devices: 10.6 us -> 8.8 us  [the longest x1 8.53 us: shards(): lax.ppermute(lax.select(parity == 0, head_rows, tail_rows), ('grp', 'blk'...]
where the time goes in v6:
time: 110 us; the launch traced here: 108 us
  starting transfers between devices  52.2 us (47%)
  other arithmetic  17.7 us (16%)
  Pallas kernels  16.2 us (15%)
  local copies, waits for them, and re-layouts  8.19 us (7%)
  matrix products  6.64 us (6%)
  waiting for transfers between devices  6.44 us (6%)
    ppermute x8, starting transfers between devices, shifted_2(): return lax.ppermute(block, axis, route)  42.1 us
    pallas_call x1, Pallas kernels, attend(): pl.pallas_call(attend_kernel, grid=(width // pair,), in_specs=[pl.BlockSp...  16.2 us
    convert_element_type x1, other arithmetic, shards(): (shifted * jax.nn.sigmoid(shifted)).astype(jnp.bfloat16)  9.78 us
    ppermute x1, starting transfers between devices, shards(): lax.ppermute(lax.select(parity == 0, head_rows, tail_rows), ('grp', 'blk'...  8.53 us
    ppermute x8, waiting for transfers between devices, shifted_2(): return lax.ppermute(block, axis, route)  6.34 us
    dot_general x1, matrix products, shards(): jnp.dot(act, pointwise_weight, preferred_element_type=jnp.float32)  4.6 us
    slice x2, local copies, waits for them, and re-layouts, shards(): depthwise_taps[tap]  3.8 us
  transfers between devices with their start and end apart: 18, of which 3 were waited for; matrix products, arithmetic and copies ran while one was open for 12% of the time, Pallas kernels for 0%

profile of v6, /device:TPU:16, one launch (start us, length us, event | category | flops | bytes accessed | tf_op | source)
XLA Modules:
  0.0 108.2 jit_solution(8837009449974558133)
XLA Ops:
  0.0 3.9 %collective-permute-start.8 = (bf16[256,768]{1,0:T(8,128)(2,1)}, bf16[256,768]{1,0:T(8,128)(2,1)}, u32[]{:S(2)}, u32[]{:S(2)}) collective-permute-start(bf16[256,768]{1,0:T(8,128)(2,1)} %refs_9_.1), channel_id=1, source_target_pairs={{0,2},{1,3},{2,4},{3,5},{4,6},{5,7},{6,8},{7,9},{8,10},{9,11},{10,... | collective-permute-start | bytes 1179656 | tf_op jit(solution)/shard_map/ppermute | solution.py:16
  4.0 7.9 %collective-permute-start.9 = (bf16[256,768]{1,0:T(8,128)(2,1)}, bf16[256,768]{1,0:T(8,128)(2,1)}, u32[]{:S(2)}, u32[]{:S(2)}) collective-permute-start(bf16[256,768]{1,0:T(8,128)(2,1)} %refs_9_.1), channel_id=1, source_target_pairs={{2,0},{3,1},{4,2},{5,3},{6,4},{7,5},{8,6},{9,7},{10,8},{11,9},{12,... | collective-permute-start | bytes 1179656 | tf_op jit(solution)/shard_map/ppermute | solution.py:16
  11.9 1.9 %collective-permute-start = (bf16[256,768]{1,0:T(8,128)(2,1)}, bf16[256,768]{1,0:T(8,128)(2,1)}, u32[]{:S(2)}, u32[]{:S(2)}) collective-permute-start(bf16[256,768]{1,0:T(8,128)(2,1)} %refs_0_.1), channel_id=1, source_target_pairs={{0,2},{1,3},{2,4},{3,5},{4,6},{5,7},{6,8},{7,9},{8,10},{9,11},{10,... | collective-permute-start | bytes 1179656 | tf_op jit(solution)/shard_map/ppermute | solution.py:16
  13.8 8.1 %collective-permute-start.1 = (bf16[256,768]{1,0:T(8,128)(2,1)}, bf16[256,768]{1,0:T(8,128)(2,1)}, u32[]{:S(2)}, u32[]{:S(2)}) collective-permute-start(bf16[256,768]{1,0:T(8,128)(2,1)} %refs_0_.1), channel_id=1, source_target_pairs={{2,0},{3,1},{4,2},{5,3},{6,4},{7,5},{8,6},{9,7},{10,8},{11,9},{12,... | collective-permute-start | bytes 1179656 | tf_op jit(solution)/shard_map/ppermute | solution.py:16
  22.3 0.8 copy.16
  24.0 1.4 %convert_reduce_fusion.1 = s32[2304]{0:T(1024)S(1)} fusion(s32[128]{0:T(128)S(1)} %sub.49, s32[2304]{0:T(1024)S(1)} %add.220), kind=kLoop, calls=%fused_computation.107 | loop fusion | flops 882432 | bytes 18944 | tf_op jit(solution)/shard_map/reduce_sum | solution.py:33
  26.4 1.9 %collective-permute-start.10 = (bf16[256,768]{1,0:T(8,128)(2,1)}, bf16[256,768]{1,0:T(8,128)(2,1)S(1)}, u32[]{:S(2)}, u32[]{:S(2)}) collective-permute-start(bf16[256,768]{1,0:T(8,128)(2,1)} %collective-permute-done.8.refs_10_), channel_id=1, source_target_pairs={{0,2},{1,3},{2,4},{3,5},{4,6},{5,7},{6,8},{7,9},{8,10},{9,11},{10,... | collective-permute-start | bytes 1179656 | tf_op jit(solution)/shard_map/ppermute | solution.py:16
  28.3 8.1 %collective-permute-start.11 = (bf16[256,768]{1,0:T(8,128)(2,1)}, bf16[256,768]{1,0:T(8,128)(2,1)S(1)}, u32[]{:S(2)}, u32[]{:S(2)}) collective-permute-start(bf16[256,768]{1,0:T(8,128)(2,1)} %collective-permute-done.9.refs_11_), channel_id=1, source_target_pairs={{2,0},{3,1},{4,2},{5,3},{6,4},{7,5},{8,6},{9,7},{10,8},{11,9},{12,... | collective-permute-start | bytes 1179656 | tf_op jit(solution)/shard_map/ppermute | solution.py:16
  36.7 1.9 %collective-permute-start.2 = (bf16[256,768]{1,0:T(8,128)(2,1)}, bf16[256,768]{1,0:T(8,128)(2,1)S(1)}, u32[]{:S(2)}, u32[]{:S(2)}) collective-permute-start(bf16[256,768]{1,0:T(8,128)(2,1)} %collective-permute-done.refs_1_), channel_id=1, source_target_pairs={{0,2},{1,3},{2,4},{3,5},{4,6},{5,7},{6,8},{7,9},{8,10},{9,11},{10,... | collective-permute-start | bytes 1179656 | tf_op jit(solution)/shard_map/ppermute | solution.py:16
  38.6 8.1 %collective-permute-start.3 = (bf16[256,768]{1,0:T(8,128)(2,1)}, bf16[256,768]{1,0:T(8,128)(2,1)S(1)}, u32[]{:S(2)}, u32[]{:S(2)}) collective-permute-start(bf16[256,768]{1,0:T(8,128)(2,1)} %collective-permute-done.1.refs_2_), channel_id=1, source_target_pairs={{2,0},{3,1},{4,2},{5,3},{6,4},{7,5},{8,6},{9,7},{10,8},{11,9},{12,... | collective-permute-start | bytes 1179656 | tf_op jit(solution)/shard_map/ppermute | solution.py:16
  48.1 0.8 broadcast_select_fusion
  48.9 5.0 %collective-permute-done.2.refs_3_ = bf16[256,768]{1,0:T(8,128)(2,1)S(1)} collective-permute-done((bf16[256,768]{1,0:T(8,128)(2,1)}, bf16[256,768]{1,0:T(8,128)(2,1)S(1)}, u32[]{:S(2)}, u32[]{:S(2)}) %collective-permute-start.2) | collective-permute-done | bytes 393248 | tf_op jit(solution)/shard_map/ppermute | solution.py:16
  53.9 1.3 %collective-permute-done.3.refs_4_ = bf16[256,768]{1,0:T(8,128)(2,1)S(1)} collective-permute-done((bf16[256,768]{1,0:T(8,128)(2,1)}, bf16[256,768]{1,0:T(8,128)(2,1)S(1)}, u32[]{:S(2)}, u32[]{:S(2)}) %collective-permute-start.3) | collective-permute-done | bytes 393248 | tf_op jit(solution)/shard_map/ppermute | solution.py:16
  55.2 0.7 copy-done.4
  56.0 0.8 broadcast_select_fusion.1
  57.4 0.8 copy.17.recq_ref
  58.2 1.3 %pad.4.reck_ref = s32[16,256]{1,0:T(8,128)} pad(s32[9,256]{1,0:T(8,128)} %broadcast_select_fusion.6, s32[]{:T(128)} %constant.55.clone.1), padding=0_7x0_0 | pad | bytes 25604 | tf_op jit(solution)/shard_map/jit(_pad)/pad | solution.py:160
  59.5 2.4 %slice_reduce_fusion.30 = (f32[1536]{0:T(1024)S(1)}, f32[1536]{0:T(1024)}, f32[1536]{0:T(1024)}, f32[1536]{0:T(1024)}, f32[1536]{0:T(1024)}, /*index=5*/f32[1536...) fusion(f32[31,1536]{1,0:T(8,128)} %param.20), kind=kLoop, calls=%fused_computation.149 | loop fusion | bytes 233472 | tf_op jit(solution)/shard_map/slice | solution.py:198
  62.7 16.2 %shard_map.118 = bf16[256,768]{1,0:T(8,128)(2,1)} custom-call(s32[256,1]{1,0:T(8,128)} %copy.17.recq_ref, s32[16,256]{1,0:T(8,128)} %pad.4.reck_ref, bf16[256,768]{1,0:T(8,128)(2,1)} %q_ref.1, bf16[256,768]{1,0:T(8,128)(2,1)} %refs_0_.1, bf16[256,768]{1,0:T(8,128)(2,1)} %collective-permute-done.refs_1_, bf16[256,768]{1,0:T(8,128)(2,1)} %collective-permute-done.1.refs_2_, ...), custom_call_target="tpu_custom_call" | custom-call | tf_op jit(solution)/shard_map/pallas_call | solution.py:97
  79.0 2.0 %fusion.1 = bf16[256,1536]{1,0:T(8,128)(2,1)S(1)} fusion(bf16[256,768]{1,0:T(8,128)(2,1)} %shard_map.118, bf16[768,1536]{1,0:T(8,128)(2,1)S(1)} %copy-done, bf16[256,1536]{1,0:T(8,128)(2,1)} %param.12), kind=kOutput, calls=%fused_computation.3 | convolution fusion | flops 605159424 | bytes 4325376 | tf_op jit(solution)/shard_map/dot_general | solution.py:164
  82.1 8.5 %collective-permute-start.16 = (bf16[15,1536]{1,0:T(8,128)(2,1)S(1)}, bf16[15,1536]{1,0:T(8,128)(2,1)S(1)}, u32[]{:S(2)}, u32[]{:S(2)}) collective-permute-start(bf16[15,1536]{1,0:T(8,128)(2,1)S(1)} %get-tuple-element.36), channel_id=1, source_target_pairs={{1,2},{3,4},{5,6},{7,8},{9,10},{11,12},{13,14},{15,16},{17,18},{19... | collective-permute-start | bytes 138248 | tf_op jit(solution)/shard_map/ppermute | solution.py:179
  90.9 1.4 %slice_reduce_fusion.29 = (f32[1536]{0:T(1024)S(1)}, f32[1536]{0:T(1024)S(1)}, f32[1536]{0:T(1024)S(1)}, f32[1536]{0:T(1024)S(1)}, f32[1536]{0:T(1024)S(1)}, /*i...) fusion(f32[31,1536]{1,0:T(8,128)} %param.20), kind=kLoop, calls=%fused_computation.148 | loop fusion | bytes 147456 | tf_op jit(solution)/shard_map/slice | solution.py:198
  93.8 9.8 %multiply_convert_fusion = bf16[256,1536]{1,0:T(8,128)(2,1)S(1)} fusion(f32[286,1536]{1,0:T(8,128)S(1)} %convert_element_type.37, f32[1536]{0:T(1024)S(1)} %copy-done.25, f32[1536]{0:T(1024)S(1)} %copy-done.26, f32[1536]{0:T(1024)S(1)} %get-tuple-element.34, f32[1536]{0:T(1024)S(1)} %get-tuple-element.35, f32[1536]{0:T(1024)S(1)} %copy-done.5, ...), kind=kLoop, calls=%fused_computation.106 | loop fusion | flops 38928384 | bytes 49755904 | tf_op jit(solution)/shard_map/convert_element_type | solution.py:201
  103.6 4.6 %fusion = bf16[256,1536]{1,0:T(8,128)(2,1)} fusion(bf16[256,1536]{1,0:T(8,128)(2,1)S(1)} %multiply_convert_fusion, bf16[1536,1536]{1,0:T(8,128)(2,1)} %param.23, bf16[256,1536]{1,0:T(8,128)(2,1)S(1)} %fusion.1), kind=kOutput, calls=%fused_computation.2 | convolution fusion | flops 1209139200 | bytes 7077888 | tf_op jit(solution)/shard_map/dot_general | solution.py:202
  (146 shorter events, 7.3 us)
Async XLA Ops:
  0.0 78.9 %copy-start = (bf16[768,1536]{1,0:T(8,128)(2,1)S(1)}, bf16[768,1536]{1,0:T(8,128)(2,1)}, u32[]{:S(2)}) copy-start(bf16[768,1536]{1,0:T(8,128)(2,1)} %param.17) | copy-start | bytes 7077892
  0.0 26.4 %collective-permute-start.8 = (bf16[256,768]{1,0:T(8,128)(2,1)}, bf16[256,768]{1,0:T(8,128)(2,1)}, u32[]{:S(2)}, u32[]{:S(2)}) collective-permute-start(bf16[256,768]{1,0:T(8,128)(2,1)} %refs_9_.1), channel_id=1, source_target_pairs={{0,2},{1,3},{2,4},{3,5},{4,6},{5,7},{6,8},{7,9},{8,10},{9,11},{10,... | collective-permute-start | bytes 1179656 | tf_op jit(solution)/shard_map/ppermute | solution.py:16
  4.0 24.4 %collective-permute-start.9 = (bf16[256,768]{1,0:T(8,128)(2,1)}, bf16[256,768]{1,0:T(8,128)(2,1)}, u32[]{:S(2)}, u32[]{:S(2)}) collective-permute-start(bf16[256,768]{1,0:T(8,128)(2,1)} %refs_9_.1), channel_id=1, source_target_pairs={{2,0},{3,1},{4,2},{5,3},{6,4},{7,5},{8,6},{9,7},{10,8},{11,9},{12,... | collective-permute-start | bytes 1179656 | tf_op jit(solution)/shard_map/ppermute | solution.py:16
  11.9 24.8 %collective-permute-start = (bf16[256,768]{1,0:T(8,128)(2,1)}, bf16[256,768]{1,0:T(8,128)(2,1)}, u32[]{:S(2)}, u32[]{:S(2)}) collective-permute-start(bf16[256,768]{1,0:T(8,128)(2,1)} %refs_0_.1), channel_id=1, source_target_pairs={{0,2},{1,3},{2,4},{3,5},{4,6},{5,7},{6,8},{7,9},{8,10},{9,11},{10,... | collective-permute-start | bytes 1179656 | tf_op jit(solution)/shard_map/ppermute | solution.py:16
  13.8 24.8 %collective-permute-start.1 = (bf16[256,768]{1,0:T(8,128)(2,1)}, bf16[256,768]{1,0:T(8,128)(2,1)}, u32[]{:S(2)}, u32[]{:S(2)}) collective-permute-start(bf16[256,768]{1,0:T(8,128)(2,1)} %refs_0_.1), channel_id=1, source_target_pairs={{2,0},{3,1},{4,2},{5,3},{6,4},{7,5},{8,6},{9,7},{10,8},{11,9},{12,... | collective-permute-start | bytes 1179656 | tf_op jit(solution)/shard_map/ppermute | solution.py:16
  22.0 34.8 %collective-permute-start.12 = (bf16[256,768]{1,0:T(8,128)(2,1)}, bf16[256,768]{1,0:T(8,128)(2,1)}, u32[]{:S(2)}, u32[]{:S(2)}) collective-permute-start(bf16[256,768]{1,0:T(8,128)(2,1)} %refs_9_.1), channel_id=1, source_target_pairs={{0,1},{1,0},{2,3},{3,2},{4,5},{5,4},{6,7},{7,6},{8,9},{9,8},{10,11... | collective-permute-start | bytes 1179656 | tf_op jit(solution)/shard_map/ppermute | solution.py:148
  26.4 21.1 %collective-permute-start.10 = (bf16[256,768]{1,0:T(8,128)(2,1)}, bf16[256,768]{1,0:T(8,128)(2,1)S(1)}, u32[]{:S(2)}, u32[]{:S(2)}) collective-permute-start(bf16[256,768]{1,0:T(8,128)(2,1)} %collective-permute-done.8.refs_10_), channel_id=1, source_target_pairs={{0,2},{1,3},{2,4},{3,5},{4,6},{5,7},{6,8},{7,9},{8,10},{9,11},{10,... | collective-permute-start | bytes 1179656 | tf_op jit(solution)/shard_map/ppermute | solution.py:16
  28.3 19.3 %collective-permute-start.11 = (bf16[256,768]{1,0:T(8,128)(2,1)}, bf16[256,768]{1,0:T(8,128)(2,1)S(1)}, u32[]{:S(2)}, u32[]{:S(2)}) collective-permute-start(bf16[256,768]{1,0:T(8,128)(2,1)} %collective-permute-done.9.refs_11_), channel_id=1, source_target_pairs={{2,0},{3,1},{4,2},{5,3},{6,4},{7,5},{8,6},{9,7},{10,8},{11,9},{12,... | collective-permute-start | bytes 1179656 | tf_op jit(solution)/shard_map/ppermute | solution.py:16
  36.7 17.2 %collective-permute-start.2 = (bf16[256,768]{1,0:T(8,128)(2,1)}, bf16[256,768]{1,0:T(8,128)(2,1)S(1)}, u32[]{:S(2)}, u32[]{:S(2)}) collective-permute-start(bf16[256,768]{1,0:T(8,128)(2,1)} %collective-permute-done.refs_1_), channel_id=1, source_target_pairs={{0,2},{1,3},{2,4},{3,5},{4,6},{5,7},{6,8},{7,9},{8,10},{9,11},{10,... | collective-permute-start | bytes 1179656 | tf_op jit(solution)/shard_map/ppermute | solution.py:16
  38.6 16.6 %collective-permute-start.3 = (bf16[256,768]{1,0:T(8,128)(2,1)}, bf16[256,768]{1,0:T(8,128)(2,1)S(1)}, u32[]{:S(2)}, u32[]{:S(2)}) collective-permute-start(bf16[256,768]{1,0:T(8,128)(2,1)} %collective-permute-done.1.refs_2_), channel_id=1, source_target_pairs={{2,0},{3,1},{4,2},{5,3},{6,4},{7,5},{8,6},{9,7},{10,8},{11,9},{12,... | collective-permute-start | bytes 1179656 | tf_op jit(solution)/shard_map/ppermute | solution.py:16
  47.5 15.2 %copy-start.1 = (bf16[256,768]{1,0:T(8,128)(2,1)}, bf16[256,768]{1,0:T(8,128)(2,1)S(1)}, u32[]{:S(2)}) copy-start(bf16[256,768]{1,0:T(8,128)(2,1)S(1)} %collective-permute-done.10.refs_12_) | copy-start | bytes 1179652
  47.5 9.3 %collective-permute-start.4 = (bf16[256,768]{1,0:T(8,128)(2,1)}, bf16[256,768]{1,0:T(8,128)(2,1)}, u32[]{:S(2)}, u32[]{:S(2)}) collective-permute-start(bf16[256,768]{1,0:T(8,128)(2,1)} %refs_0_.1), channel_id=1, source_target_pairs={{0,1},{1,0},{2,3},{3,2},{4,5},{5,4},{6,7},{7,6},{8,9},{9,8},{10,11... | collective-permute-start | bytes 1179656 | tf_op jit(solution)/shard_map/ppermute | solution.py:148
  47.6 15.1 %copy-start.2 = (bf16[256,768]{1,0:T(8,128)(2,1)}, bf16[256,768]{1,0:T(8,128)(2,1)S(1)}, u32[]{:S(2)}) copy-start(bf16[256,768]{1,0:T(8,128)(2,1)S(1)} %collective-permute-done.11.refs_13_) | copy-start | bytes 1179652
  47.6 9.7 %collective-permute-start.13 = (bf16[256,768]{1,0:T(8,128)(2,1)}, bf16[256,768]{1,0:T(8,128)(2,1)}, u32[]{:S(2)}, u32[]{:S(2)}) collective-permute-start(bf16[256,768]{1,0:T(8,128)(2,1)} %collective-permute-done.8.refs_10_), channel_id=1, source_target_pairs={{0,1},{1,0},{2,3},{3,2},{4,5},{5,4},{6,7},{7,6},{8,9},{9,8},{10,11... | collective-permute-start | bytes 1179656 | tf_op jit(solution)/shard_map/ppermute | solution.py:148
  53.9 8.8 %copy-start.3 = (bf16[256,768]{1,0:T(8,128)(2,1)}, bf16[256,768]{1,0:T(8,128)(2,1)S(1)}, u32[]{:S(2)}) copy-start(bf16[256,768]{1,0:T(8,128)(2,1)S(1)} %collective-permute-done.2.refs_3_) | copy-start | bytes 1179652
  53.9 8.7 %collective-permute-start.14 = (bf16[256,768]{1,0:T(8,128)(2,1)}, bf16[256,768]{1,0:T(8,128)(2,1)}, u32[]{:S(2)}, u32[]{:S(2)}) collective-permute-start(bf16[256,768]{1,0:T(8,128)(2,1)} %collective-permute-done.9.refs_11_), channel_id=1, source_target_pairs={{0,1},{1,0},{2,3},{3,2},{4,5},{5,4},{6,7},{7,6},{8,9},{9,8},{10,11... | collective-permute-start | bytes 1179656 | tf_op jit(solution)/shard_map/ppermute | solution.py:148
  55.2 7.4 %collective-permute-start.5 = (bf16[256,768]{1,0:T(8,128)(2,1)}, bf16[256,768]{1,0:T(8,128)(2,1)}, u32[]{:S(2)}, u32[]{:S(2)}) collective-permute-start(bf16[256,768]{1,0:T(8,128)(2,1)} %collective-permute-done.refs_1_), channel_id=1, source_target_pairs={{0,1},{1,0},{2,3},{3,2},{4,5},{5,4},{6,7},{7,6},{8,9},{9,8},{10,11... | collective-permute-start | bytes 1179656 | tf_op jit(solution)/shard_map/ppermute | solution.py:148
  56.8 5.9 %collective-permute-start.6 = (bf16[256,768]{1,0:T(8,128)(2,1)}, bf16[256,768]{1,0:T(8,128)(2,1)}, u32[]{:S(2)}, u32[]{:S(2)}) collective-permute-start(bf16[256,768]{1,0:T(8,128)(2,1)} %collective-permute-done.1.refs_2_), channel_id=1, source_target_pairs={{0,1},{1,0},{2,3},{3,2},{4,5},{5,4},{6,7},{7,6},{8,9},{9,8},{10,11... | collective-permute-start | bytes 1179656 | tf_op jit(solution)/shard_map/ppermute | solution.py:148
  56.8 5.9 %collective-permute-start.15 = (bf16[256,768]{1,0:T(8,128)(2,1)}, bf16[256,768]{1,0:T(8,128)(2,1)}, u32[]{:S(2)}, u32[]{:S(2)}) collective-permute-start(bf16[256,768]{1,0:T(8,128)(2,1)} %broadcast_select_fusion), channel_id=1, source_target_pairs={{0,1},{1,0},{2,3},{3,2},{4,5},{5,4},{6,7},{7,6},{8,9},{9,8},{10,11... | collective-permute-start | bytes 1179656 | tf_op jit(solution)/shard_map/ppermute | solution.py:148
  57.3 5.4 %collective-permute-start.7 = (bf16[256,768]{1,0:T(8,128)(2,1)}, bf16[256,768]{1,0:T(8,128)(2,1)}, u32[]{:S(2)}, u32[]{:S(2)}) collective-permute-start(bf16[256,768]{1,0:T(8,128)(2,1)} %broadcast_select_fusion.1), channel_id=1, source_target_pairs={{0,1},{1,0},{2,3},{3,2},{4,5},{5,4},{6,7},{7,6},{8,9},{9,8},{10,11... | collective-permute-start | bytes 1179656 | tf_op jit(solution)/shard_map/ppermute | solution.py:148
  82.1 10.3 %collective-permute-start.16 = (bf16[15,1536]{1,0:T(8,128)(2,1)S(1)}, bf16[15,1536]{1,0:T(8,128)(2,1)S(1)}, u32[]{:S(2)}, u32[]{:S(2)}) collective-permute-start(bf16[15,1536]{1,0:T(8,128)(2,1)S(1)} %get-tuple-element.36), channel_id=1, source_target_pairs={{1,2},{3,4},{5,6},{7,8},{9,10},{11,12},{13,14},{15,16},{17,18},{19... | collective-permute-start | bytes 138248 | tf_op jit(solution)/shard_map/ppermute | solution.py:179
  90.6 1.8 %collective-permute-start.17 = (bf16[15,1536]{1,0:T(8,128)(2,1)S(1)}, bf16[15,1536]{1,0:T(8,128)(2,1)S(1)}, u32[]{:S(2)}, u32[]{:S(2)}) collective-permute-start(bf16[15,1536]{1,0:T(8,128)(2,1)S(1)} %get-tuple-element.37), channel_id=1, source_target_pairs={{0,1},{1,0},{2,3},{3,2},{4,5},{5,4},{6,7},{7,6},{8,9},{9,8},{10,11... | collective-permute-start | bytes 138248 | tf_op jit(solution)/shard_map/ppermute | solution.py:182
  92.8 0.8 copy-start.25
  92.8 0.8 copy-start.26
  (41 other events, 31.3 us)

commit v7 on v6

--- a/solution.py
+++ b/solution.py
@@ -172,33 +172,45 @@
         jnp.bfloat16
     )
     rim_width = (depthwise_taps.shape[0] - 1) // 2
-    head_rows = normed[:rim_width]
-    tail_rows = normed[frames - rim_width :]
+    ntaps = depthwise_taps.shape[0]
+
+    def conv_rows(source32, source_rec, out_rec):
+        n = out_rec.shape[0]
+        summed = jnp.zeros((n, normed.shape[1]), jnp.float32)
+        for tap in range(ntaps):
+            same_rec = (source_rec[tap : tap + n] == out_rec)[:, None]
+            summed = summed + jnp.where(
+                same_rec, source32[tap : tap + n] * depthwise_taps[tap], 0.0
+            )
+        shifted = summed * conv_gain + conv_bias
+        return (shifted * jax.nn.sigmoid(shifted)).astype(jnp.bfloat16)
+
+    normed32 = normed.astype(jnp.float32)
+    act_mid = conv_rows(normed32, own_rec, own_rec[rim_width : frames - rim_width])
+    act_mid, head_rows, tail_rows = lax.optimization_barrier(
+        (act_mid, normed[: 2 * rim_width], normed[frames - 2 * rim_width :])
+    )
     cross = [(i, i + 1) for i in range(1, nblocks - 1, 2)]
     cross = cross + [(j, i) for i, j in cross]
     over_link = lax.ppermute(
-        lax.select(parity == 0, head_rows, tail_rows), ("grp", "blk"), cross
+        lax.select(parity == 0, head_rows[:rim_width], tail_rows[rim_width:]), ("grp", "blk"), cross
     )
     on_chip = lax.ppermute(
-        lax.select(parity == 0, tail_rows, head_rows), ("grp", "blk"), swap
+        lax.select(parity == 0, tail_rows[rim_width:], head_rows[:rim_width]), ("grp", "blk"), swap
     )
     low = lax.select(parity == 0, over_link, on_chip)
     high = lax.select(parity == 0, on_chip, over_link)
-    extended = jnp.concatenate([low, normed, high], axis=0)
     ext_positions = (
         block_here * frames - rim_width + jnp.arange(frames + 2 * rim_width, dtype=jnp.int32)
     )
     ext_inside = (ext_positions >= 0) & (ext_positions < nblocks * frames)
     ext_rec = jnp.where(ext_inside, segment_of(ext_positions, starts), -1)
-    extended32 = lax.optimization_barrier(extended).astype(jnp.float32)
-    summed = jnp.zeros((frames, normed.shape[1]), jnp.float32)
-    for tap in range(depthwise_taps.shape[0]):
-        same_rec = (ext_rec[tap : tap + frames] == own_rec)[:, None]
-        summed = summed + jnp.where(
-            same_rec, extended32[tap : tap + frames] * depthwise_taps[tap], 0.0
-        )
-    shifted = summed * conv_gain + conv_bias
-    act = lax.optimization_barrier((shifted * jax.nn.sigmoid(shifted)).astype(jnp.bfloat16))
+    edge = 3 * rim_width
+    lo_src = jnp.concatenate([low, head_rows], axis=0).astype(jnp.float32)
+    hi_src = jnp.concatenate([tail_rows, high], axis=0).astype(jnp.float32)
+    act_lo = conv_rows(lo_src, ext_rec[:edge], own_rec[:rim_width])
+    act_hi = conv_rows(hi_src, ext_rec[-edge:], own_rec[frames - rim_width :])
+    act = jnp.concatenate([act_lo, act_mid, act_hi], axis=0)
     return (resid32 + jnp.dot(act, pointwise_weight, preferred_element_type=jnp.float32)).astype(
         jnp.bfloat16
     )

time: 110 us -> 116 us (1.055)
  other arithmetic: 17.7 us -> 24.8 us
  matrix products: 6.64 us -> 4.04 us
  waiting for transfers between devices: 6.44 us -> 8.08 us
    eq x2 -> x11, other arithmetic: 1.43 us -> 6.91 us  [conv_rows(): same_rec = (source_rec[tap:tap + n] == out_rec)[:, None]]
    dot_general x1, matrix products: 4.6 us -> 2.27 us  [shards(): jnp.dot(act, pointwise_weight, preferred_element_type=jnp.float32)]
    convert_element_type x3 -> x5, other arithmetic: 10.4 us -> 12.1 us  [the longest x3 11.7 us: conv_rows(): return (shifted * jax.nn.sigmoid(shifted)).astype(jnp.bfloat16)]
    ppermute x2, waiting for transfers between devices: 0.08 us -> 1.58 us  [the longest x1 1.58 us: shards(): lax.ppermute(lax.select(parity == 0, head_rows[:rim_width], tail_rows[rim...]
    slice x2 -> x3, local copies, waits for them, and re-layouts: 3.8 us -> 4.47 us  [the longest x2 4.45 us: conv_rows(): depthwise_taps[tap]]
  transfers between devices with their start and end apart: 18 -> 18, of which waited for: 3 -> 3; matrix products, arithmetic and copies ran while one was open for 12% -> 17% of each run, Pallas kernels for 0% -> 0%
where the time goes in v7:
time: 116 us; the launch traced here: 115 us
  starting transfers between devices  51.9 us (45%)
  other arithmetic  24.8 us (21%)
  Pallas kernels  16.2 us (14%)
  local copies, waits for them, and re-layouts  8.69 us (7%)
  waiting for transfers between devices  8.08 us (7%)
  matrix products  4.04 us (3%)
  between operations  1.43 us (1%)
    ppermute x8, starting transfers between devices, shifted_2(): return lax.ppermute(block, axis, route)  42.1 us
    pallas_call x1, Pallas kernels, attend(): pl.pallas_call(attend_kernel, grid=(width // pair,), in_specs=[pl.BlockSp...  16.2 us
    convert_element_type x3, other arithmetic, conv_rows(): return (shifted * jax.nn.sigmoid(shifted)).astype(jnp.bfloat16)  11.7 us
    ppermute x1, starting transfers between devices, shards(): lax.ppermute(lax.select(parity == 0, head_rows[:rim_width], tail_rows[rim...  8.35 us
    eq x11, other arithmetic, conv_rows(): same_rec = (source_rec[tap:tap + n] == out_rec)[:, None]  6.91 us
    ppermute x8, waiting for transfers between devices, shifted_2(): return lax.ppermute(block, axis, route)  6.48 us
    slice x2, local copies, waits for them, and re-layouts, conv_rows(): depthwise_taps[tap]  4.45 us
  transfers between devices with their start and end apart: 18, of which 3 were waited for; matrix products, arithmetic and copies ran while one was open for 17% of the time, Pallas kernels for 0%

profile of v7, /device:TPU:16, one launch (start us, length us, event | category | flops | bytes accessed | tf_op | source)
XLA Modules:
  0.0 115.2 jit_solution(7740564664535915083)
XLA Ops:
  0.0 3.9 %collective-permute-start.8 = (bf16[256,768]{1,0:T(8,128)(2,1)}, bf16[256,768]{1,0:T(8,128)(2,1)}, u32[]{:S(2)}, u32[]{:S(2)}) collective-permute-start(bf16[256,768]{1,0:T(8,128)(2,1)} %refs_9_.1), channel_id=1, source_target_pairs={{0,2},{1,3},{2,4},{3,5},{4,6},{5,7},{6,8},{7,9},{8,10},{9,11},{10,... | collective-permute-start | bytes 1179656 | tf_op jit(solution)/shard_map/ppermute | solution.py:16
  4.0 7.9 %collective-permute-start.9 = (bf16[256,768]{1,0:T(8,128)(2,1)}, bf16[256,768]{1,0:T(8,128)(2,1)}, u32[]{:S(2)}, u32[]{:S(2)}) collective-permute-start(bf16[256,768]{1,0:T(8,128)(2,1)} %refs_9_.1), channel_id=1, source_target_pairs={{2,0},{3,1},{4,2},{5,3},{6,4},{7,5},{8,6},{9,7},{10,8},{11,9},{12,... | collective-permute-start | bytes 1179656 | tf_op jit(solution)/shard_map/ppermute | solution.py:16
  11.9 1.9 %collective-permute-start = (bf16[256,768]{1,0:T(8,128)(2,1)}, bf16[256,768]{1,0:T(8,128)(2,1)}, u32[]{:S(2)}, u32[]{:S(2)}) collective-permute-start(bf16[256,768]{1,0:T(8,128)(2,1)} %refs_0_.1), channel_id=1, source_target_pairs={{0,2},{1,3},{2,4},{3,5},{4,6},{5,7},{6,8},{7,9},{8,10},{9,11},{10,... | collective-permute-start | bytes 1179656 | tf_op jit(solution)/shard_map/ppermute | solution.py:16
  13.8 8.1 %collective-permute-start.1 = (bf16[256,768]{1,0:T(8,128)(2,1)}, bf16[256,768]{1,0:T(8,128)(2,1)}, u32[]{:S(2)}, u32[]{:S(2)}) collective-permute-start(bf16[256,768]{1,0:T(8,128)(2,1)} %refs_0_.1), channel_id=1, source_target_pairs={{2,0},{3,1},{4,2},{5,3},{6,4},{7,5},{8,6},{9,7},{10,8},{11,9},{12,... | collective-permute-start | bytes 1179656 | tf_op jit(solution)/shard_map/ppermute | solution.py:16
  27.9 1.4 %convert_reduce_fusion.1 = s32[2304]{0:T(1024)S(1)} fusion(s32[128]{0:T(128)S(1)} %sub.49, s32[2304]{0:T(1024)S(1)} %add.420), kind=kLoop, calls=%fused_computation.106 | loop fusion | flops 882432 | bytes 18944 | tf_op jit(solution)/shard_map/reduce_sum | solution.py:33
  31.4 1.9 %collective-permute-start.10 = (bf16[256,768]{1,0:T(8,128)(2,1)}, bf16[256,768]{1,0:T(8,128)(2,1)S(1)}, u32[]{:S(2)}, u32[]{:S(2)}) collective-permute-start(bf16[256,768]{1,0:T(8,128)(2,1)} %collective-permute-done.8.refs_10_), channel_id=1, source_target_pairs={{0,2},{1,3},{2,4},{3,5},{4,6},{5,7},{6,8},{7,9},{8,10},{9,11},{10,... | collective-permute-start | bytes 1179656 | tf_op jit(solution)/shard_map/ppermute | solution.py:16
  33.3 8.1 %collective-permute-start.11 = (bf16[256,768]{1,0:T(8,128)(2,1)}, bf16[256,768]{1,0:T(8,128)(2,1)S(1)}, u32[]{:S(2)}, u32[]{:S(2)}) collective-permute-start(bf16[256,768]{1,0:T(8,128)(2,1)} %collective-permute-done.9.refs_11_), channel_id=1, source_target_pairs={{2,0},{3,1},{4,2},{5,3},{6,4},{7,5},{8,6},{9,7},{10,8},{11,9},{12,... | collective-permute-start | bytes 1179656 | tf_op jit(solution)/shard_map/ppermute | solution.py:16
  42.2 1.9 %collective-permute-start.2 = (bf16[256,768]{1,0:T(8,128)(2,1)}, bf16[256,768]{1,0:T(8,128)(2,1)S(1)}, u32[]{:S(2)}, u32[]{:S(2)}) collective-permute-start(bf16[256,768]{1,0:T(8,128)(2,1)} %collective-permute-done.refs_1_), channel_id=1, source_target_pairs={{0,2},{1,3},{2,4},{3,5},{4,6},{5,7},{6,8},{7,9},{8,10},{9,11},{10,... | collective-permute-start | bytes 1179656 | tf_op jit(solution)/shard_map/ppermute | solution.py:16
  44.1 8.1 %collective-permute-start.3 = (bf16[256,768]{1,0:T(8,128)(2,1)}, bf16[256,768]{1,0:T(8,128)(2,1)S(1)}, u32[]{:S(2)}, u32[]{:S(2)}) collective-permute-start(bf16[256,768]{1,0:T(8,128)(2,1)} %collective-permute-done.1.refs_2_), channel_id=1, source_target_pairs={{2,0},{3,1},{4,2},{5,3},{6,4},{7,5},{8,6},{9,7},{10,8},{11,9},{12,... | collective-permute-start | bytes 1179656 | tf_op jit(solution)/shard_map/ppermute | solution.py:16
  53.4 0.8 broadcast_select_fusion
  54.2 5.2 %collective-permute-done.2.refs_3_ = bf16[256,768]{1,0:T(8,128)(2,1)S(1)} collective-permute-done((bf16[256,768]{1,0:T(8,128)(2,1)}, bf16[256,768]{1,0:T(8,128)(2,1)S(1)}, u32[]{:S(2)}, u32[]{:S(2)}) %collective-permute-start.2) | collective-permute-done | bytes 393248 | tf_op jit(solution)/shard_map/ppermute | solution.py:16
  59.4 1.3 %collective-permute-done.3.refs_4_ = bf16[256,768]{1,0:T(8,128)(2,1)S(1)} collective-permute-done((bf16[256,768]{1,0:T(8,128)(2,1)}, bf16[256,768]{1,0:T(8,128)(2,1)S(1)}, u32[]{:S(2)}, u32[]{:S(2)}) %collective-permute-start.3) | collective-permute-done | bytes 393248 | tf_op jit(solution)/shard_map/ppermute | solution.py:16
  61.4 0.8 broadcast_select_fusion.1
  63.0 2.0 %slice_reduce_fusion.29 = (f32[1536]{0:T(1024)}, f32[1536]{0:T(1024)}, f32[1536]{0:T(1024)}, f32[1536]{0:T(1024)}, f32[1536]{0:T(1024)}, /*index=5*/f32[1536]{0:...) fusion(f32[31,1536]{1,0:T(8,128)} %param.20), kind=kLoop, calls=%fused_computation.343 | loop fusion | bytes 147456 | tf_op jit(solution)/shard_map/slice | solution.py:183
  65.1 0.8 copy.17.recq_ref
  65.9 1.3 %pad.4.reck_ref = s32[16,256]{1,0:T(8,128)} pad(s32[9,256]{1,0:T(8,128)} %broadcast_select_fusion.6, s32[]{:T(128)} %constant.57.clone.1), padding=0_7x0_0 | pad | bytes 25604 | tf_op jit(solution)/shard_map/jit(_pad)/pad | solution.py:160
  67.2 2.4 %slice_reduce_fusion.30 = (f32[1536]{0:T(1024)S(1)}, f32[1536]{0:T(1024)}, f32[1536]{0:T(1024)}, f32[1536]{0:T(1024)}, f32[1536]{0:T(1024)}, /*index=5*/f32[1536...) fusion(f32[31,1536]{1,0:T(8,128)} %param.20), kind=kLoop, calls=%fused_computation.344 | loop fusion | bytes 233472 | tf_op jit(solution)/shard_map/slice | solution.py:183
  70.4 16.2 %shard_map.118 = bf16[256,768]{1,0:T(8,128)(2,1)} custom-call(s32[256,1]{1,0:T(8,128)} %copy.17.recq_ref, s32[16,256]{1,0:T(8,128)} %pad.4.reck_ref, bf16[256,768]{1,0:T(8,128)(2,1)} %q_ref.1, bf16[256,768]{1,0:T(8,128)(2,1)} %refs_0_.1, bf16[256,768]{1,0:T(8,128)(2,1)} %collective-permute-done.refs_1_, bf16[256,768]{1,0:T(8,128)(2,1)} %collective-permute-done.1.refs_2_, ...), custom_call_target="tpu_custom_call" | custom-call | tf_op jit(solution)/shard_map/pallas_call | solution.py:97
  86.6 1.8 %fusion.1 = bf16[256,1536]{1,0:T(8,128)(2,1)S(1)} fusion(bf16[256,768]{1,0:T(8,128)(2,1)} %shard_map.118, bf16[768,1536]{1,0:T(8,128)(2,1)S(1)} %copy-done, bf16[256,1536]{1,0:T(8,128)(2,1)S(1)} %copy-done.77), kind=kOutput, calls=%fused_computation.3 | convolution fusion | flops 605159424 | bytes 4325376 | tf_op jit(solution)/shard_map/dot_general | solution.py:164
  90.3 9.6 %multiply_convert_fusion = bf16[226,1536]{1,0:T(8,128)(2,1)S(1)} fusion(f32[256,1536]{1,0:T(8,128)S(1)} %get-tuple-element.42, f32[1536]{0:T(1024)S(1)} %copy-done.35, f32[1536]{0:T(1024)S(1)} %copy-done.36, f32[1536]{0:T(1024)S(1)} %copy-done.33, f32[1536]{0:T(1024)S(1)} %copy-done.34, f32[1536]{0:T(1024)S(1)} %copy-done.5, f32[1536]{0:T(1024)S(1)} %copy-done.6, ...), kind=kLoop, calls=%fused_computation.105 | loop fusion | flops 34019328 | bytes 43948668 | tf_op jit(solution)/shard_map/convert_element_type | solution.py:186
  99.9 8.3 %collective-permute-start.16 = (bf16[15,1536]{1,0:T(8,128)(2,1)S(1)}, bf16[15,1536]{1,0:T(8,128)(2,1)S(1)}, u32[]{:S(2)}, u32[]{:S(2)}) collective-permute-start(bf16[15,1536]{1,0:T(8,128)(2,1)S(1)} %get-tuple-element.46), channel_id=1, source_target_pairs={{1,2},{3,4},{5,6},{7,8},{9,10},{11,12},{13,14},{15,16},{17,18},{19... | collective-permute-start | bytes 138248 | tf_op jit(solution)/shard_map/ppermute | solution.py:195
  108.4 1.6 %collective-permute-done.16 = bf16[15,1536]{1,0:T(8,128)(2,1)S(1)} collective-permute-done((bf16[15,1536]{1,0:T(8,128)(2,1)S(1)}, bf16[15,1536]{1,0:T(8,128)(2,1)S(1)}, u32[]{:S(2)}, u32[]{:S(2)}) %collective-permute-start.16) | collective-permute-done | bytes 46112 | tf_op jit(solution)/shard_map/ppermute | solution.py:195
  110.4 1.6 %multiply_convert_fusion.2 = bf16[15,1536]{1,0:T(8,128)(2,1)S(1)} fusion(f32[45,1536]{1,0:T(8,128)S(1)} %get-tuple-element.142, f32[1536]{0:T(1024)S(1)} %copy-done.35, f32[1536]{0:T(1024)S(1)} %copy-done.36, f32[1536]{0:T(1024)S(1)} %copy-done.33, f32[1536]{0:T(1024)S(1)} %copy-done.34, f32[1536]{0:T(1024)S(1)} %copy-done.5, f32[1536]{0:T(1024)S(1)} %copy-done.6, ...), kind=kLoop, calls=%fused_computation.307 | loop fusion | flops 2280960 | bytes 3106257 | tf_op jit(solution)/shard_map/convert_element_type | solution.py:186
  112.9 2.3 %fusion = bf16[256,1536]{1,0:T(8,128)(2,1)} fusion(bf16[1536,1536]{1,0:T(8,128)(2,1)S(1)} %copy-done.76, bf16[256,1536]{1,0:T(8,128)(2,1)S(1)} %fusion.1, bf16[15,1536]{1,0:T(8,128)(2,1)S(1)} %multiply_convert_fusion.1, bf16[226,1536]{1,0:T(8,128)(2,1)S(1)} %multiply_convert_fusion, bf16[15,1536]{1,0:T(8,128)(2,1)S(1)} %multiply_convert_fusion.2), kind=kOutput, calls=%fused_computation.2 | convolution fusion | flops 1211498496 | bytes 7077888 | tf_op jit(solution)/shard_map/dot_general | solution.py:214
  (219 shorter events, 14.3 us)
Async XLA Ops:
  0.0 86.6 %copy-start = (bf16[768,1536]{1,0:T(8,128)(2,1)S(1)}, bf16[768,1536]{1,0:T(8,128)(2,1)}, u32[]{:S(2)}) copy-start(bf16[768,1536]{1,0:T(8,128)(2,1)} %param.17) | copy-start | bytes 7077892
  0.0 31.4 %collective-permute-start.8 = (bf16[256,768]{1,0:T(8,128)(2,1)}, bf16[256,768]{1,0:T(8,128)(2,1)}, u32[]{:S(2)}, u32[]{:S(2)}) collective-permute-start(bf16[256,768]{1,0:T(8,128)(2,1)} %refs_9_.1), channel_id=1, source_target_pairs={{0,2},{1,3},{2,4},{3,5},{4,6},{5,7},{6,8},{7,9},{8,10},{9,11},{10,... | collective-permute-start | bytes 1179656 | tf_op jit(solution)/shard_map/ppermute | solution.py:16
  4.0 29.4 %collective-permute-start.9 = (bf16[256,768]{1,0:T(8,128)(2,1)}, bf16[256,768]{1,0:T(8,128)(2,1)}, u32[]{:S(2)}, u32[]{:S(2)}) collective-permute-start(bf16[256,768]{1,0:T(8,128)(2,1)} %refs_9_.1), channel_id=1, source_target_pairs={{2,0},{3,1},{4,2},{5,3},{6,4},{7,5},{8,6},{9,7},{10,8},{11,9},{12,... | collective-permute-start | bytes 1179656 | tf_op jit(solution)/shard_map/ppermute | solution.py:16
  11.9 30.2 %collective-permute-start = (bf16[256,768]{1,0:T(8,128)(2,1)}, bf16[256,768]{1,0:T(8,128)(2,1)}, u32[]{:S(2)}, u32[]{:S(2)}) collective-permute-start(bf16[256,768]{1,0:T(8,128)(2,1)} %refs_0_.1), channel_id=1, source_target_pairs={{0,2},{1,3},{2,4},{3,5},{4,6},{5,7},{6,8},{7,9},{8,10},{9,11},{10,... | collective-permute-start | bytes 1179656 | tf_op jit(solution)/shard_map/ppermute | solution.py:16
  13.8 30.2 %collective-permute-start.1 = (bf16[256,768]{1,0:T(8,128)(2,1)}, bf16[256,768]{1,0:T(8,128)(2,1)}, u32[]{:S(2)}, u32[]{:S(2)}) collective-permute-start(bf16[256,768]{1,0:T(8,128)(2,1)} %refs_0_.1), channel_id=1, source_target_pairs={{2,0},{3,1},{4,2},{5,3},{6,4},{7,5},{8,6},{9,7},{10,8},{11,9},{12,... | collective-permute-start | bytes 1179656 | tf_op jit(solution)/shard_map/ppermute | solution.py:16
  22.0 40.2 %collective-permute-start.12 = (bf16[256,768]{1,0:T(8,128)(2,1)}, bf16[256,768]{1,0:T(8,128)(2,1)}, u32[]{:S(2)}, u32[]{:S(2)}) collective-permute-start(bf16[256,768]{1,0:T(8,128)(2,1)} %refs_9_.1), channel_id=1, source_target_pairs={{0,1},{1,0},{2,3},{3,2},{4,5},{5,4},{6,7},{7,6},{8,9},{9,8},{10,11... | collective-permute-start | bytes 1179656 | tf_op jit(solution)/shard_map/ppermute | solution.py:148
  31.4 21.5 %collective-permute-start.10 = (bf16[256,768]{1,0:T(8,128)(2,1)}, bf16[256,768]{1,0:T(8,128)(2,1)S(1)}, u32[]{:S(2)}, u32[]{:S(2)}) collective-permute-start(bf16[256,768]{1,0:T(8,128)(2,1)} %collective-permute-done.8.refs_10_), channel_id=1, source_target_pairs={{0,2},{1,3},{2,4},{3,5},{4,6},{5,7},{6,8},{7,9},{8,10},{9,11},{10,... | collective-permute-start | bytes 1179656 | tf_op jit(solution)/shard_map/ppermute | solution.py:16
  33.3 19.6 %collective-permute-start.11 = (bf16[256,768]{1,0:T(8,128)(2,1)}, bf16[256,768]{1,0:T(8,128)(2,1)S(1)}, u32[]{:S(2)}, u32[]{:S(2)}) collective-permute-start(bf16[256,768]{1,0:T(8,128)(2,1)} %collective-permute-done.9.refs_11_), channel_id=1, source_target_pairs={{2,0},{3,1},{4,2},{5,3},{6,4},{7,5},{8,6},{9,7},{10,8},{11,9},{12,... | collective-permute-start | bytes 1179656 | tf_op jit(solution)/shard_map/ppermute | solution.py:16
  42.2 17.2 %collective-permute-start.2 = (bf16[256,768]{1,0:T(8,128)(2,1)}, bf16[256,768]{1,0:T(8,128)(2,1)S(1)}, u32[]{:S(2)}, u32[]{:S(2)}) collective-permute-start(bf16[256,768]{1,0:T(8,128)(2,1)} %collective-permute-done.refs_1_), channel_id=1, source_target_pairs={{0,2},{1,3},{2,4},{3,5},{4,6},{5,7},{6,8},{7,9},{8,10},{9,11},{10,... | collective-permute-start | bytes 1179656 | tf_op jit(solution)/shard_map/ppermute | solution.py:16
  44.1 16.6 %collective-permute-start.3 = (bf16[256,768]{1,0:T(8,128)(2,1)}, bf16[256,768]{1,0:T(8,128)(2,1)S(1)}, u32[]{:S(2)}, u32[]{:S(2)}) collective-permute-start(bf16[256,768]{1,0:T(8,128)(2,1)} %collective-permute-done.1.refs_2_), channel_id=1, source_target_pairs={{2,0},{3,1},{4,2},{5,3},{6,4},{7,5},{8,6},{9,7},{10,8},{11,9},{12,... | collective-permute-start | bytes 1179656 | tf_op jit(solution)/shard_map/ppermute | solution.py:16
  52.9 16.7 %copy-start.1 = (bf16[256,768]{1,0:T(8,128)(2,1)}, bf16[256,768]{1,0:T(8,128)(2,1)S(1)}, u32[]{:S(2)}) copy-start(bf16[256,768]{1,0:T(8,128)(2,1)S(1)} %collective-permute-done.10.refs_12_) | copy-start | bytes 1179652
  52.9 9.3 %collective-permute-start.4 = (bf16[256,768]{1,0:T(8,128)(2,1)}, bf16[256,768]{1,0:T(8,128)(2,1)}, u32[]{:S(2)}, u32[]{:S(2)}) collective-permute-start(bf16[256,768]{1,0:T(8,128)(2,1)} %refs_0_.1), channel_id=1, source_target_pairs={{0,1},{1,0},{2,3},{3,2},{4,5},{5,4},{6,7},{7,6},{8,9},{9,8},{10,11... | collective-permute-start | bytes 1179656 | tf_op jit(solution)/shard_map/ppermute | solution.py:148
  52.9 16.7 %copy-start.2 = (bf16[256,768]{1,0:T(8,128)(2,1)}, bf16[256,768]{1,0:T(8,128)(2,1)S(1)}, u32[]{:S(2)}) copy-start(bf16[256,768]{1,0:T(8,128)(2,1)S(1)} %collective-permute-done.11.refs_13_) | copy-start | bytes 1179652
  52.9 9.8 %collective-permute-start.13 = (bf16[256,768]{1,0:T(8,128)(2,1)}, bf16[256,768]{1,0:T(8,128)(2,1)}, u32[]{:S(2)}, u32[]{:S(2)}) collective-permute-start(bf16[256,768]{1,0:T(8,128)(2,1)} %collective-permute-done.8.refs_10_), channel_id=1, source_target_pairs={{0,1},{1,0},{2,3},{3,2},{4,5},{5,4},{6,7},{7,6},{8,9},{9,8},{10,11... | collective-permute-start | bytes 1179656 | tf_op jit(solution)/shard_map/ppermute | solution.py:148
  59.4 11.0 %copy-start.3 = (bf16[256,768]{1,0:T(8,128)(2,1)}, bf16[256,768]{1,0:T(8,128)(2,1)S(1)}, u32[]{:S(2)}) copy-start(bf16[256,768]{1,0:T(8,128)(2,1)S(1)} %collective-permute-done.2.refs_3_) | copy-start | bytes 1179652
  59.4 10.9 %collective-permute-start.14 = (bf16[256,768]{1,0:T(8,128)(2,1)}, bf16[256,768]{1,0:T(8,128)(2,1)}, u32[]{:S(2)}, u32[]{:S(2)}) collective-permute-start(bf16[256,768]{1,0:T(8,128)(2,1)} %collective-permute-done.9.refs_11_), channel_id=1, source_target_pairs={{0,1},{1,0},{2,3},{3,2},{4,5},{5,4},{6,7},{7,6},{8,9},{9,8},{10,11... | collective-permute-start | bytes 1179656 | tf_op jit(solution)/shard_map/ppermute | solution.py:148
  60.7 9.6 %collective-permute-start.5 = (bf16[256,768]{1,0:T(8,128)(2,1)}, bf16[256,768]{1,0:T(8,128)(2,1)}, u32[]{:S(2)}, u32[]{:S(2)}) collective-permute-start(bf16[256,768]{1,0:T(8,128)(2,1)} %collective-permute-done.refs_1_), channel_id=1, source_target_pairs={{0,1},{1,0},{2,3},{3,2},{4,5},{5,4},{6,7},{7,6},{8,9},{9,8},{10,11... | collective-permute-start | bytes 1179656 | tf_op jit(solution)/shard_map/ppermute | solution.py:148
  62.2 8.1 %collective-permute-start.6 = (bf16[256,768]{1,0:T(8,128)(2,1)}, bf16[256,768]{1,0:T(8,128)(2,1)}, u32[]{:S(2)}, u32[]{:S(2)}) collective-permute-start(bf16[256,768]{1,0:T(8,128)(2,1)} %collective-permute-done.1.refs_2_), channel_id=1, source_target_pairs={{0,1},{1,0},{2,3},{3,2},{4,5},{5,4},{6,7},{7,6},{8,9},{9,8},{10,11... | collective-permute-start | bytes 1179656 | tf_op jit(solution)/shard_map/ppermute | solution.py:148
  62.3 8.1 %collective-permute-start.15 = (bf16[256,768]{1,0:T(8,128)(2,1)}, bf16[256,768]{1,0:T(8,128)(2,1)}, u32[]{:S(2)}, u32[]{:S(2)}) collective-permute-start(bf16[256,768]{1,0:T(8,128)(2,1)} %broadcast_select_fusion), channel_id=1, source_target_pairs={{0,1},{1,0},{2,3},{3,2},{4,5},{5,4},{6,7},{7,6},{8,9},{9,8},{10,11... | collective-permute-start | bytes 1179656 | tf_op jit(solution)/shard_map/ppermute | solution.py:148
  62.8 7.6 %collective-permute-start.7 = (bf16[256,768]{1,0:T(8,128)(2,1)}, bf16[256,768]{1,0:T(8,128)(2,1)}, u32[]{:S(2)}, u32[]{:S(2)}) collective-permute-start(bf16[256,768]{1,0:T(8,128)(2,1)} %broadcast_select_fusion.1), channel_id=1, source_target_pairs={{0,1},{1,0},{2,3},{3,2},{4,5},{5,4},{6,7},{7,6},{8,9},{9,8},{10,11... | collective-permute-start | bytes 1179656 | tf_op jit(solution)/shard_map/ppermute | solution.py:148
  70.3 16.3 %copy-start.77 = (bf16[256,1536]{1,0:T(8,128)(2,1)S(1)}, bf16[256,1536]{1,0:T(8,128)(2,1)}, u32[]{:S(2)}) copy-start(bf16[256,1536]{1,0:T(8,128)(2,1)} %param.12) | copy-start | bytes 2359300
  99.9 10.1 %collective-permute-start.16 = (bf16[15,1536]{1,0:T(8,128)(2,1)S(1)}, bf16[15,1536]{1,0:T(8,128)(2,1)S(1)}, u32[]{:S(2)}, u32[]{:S(2)}) collective-permute-start(bf16[15,1536]{1,0:T(8,128)(2,1)S(1)} %get-tuple-element.46), channel_id=1, source_target_pairs={{1,2},{3,4},{5,6},{7,8},{9,10},{11,12},{13,14},{15,16},{17,18},{19... | collective-permute-start | bytes 138248 | tf_op jit(solution)/shard_map/ppermute | solution.py:195
  108.2 1.8 %collective-permute-start.17 = (bf16[15,1536]{1,0:T(8,128)(2,1)S(1)}, bf16[15,1536]{1,0:T(8,128)(2,1)S(1)}, u32[]{:S(2)}, u32[]{:S(2)}) collective-permute-start(bf16[15,1536]{1,0:T(8,128)(2,1)S(1)} %get-tuple-element.47), channel_id=1, source_target_pairs={{0,1},{1,0},{2,3},{3,2},{4,5},{5,4},{6,7},{7,6},{8,9},{9,8},{10,11... | collective-permute-start | bytes 138248 | tf_op jit(solution)/shard_map/ppermute | solution.py:198
  110.4 2.5 %copy-start.76 = (bf16[1536,1536]{1,0:T(8,128)(2,1)S(1)}, bf16[1536,1536]{1,0:T(8,128)(2,1)}, u32[]{:S(2)}) copy-start(bf16[1536,1536]{1,0:T(8,128)(2,1)} %param.23) | copy-start | bytes 14155780
  (72 other events, 91.1 us)

commit v8 on v6

--- a/solution.py
+++ b/solution.py
@@ -64,15 +64,15 @@
         for j in range(NBLK):
             bias_scr[j] = jnp.where(rec_q == reck_ref[j : j + 1, :], 0.0, -1e30)
 
-    for hh in range(2):
+    for hh in range(q_ref.shape[1] // HD):
         cols = slice(hh * HD, (hh + 1) * HD)
-        q_h = q_ref[:, cols]
+        q_h = (q_ref[:, cols].astype(jnp.float32) * (HD ** (-0.5))).astype(q_ref.dtype)
         wide_top = None
         for j in range(NBLK):
             s = lax.dot_general(
                 q_h, k_refs[j][:, cols], (((1,), (1,)), ((), ())),
                 preferred_element_type=jnp.float32,
-            ) * (HD ** (-0.5)) + bias_scr[j]
+            ) + bias_scr[j]
             s_scr[j] = s
             part = fold_lanes(s, jnp.maximum)
             wide_top = part if wide_top is None else jnp.maximum(wide_top, part)
@@ -92,7 +92,7 @@
 
 def attend(rec_q, rec_k, query, keys, vals):
     frames, width = query.shape
-    pair = 2 * HD
+    pair = 4 * HD
     tile = pl.BlockSpec((frames, pair), lambda g: (0, g))
     return pl.pallas_call(
         attend_kernel,

time: 110 us -> 109 us (level)
  no operation moved by 1% of the time
where the time goes in v8:
time: 109 us; the launch traced here: 108 us
  starting transfers between devices  52 us (48%)
  other arithmetic  17.7 us (16%)
  Pallas kernels  15.6 us (14%)
  local copies, waits for them, and re-layouts  8.19 us (8%)
  matrix products  6.64 us (6%)
  waiting for transfers between devices  6.62 us (6%)
    ppermute x8, starting transfers between devices, shifted_2(): return lax.ppermute(block, axis, route)  42.1 us
    pallas_call x1, Pallas kernels, attend(): pl.pallas_call(attend_kernel, grid=(width // pair,), in_specs=[pl.BlockSp...  15.6 us
    convert_element_type x1, other arithmetic, shards(): (shifted * jax.nn.sigmoid(shifted)).astype(jnp.bfloat16)  9.78 us
    ppermute x1, starting transfers between devices, shards(): lax.ppermute(lax.select(parity == 0, head_rows, tail_rows), ('grp', 'blk'...  8.34 us
    ppermute x8, waiting for transfers between devices, shifted_2(): return lax.ppermute(block, axis, route)  6.34 us
    dot_general x1, matrix products, shards(): jnp.dot(act, pointwise_weight, preferred_element_type=jnp.float32)  4.6 us
    slice x2, local copies, waits for them, and re-layouts, shards(): depthwise_taps[tap]  3.8 us
  transfers between devices with their start and end apart: 18, of which 3 were waited for; matrix products, arithmetic and copies ran while one was open for 12% of the time, Pallas kernels for 0%

profile of v8, /device:TPU:16, one launch (start us, length us, event | category | flops | bytes accessed | tf_op | source)
XLA Modules:
  0.0 107.6 jit_solution(5794474623783412301)
XLA Ops:
  0.0 3.9 %collective-permute-start.8 = (bf16[256,768]{1,0:T(8,128)(2,1)}, bf16[256,768]{1,0:T(8,128)(2,1)}, u32[]{:S(2)}, u32[]{:S(2)}) collective-permute-start(bf16[256,768]{1,0:T(8,128)(2,1)} %refs_9_.1), channel_id=1, source_target_pairs={{0,2},{1,3},{2,4},{3,5},{4,6},{5,7},{6,8},{7,9},{8,10},{9,11},{10,... | collective-permute-start | bytes 1179656 | tf_op jit(solution)/shard_map/ppermute | solution.py:16
  4.0 7.9 %collective-permute-start.9 = (bf16[256,768]{1,0:T(8,128)(2,1)}, bf16[256,768]{1,0:T(8,128)(2,1)}, u32[]{:S(2)}, u32[]{:S(2)}) collective-permute-start(bf16[256,768]{1,0:T(8,128)(2,1)} %refs_9_.1), channel_id=1, source_target_pairs={{2,0},{3,1},{4,2},{5,3},{6,4},{7,5},{8,6},{9,7},{10,8},{11,9},{12,... | collective-permute-start | bytes 1179656 | tf_op jit(solution)/shard_map/ppermute | solution.py:16
  11.9 1.9 %collective-permute-start = (bf16[256,768]{1,0:T(8,128)(2,1)}, bf16[256,768]{1,0:T(8,128)(2,1)}, u32[]{:S(2)}, u32[]{:S(2)}) collective-permute-start(bf16[256,768]{1,0:T(8,128)(2,1)} %refs_0_.1), channel_id=1, source_target_pairs={{0,2},{1,3},{2,4},{3,5},{4,6},{5,7},{6,8},{7,9},{8,10},{9,11},{10,... | collective-permute-start | bytes 1179656 | tf_op jit(solution)/shard_map/ppermute | solution.py:16
  13.8 8.1 %collective-permute-start.1 = (bf16[256,768]{1,0:T(8,128)(2,1)}, bf16[256,768]{1,0:T(8,128)(2,1)}, u32[]{:S(2)}, u32[]{:S(2)}) collective-permute-start(bf16[256,768]{1,0:T(8,128)(2,1)} %refs_0_.1), channel_id=1, source_target_pairs={{2,0},{3,1},{4,2},{5,3},{6,4},{7,5},{8,6},{9,7},{10,8},{11,9},{12,... | collective-permute-start | bytes 1179656 | tf_op jit(solution)/shard_map/ppermute | solution.py:16
  22.3 0.8 copy.16
  24.0 1.4 %convert_reduce_fusion.1 = s32[2304]{0:T(1024)S(1)} fusion(s32[128]{0:T(128)S(1)} %sub.49, s32[2304]{0:T(1024)S(1)} %add.220), kind=kLoop, calls=%fused_computation.107 | loop fusion | flops 882432 | bytes 18944 | tf_op jit(solution)/shard_map/reduce_sum | solution.py:33
  26.4 1.9 %collective-permute-start.10 = (bf16[256,768]{1,0:T(8,128)(2,1)}, bf16[256,768]{1,0:T(8,128)(2,1)S(1)}, u32[]{:S(2)}, u32[]{:S(2)}) collective-permute-start(bf16[256,768]{1,0:T(8,128)(2,1)} %collective-permute-done.8.refs_10_), channel_id=1, source_target_pairs={{0,2},{1,3},{2,4},{3,5},{4,6},{5,7},{6,8},{7,9},{8,10},{9,11},{10,... | collective-permute-start | bytes 1179656 | tf_op jit(solution)/shard_map/ppermute | solution.py:16
  28.3 8.1 %collective-permute-start.11 = (bf16[256,768]{1,0:T(8,128)(2,1)}, bf16[256,768]{1,0:T(8,128)(2,1)S(1)}, u32[]{:S(2)}, u32[]{:S(2)}) collective-permute-start(bf16[256,768]{1,0:T(8,128)(2,1)} %collective-permute-done.9.refs_11_), channel_id=1, source_target_pairs={{2,0},{3,1},{4,2},{5,3},{6,4},{7,5},{8,6},{9,7},{10,8},{11,9},{12,... | collective-permute-start | bytes 1179656 | tf_op jit(solution)/shard_map/ppermute | solution.py:16
  36.7 1.9 %collective-permute-start.2 = (bf16[256,768]{1,0:T(8,128)(2,1)}, bf16[256,768]{1,0:T(8,128)(2,1)S(1)}, u32[]{:S(2)}, u32[]{:S(2)}) collective-permute-start(bf16[256,768]{1,0:T(8,128)(2,1)} %collective-permute-done.refs_1_), channel_id=1, source_target_pairs={{0,2},{1,3},{2,4},{3,5},{4,6},{5,7},{6,8},{7,9},{8,10},{9,11},{10,... | collective-permute-start | bytes 1179656 | tf_op jit(solution)/shard_map/ppermute | solution.py:16
  38.6 8.1 %collective-permute-start.3 = (bf16[256,768]{1,0:T(8,128)(2,1)}, bf16[256,768]{1,0:T(8,128)(2,1)S(1)}, u32[]{:S(2)}, u32[]{:S(2)}) collective-permute-start(bf16[256,768]{1,0:T(8,128)(2,1)} %collective-permute-done.1.refs_2_), channel_id=1, source_target_pairs={{2,0},{3,1},{4,2},{5,3},{6,4},{7,5},{8,6},{9,7},{10,8},{11,9},{12,... | collective-permute-start | bytes 1179656 | tf_op jit(solution)/shard_map/ppermute | solution.py:16
  48.1 0.8 broadcast_select_fusion
  48.9 5.0 %collective-permute-done.2.refs_3_ = bf16[256,768]{1,0:T(8,128)(2,1)S(1)} collective-permute-done((bf16[256,768]{1,0:T(8,128)(2,1)}, bf16[256,768]{1,0:T(8,128)(2,1)S(1)}, u32[]{:S(2)}, u32[]{:S(2)}) %collective-permute-start.2) | collective-permute-done | bytes 393248 | tf_op jit(solution)/shard_map/ppermute | solution.py:16
  53.9 1.3 %collective-permute-done.3.refs_4_ = bf16[256,768]{1,0:T(8,128)(2,1)S(1)} collective-permute-done((bf16[256,768]{1,0:T(8,128)(2,1)}, bf16[256,768]{1,0:T(8,128)(2,1)S(1)}, u32[]{:S(2)}, u32[]{:S(2)}) %collective-permute-start.3) | collective-permute-done | bytes 393248 | tf_op jit(solution)/shard_map/ppermute | solution.py:16
  55.2 0.7 copy-done.4
  56.0 0.8 broadcast_select_fusion.1
  57.6 0.8 copy.17.recq_ref
  58.4 1.3 %pad.4.reck_ref = s32[16,256]{1,0:T(8,128)} pad(s32[9,256]{1,0:T(8,128)} %broadcast_select_fusion.6, s32[]{:T(128)} %constant.55.clone.1), padding=0_7x0_0 | pad | bytes 25604 | tf_op jit(solution)/shard_map/jit(_pad)/pad | solution.py:160
  59.7 2.4 %slice_reduce_fusion.30 = (f32[1536]{0:T(1024)S(1)}, f32[1536]{0:T(1024)}, f32[1536]{0:T(1024)}, f32[1536]{0:T(1024)}, f32[1536]{0:T(1024)}, /*index=5*/f32[1536...) fusion(f32[31,1536]{1,0:T(8,128)} %param.20), kind=kLoop, calls=%fused_computation.149 | loop fusion | bytes 233472 | tf_op jit(solution)/shard_map/slice | solution.py:198
  62.9 15.6 %shard_map.118 = bf16[256,768]{1,0:T(8,128)(2,1)} custom-call(s32[256,1]{1,0:T(8,128)} %copy.17.recq_ref, s32[16,256]{1,0:T(8,128)} %pad.4.reck_ref, bf16[256,768]{1,0:T(8,128)(2,1)} %q_ref.1, bf16[256,768]{1,0:T(8,128)(2,1)} %refs_0_.1, bf16[256,768]{1,0:T(8,128)(2,1)} %collective-permute-done.refs_1_, bf16[256,768]{1,0:T(8,128)(2,1)} %collective-permute-done.1.refs_2_, ...), custom_call_target="tpu_custom_call" | custom-call | tf_op jit(solution)/shard_map/pallas_call | solution.py:97
  78.5 2.0 %fusion.1 = bf16[256,1536]{1,0:T(8,128)(2,1)S(1)} fusion(bf16[256,768]{1,0:T(8,128)(2,1)} %shard_map.118, bf16[768,1536]{1,0:T(8,128)(2,1)S(1)} %copy-done, bf16[256,1536]{1,0:T(8,128)(2,1)} %param.12), kind=kOutput, calls=%fused_computation.3 | convolution fusion | flops 605159424 | bytes 4325376 | tf_op jit(solution)/shard_map/dot_general | solution.py:164
  81.7 8.3 %collective-permute-start.16 = (bf16[15,1536]{1,0:T(8,128)(2,1)S(1)}, bf16[15,1536]{1,0:T(8,128)(2,1)S(1)}, u32[]{:S(2)}, u32[]{:S(2)}) collective-permute-start(bf16[15,1536]{1,0:T(8,128)(2,1)S(1)} %get-tuple-element.36), channel_id=1, source_target_pairs={{1,2},{3,4},{5,6},{7,8},{9,10},{11,12},{13,14},{15,16},{17,18},{19... | collective-permute-start | bytes 138248 | tf_op jit(solution)/shard_map/ppermute | solution.py:179
  90.1 1.4 %slice_reduce_fusion.29 = (f32[1536]{0:T(1024)S(1)}, f32[1536]{0:T(1024)S(1)}, f32[1536]{0:T(1024)S(1)}, f32[1536]{0:T(1024)S(1)}, f32[1536]{0:T(1024)S(1)}, /*i...) fusion(f32[31,1536]{1,0:T(8,128)} %param.20), kind=kLoop, calls=%fused_computation.148 | loop fusion | bytes 147456 | tf_op jit(solution)/shard_map/slice | solution.py:198
  93.2 9.8 %multiply_convert_fusion = bf16[256,1536]{1,0:T(8,128)(2,1)S(1)} fusion(f32[286,1536]{1,0:T(8,128)S(1)} %convert_element_type.37, f32[1536]{0:T(1024)S(1)} %copy-done.25, f32[1536]{0:T(1024)S(1)} %copy-done.26, f32[1536]{0:T(1024)S(1)} %get-tuple-element.34, f32[1536]{0:T(1024)S(1)} %get-tuple-element.35, f32[1536]{0:T(1024)S(1)} %copy-done.5, ...), kind=kLoop, calls=%fused_computation.106 | loop fusion | flops 38928384 | bytes 49755904 | tf_op jit(solution)/shard_map/convert_element_type | solution.py:201
  103.0 4.6 %fusion = bf16[256,1536]{1,0:T(8,128)(2,1)} fusion(bf16[256,1536]{1,0:T(8,128)(2,1)S(1)} %multiply_convert_fusion, bf16[1536,1536]{1,0:T(8,128)(2,1)} %param.23, bf16[256,1536]{1,0:T(8,128)(2,1)S(1)} %fusion.1), kind=kOutput, calls=%fused_computation.2 | convolution fusion | flops 1209139200 | bytes 7077888 | tf_op jit(solution)/shard_map/dot_general | solution.py:202
  (146 shorter events, 7.5 us)
Async XLA Ops:
  0.0 78.5 %copy-start = (bf16[768,1536]{1,0:T(8,128)(2,1)S(1)}, bf16[768,1536]{1,0:T(8,128)(2,1)}, u32[]{:S(2)}) copy-start(bf16[768,1536]{1,0:T(8,128)(2,1)} %param.17) | copy-start | bytes 7077892
  0.0 26.4 %collective-permute-start.8 = (bf16[256,768]{1,0:T(8,128)(2,1)}, bf16[256,768]{1,0:T(8,128)(2,1)}, u32[]{:S(2)}, u32[]{:S(2)}) collective-permute-start(bf16[256,768]{1,0:T(8,128)(2,1)} %refs_9_.1), channel_id=1, source_target_pairs={{0,2},{1,3},{2,4},{3,5},{4,6},{5,7},{6,8},{7,9},{8,10},{9,11},{10,... | collective-permute-start | bytes 1179656 | tf_op jit(solution)/shard_map/ppermute | solution.py:16
  4.0 24.4 %collective-permute-start.9 = (bf16[256,768]{1,0:T(8,128)(2,1)}, bf16[256,768]{1,0:T(8,128)(2,1)}, u32[]{:S(2)}, u32[]{:S(2)}) collective-permute-start(bf16[256,768]{1,0:T(8,128)(2,1)} %refs_9_.1), channel_id=1, source_target_pairs={{2,0},{3,1},{4,2},{5,3},{6,4},{7,5},{8,6},{9,7},{10,8},{11,9},{12,... | collective-permute-start | bytes 1179656 | tf_op jit(solution)/shard_map/ppermute | solution.py:16
  11.9 24.8 %collective-permute-start = (bf16[256,768]{1,0:T(8,128)(2,1)}, bf16[256,768]{1,0:T(8,128)(2,1)}, u32[]{:S(2)}, u32[]{:S(2)}) collective-permute-start(bf16[256,768]{1,0:T(8,128)(2,1)} %refs_0_.1), channel_id=1, source_target_pairs={{0,2},{1,3},{2,4},{3,5},{4,6},{5,7},{6,8},{7,9},{8,10},{9,11},{10,... | collective-permute-start | bytes 1179656 | tf_op jit(solution)/shard_map/ppermute | solution.py:16
  13.8 24.8 %collective-permute-start.1 = (bf16[256,768]{1,0:T(8,128)(2,1)}, bf16[256,768]{1,0:T(8,128)(2,1)}, u32[]{:S(2)}, u32[]{:S(2)}) collective-permute-start(bf16[256,768]{1,0:T(8,128)(2,1)} %refs_0_.1), channel_id=1, source_target_pairs={{2,0},{3,1},{4,2},{5,3},{6,4},{7,5},{8,6},{9,7},{10,8},{11,9},{12,... | collective-permute-start | bytes 1179656 | tf_op jit(solution)/shard_map/ppermute | solution.py:16
  22.0 34.8 %collective-permute-start.12 = (bf16[256,768]{1,0:T(8,128)(2,1)}, bf16[256,768]{1,0:T(8,128)(2,1)}, u32[]{:S(2)}, u32[]{:S(2)}) collective-permute-start(bf16[256,768]{1,0:T(8,128)(2,1)} %refs_9_.1), channel_id=1, source_target_pairs={{0,1},{1,0},{2,3},{3,2},{4,5},{5,4},{6,7},{7,6},{8,9},{9,8},{10,11... | collective-permute-start | bytes 1179656 | tf_op jit(solution)/shard_map/ppermute | solution.py:148
  26.4 21.1 %collective-permute-start.10 = (bf16[256,768]{1,0:T(8,128)(2,1)}, bf16[256,768]{1,0:T(8,128)(2,1)S(1)}, u32[]{:S(2)}, u32[]{:S(2)}) collective-permute-start(bf16[256,768]{1,0:T(8,128)(2,1)} %collective-permute-done.8.refs_10_), channel_id=1, source_target_pairs={{0,2},{1,3},{2,4},{3,5},{4,6},{5,7},{6,8},{7,9},{8,10},{9,11},{10,... | collective-permute-start | bytes 1179656 | tf_op jit(solution)/shard_map/ppermute | solution.py:16
  28.3 19.3 %collective-permute-start.11 = (bf16[256,768]{1,0:T(8,128)(2,1)}, bf16[256,768]{1,0:T(8,128)(2,1)S(1)}, u32[]{:S(2)}, u32[]{:S(2)}) collective-permute-start(bf16[256,768]{1,0:T(8,128)(2,1)} %collective-permute-done.9.refs_11_), channel_id=1, source_target_pairs={{2,0},{3,1},{4,2},{5,3},{6,4},{7,5},{8,6},{9,7},{10,8},{11,9},{12,... | collective-permute-start | bytes 1179656 | tf_op jit(solution)/shard_map/ppermute | solution.py:16
  36.7 17.2 %collective-permute-start.2 = (bf16[256,768]{1,0:T(8,128)(2,1)}, bf16[256,768]{1,0:T(8,128)(2,1)S(1)}, u32[]{:S(2)}, u32[]{:S(2)}) collective-permute-start(bf16[256,768]{1,0:T(8,128)(2,1)} %collective-permute-done.refs_1_), channel_id=1, source_target_pairs={{0,2},{1,3},{2,4},{3,5},{4,6},{5,7},{6,8},{7,9},{8,10},{9,11},{10,... | collective-permute-start | bytes 1179656 | tf_op jit(solution)/shard_map/ppermute | solution.py:16
  38.6 16.6 %collective-permute-start.3 = (bf16[256,768]{1,0:T(8,128)(2,1)}, bf16[256,768]{1,0:T(8,128)(2,1)S(1)}, u32[]{:S(2)}, u32[]{:S(2)}) collective-permute-start(bf16[256,768]{1,0:T(8,128)(2,1)} %collective-permute-done.1.refs_2_), channel_id=1, source_target_pairs={{2,0},{3,1},{4,2},{5,3},{6,4},{7,5},{8,6},{9,7},{10,8},{11,9},{12,... | collective-permute-start | bytes 1179656 | tf_op jit(solution)/shard_map/ppermute | solution.py:16
  47.5 15.4 %copy-start.1 = (bf16[256,768]{1,0:T(8,128)(2,1)}, bf16[256,768]{1,0:T(8,128)(2,1)S(1)}, u32[]{:S(2)}) copy-start(bf16[256,768]{1,0:T(8,128)(2,1)S(1)} %collective-permute-done.10.refs_12_) | copy-start | bytes 1179652
  47.5 9.3 %collective-permute-start.4 = (bf16[256,768]{1,0:T(8,128)(2,1)}, bf16[256,768]{1,0:T(8,128)(2,1)}, u32[]{:S(2)}, u32[]{:S(2)}) collective-permute-start(bf16[256,768]{1,0:T(8,128)(2,1)} %refs_0_.1), channel_id=1, source_target_pairs={{0,1},{1,0},{2,3},{3,2},{4,5},{5,4},{6,7},{7,6},{8,9},{9,8},{10,11... | collective-permute-start | bytes 1179656 | tf_op jit(solution)/shard_map/ppermute | solution.py:148
  47.6 15.3 %copy-start.2 = (bf16[256,768]{1,0:T(8,128)(2,1)}, bf16[256,768]{1,0:T(8,128)(2,1)S(1)}, u32[]{:S(2)}) copy-start(bf16[256,768]{1,0:T(8,128)(2,1)S(1)} %collective-permute-done.11.refs_13_) | copy-start | bytes 1179652
  47.6 9.7 %collective-permute-start.13 = (bf16[256,768]{1,0:T(8,128)(2,1)}, bf16[256,768]{1,0:T(8,128)(2,1)}, u32[]{:S(2)}, u32[]{:S(2)}) collective-permute-start(bf16[256,768]{1,0:T(8,128)(2,1)} %collective-permute-done.8.refs_10_), channel_id=1, source_target_pairs={{0,1},{1,0},{2,3},{3,2},{4,5},{5,4},{6,7},{7,6},{8,9},{9,8},{10,11... | collective-permute-start | bytes 1179656 | tf_op jit(solution)/shard_map/ppermute | solution.py:148
  53.9 9.0 %copy-start.3 = (bf16[256,768]{1,0:T(8,128)(2,1)}, bf16[256,768]{1,0:T(8,128)(2,1)S(1)}, u32[]{:S(2)}) copy-start(bf16[256,768]{1,0:T(8,128)(2,1)S(1)} %collective-permute-done.2.refs_3_) | copy-start | bytes 1179652
  53.9 8.9 %collective-permute-start.14 = (bf16[256,768]{1,0:T(8,128)(2,1)}, bf16[256,768]{1,0:T(8,128)(2,1)}, u32[]{:S(2)}, u32[]{:S(2)}) collective-permute-start(bf16[256,768]{1,0:T(8,128)(2,1)} %collective-permute-done.9.refs_11_), channel_id=1, source_target_pairs={{0,1},{1,0},{2,3},{3,2},{4,5},{5,4},{6,7},{7,6},{8,9},{9,8},{10,11... | collective-permute-start | bytes 1179656 | tf_op jit(solution)/shard_map/ppermute | solution.py:148
  55.2 7.6 %collective-permute-start.5 = (bf16[256,768]{1,0:T(8,128)(2,1)}, bf16[256,768]{1,0:T(8,128)(2,1)}, u32[]{:S(2)}, u32[]{:S(2)}) collective-permute-start(bf16[256,768]{1,0:T(8,128)(2,1)} %collective-permute-done.refs_1_), channel_id=1, source_target_pairs={{0,1},{1,0},{2,3},{3,2},{4,5},{5,4},{6,7},{7,6},{8,9},{9,8},{10,11... | collective-permute-start | bytes 1179656 | tf_op jit(solution)/shard_map/ppermute | solution.py:148
  56.8 6.1 %collective-permute-start.6 = (bf16[256,768]{1,0:T(8,128)(2,1)}, bf16[256,768]{1,0:T(8,128)(2,1)}, u32[]{:S(2)}, u32[]{:S(2)}) collective-permute-start(bf16[256,768]{1,0:T(8,128)(2,1)} %collective-permute-done.1.refs_2_), channel_id=1, source_target_pairs={{0,1},{1,0},{2,3},{3,2},{4,5},{5,4},{6,7},{7,6},{8,9},{9,8},{10,11... | collective-permute-start | bytes 1179656 | tf_op jit(solution)/shard_map/ppermute | solution.py:148
  56.8 6.1 %collective-permute-start.15 = (bf16[256,768]{1,0:T(8,128)(2,1)}, bf16[256,768]{1,0:T(8,128)(2,1)}, u32[]{:S(2)}, u32[]{:S(2)}) collective-permute-start(bf16[256,768]{1,0:T(8,128)(2,1)} %broadcast_select_fusion), channel_id=1, source_target_pairs={{0,1},{1,0},{2,3},{3,2},{4,5},{5,4},{6,7},{7,6},{8,9},{9,8},{10,11... | collective-permute-start | bytes 1179656 | tf_op jit(solution)/shard_map/ppermute | solution.py:148
  57.3 5.6 %collective-permute-start.7 = (bf16[256,768]{1,0:T(8,128)(2,1)}, bf16[256,768]{1,0:T(8,128)(2,1)}, u32[]{:S(2)}, u32[]{:S(2)}) collective-permute-start(bf16[256,768]{1,0:T(8,128)(2,1)} %broadcast_select_fusion.1), channel_id=1, source_target_pairs={{0,1},{1,0},{2,3},{3,2},{4,5},{5,4},{6,7},{7,6},{8,9},{9,8},{10,11... | collective-permute-start | bytes 1179656 | tf_op jit(solution)/shard_map/ppermute | solution.py:148
  81.7 10.1 %collective-permute-start.16 = (bf16[15,1536]{1,0:T(8,128)(2,1)S(1)}, bf16[15,1536]{1,0:T(8,128)(2,1)S(1)}, u32[]{:S(2)}, u32[]{:S(2)}) collective-permute-start(bf16[15,1536]{1,0:T(8,128)(2,1)S(1)} %get-tuple-element.36), channel_id=1, source_target_pairs={{1,2},{3,4},{5,6},{7,8},{9,10},{11,12},{13,14},{15,16},{17,18},{19... | collective-permute-start | bytes 138248 | tf_op jit(solution)/shard_map/ppermute | solution.py:179
  90.0 1.8 %collective-permute-start.17 = (bf16[15,1536]{1,0:T(8,128)(2,1)S(1)}, bf16[15,1536]{1,0:T(8,128)(2,1)S(1)}, u32[]{:S(2)}, u32[]{:S(2)}) collective-permute-start(bf16[15,1536]{1,0:T(8,128)(2,1)S(1)} %get-tuple-element.37), channel_id=1, source_target_pairs={{0,1},{1,0},{2,3},{3,2},{4,5},{5,4},{6,7},{7,6},{8,9},{9,8},{10,11... | collective-permute-start | bytes 138248 | tf_op jit(solution)/shard_map/ppermute | solution.py:182
  92.2 0.8 copy-start.25
  92.2 0.8 copy-start.26
  (41 other events, 31.3 us)

commit v9 on v8

--- a/solution.py
+++ b/solution.py
@@ -94,6 +94,7 @@
     frames, width = query.shape
     pair = 4 * HD
     tile = pl.BlockSpec((frames, pair), lambda g: (0, g))
+    v_tile = pl.BlockSpec((frames, pair), lambda g: (0, g + width // pair))
     return pl.pallas_call(
         attend_kernel,
         grid=(width // pair,),
@@ -102,7 +103,8 @@
             pl.BlockSpec(rec_k.shape, lambda g: (0, 0)),
             tile,
         ]
-        + [tile] * (2 * NBLK),
+        + [tile] * NBLK
+        + [v_tile] * NBLK,
         out_specs=tile,
         out_shape=jax.ShapeDtypeStruct((frames, width), jnp.bfloat16),
         scratch_shapes=[pltpu.VMEM((NBLK, frames, frames), jnp.float32)] * 2,
@@ -135,7 +137,7 @@
     def hop(pair, distance):
         return tuple(shifted_2(x, ("grp", "blk"), distance) for x in pair)
 
-    own_pair = (key_vectors, values)
+    own_pair = (jnp.concatenate([key_vectors, values], axis=1),)
     from_m2 = hop(own_pair, 2)
     from_p2 = hop(own_pair, -2)
     from_m4 = hop(from_m2, 2)
@@ -159,7 +161,7 @@
     rows = -(-NBLK // 8) * 8
     key_rec = jnp.pad(key_rec, ((0, rows - NBLK), (0, 0)), constant_values=-1)
     keys = [p[0] for p in pairs]
-    vals = [p[1] for p in pairs]
+    vals = keys
     attended = attend(own_rec[:, None], key_rec, queries, keys, vals)
     projected = jnp.dot(attended, output_weight, preferred_element_type=jnp.float32)
     resid = lax.optimization_barrier(

time: 109 us -> 103 us (0.945); the launches traced: 108 us -> 103 us
  waiting for transfers between devices: 6.62 us -> 29.4 us
  starting transfers between devices: 52 us -> 31.2 us
  matrix products: 6.64 us -> 4.3 us
  other arithmetic: 17.7 us -> 15.5 us
  local copies, waits for them, and re-layouts: 8.19 us -> 6.36 us
    ppermute x8 -> x4, waiting for transfers between devices: 6.34 us -> 27.3 us  [shifted_2(): return lax.ppermute(block, axis, route)]
    ppermute x8 -> x4, starting transfers between devices: 42.1 us -> 21.8 us  [shifted_2(): return lax.ppermute(block, axis, route)]
    slice x2, local copies, waits for them, and re-layouts: 3.8 us -> 0.51 us  [shards(): depthwise_taps[tap]]
    dot_general x1, matrix products: 4.6 us -> 2.27 us  [shards(): jnp.dot(act, pointwise_weight, preferred_element_type=jnp.float32)]
    concatenate x0 -> x1, local copies, waits for them, and re-layouts: none -> 1.77 us  [shards(): own_pair = (jnp.concatenate([key_vectors, values], axis=1),)]
    unnamed x94 -> x57, local copies, waits for them, and re-layouts: 1.41 us -> 2.47 us
  transfers between devices with their start and end apart: 18 -> 10, of which waited for: 3 -> 5; matrix products, arithmetic and copies ran while one was open for 12% -> 7% of each run, Pallas kernels for 0% -> 0%
where the time goes in v9:
time: 103 us
  starting transfers between devices  31.2 us (30%)
  waiting for transfers between devices  29.4 us (29%)
  Pallas kernels  15.6 us (15%)
  other arithmetic  15.5 us (15%)
  local copies, waits for them, and re-layouts  6.36 us (6%)
  matrix products  4.3 us (4%)
    ppermute x4, waiting for transfers between devices, shifted_2(): return lax.ppermute(block, axis, route)  27.3 us
    ppermute x4, starting transfers between devices, shifted_2(): return lax.ppermute(block, axis, route)  21.8 us
    pallas_call x1, Pallas kernels, attend(): pl.pallas_call(attend_kernel, grid=(width // pair,), in_specs=[pl.BlockSp...  15.6 us
    convert_element_type x1, other arithmetic, shards(): (shifted * jax.nn.sigmoid(shifted)).astype(jnp.bfloat16)  9.27 us
    ppermute x1, starting transfers between devices, shards(): lax.ppermute(lax.select(parity == 0, head_rows, tail_rows), ('grp', 'blk'...  8.35 us
    unnamed x57, local copies, waits for them, and re-layouts  2.47 us
    dot_general x1, matrix products, shards(): jnp.dot(act, pointwise_weight, preferred_element_type=jnp.float32)  2.27 us
  transfers between devices with their start and end apart: 10, of which 5 were waited for; matrix products, arithmetic and copies ran while one was open for 7% of the time, Pallas kernels for 0%

profile of v9, /device:TPU:16, one launch (start us, length us, event | category | flops | bytes accessed | tf_op | source)
XLA Modules:
  0.0 103.0 jit_solution(8757457003295846960)
XLA Ops:
  0.0 1.9 %constant_dynamic-update-slice_fusion.1 = bf16[256,1536]{1,0:T(8,128)(2,1)} fusion(bf16[256,768]{1,0:T(8,128)(2,1)} %param.14), kind=kLoop, calls=%fused_computation.119 | loop fusion | bytes 786432
  1.9 1.8 %constant_dynamic-update-slice_fusion.refs_0_.refs_9_ = bf16[256,1536]{1,0:T(8,128)(2,1)} fusion(bf16[256,1536]{1,0:T(8,128)(2,1)} %constant_dynamic-update-slice_fusion.1, bf16[256,768]{1,0:T(8,128)(2,1)} %param.15), kind=kLoop, calls=%fused_computation.118 | loop fusion | bytes 786432 | tf_op jit(solution)/shard_map/concatenate | solution.py:140
  3.7 3.8 %collective-permute-start = (bf16[256,1536]{1,0:T(8,128)(2,1)}, bf16[256,1536]{1,0:T(8,128)(2,1)}, u32[]{:S(2)}, u32[]{:S(2)}) collective-permute-start(bf16[256,1536]{1,0:T(8,128)(2,1)} %constant_dynamic-update-slice_fusion.refs_0_.refs_9_), channel_id=1, source_target_pairs={{0,2},{1,3},{2,4},{3,5},{4,6},{5,7},{6,8},{7,9},{8,10},{9,11},{10,... | collective-permute-start | bytes 2359304 | tf_op jit(solution)/shard_map/ppermute | solution.py:16
  7.5 7.9 %collective-permute-start.1 = (bf16[256,1536]{1,0:T(8,128)(2,1)}, bf16[256,1536]{1,0:T(8,128)(2,1)}, u32[]{:S(2)}, u32[]{:S(2)}) collective-permute-start(bf16[256,1536]{1,0:T(8,128)(2,1)} %constant_dynamic-update-slice_fusion.refs_0_.refs_9_), channel_id=1, source_target_pairs={{2,0},{3,1},{4,2},{5,3},{6,4},{7,5},{8,6},{9,7},{10,8},{11,9},{12,... | collective-permute-start | bytes 2359304 | tf_op jit(solution)/shard_map/ppermute | solution.py:16
  16.4 1.5 %convert_reduce_fusion.1 = s32[2304]{0:T(1024)S(1)} fusion(s32[128]{0:T(128)S(1)} %sub.49, s32[2304]{0:T(1024)S(1)} %add.220), kind=kLoop, calls=%fused_computation.107 | loop fusion | flops 882432 | bytes 18944 | tf_op jit(solution)/shard_map/reduce_sum | solution.py:33
  17.8 13.5 %collective-permute-done.refs_1_.refs_10_ = bf16[256,1536]{1,0:T(8,128)(2,1)} collective-permute-done((bf16[256,1536]{1,0:T(8,128)(2,1)}, bf16[256,1536]{1,0:T(8,128)(2,1)}, u32[]{:S(2)}, u32[]{:S(2)}) %collective-permute-start) | collective-permute-done | bytes 786464 | tf_op jit(solution)/shard_map/ppermute | solution.py:16
  31.4 1.9 %collective-permute-start.2 = (bf16[256,1536]{1,0:T(8,128)(2,1)}, bf16[256,1536]{1,0:T(8,128)(2,1)S(1)}, u32[]{:S(2)}, u32[]{:S(2)}) collective-permute-start(bf16[256,1536]{1,0:T(8,128)(2,1)} %collective-permute-done.refs_1_.refs_10_), channel_id=1, source_target_pairs={{0,2},{1,3},{2,4},{3,5},{4,6},{5,7},{6,8},{7,9},{8,10},{9,11},{10,... | collective-permute-start | bytes 2359304 | tf_op jit(solution)/shard_map/ppermute | solution.py:16
  33.3 8.1 %collective-permute-start.3 = (bf16[256,1536]{1,0:T(8,128)(2,1)}, bf16[256,1536]{1,0:T(8,128)(2,1)}, u32[]{:S(2)}, u32[]{:S(2)}) collective-permute-start(bf16[256,1536]{1,0:T(8,128)(2,1)} %collective-permute-done.1.refs_2_.refs_11_), channel_id=1, source_target_pairs={{2,0},{3,1},{4,2},{5,3},{6,4},{7,5},{8,6},{9,7},{10,8},{11,9},{12,... | collective-permute-start | bytes 2359304 | tf_op jit(solution)/shard_map/ppermute | solution.py:16
  41.5 0.8 copy.17.recq_ref
  42.4 0.6 pad.4.reck_ref
  43.4 0.5 collective-permute-start.6
  43.9 12.5 %collective-permute-done.2.refs_3_.refs_12_ = bf16[256,1536]{1,0:T(8,128)(2,1)S(1)} collective-permute-done((bf16[256,1536]{1,0:T(8,128)(2,1)}, bf16[256,1536]{1,0:T(8,128)(2,1)S(1)}, u32[]{:S(2)}, u32[]{:S(2)}) %collective-permute-start.2) | collective-permute-done | bytes 786464 | tf_op jit(solution)/shard_map/ppermute | solution.py:16
  56.4 1.3 %collective-permute-done.3.refs_4_.refs_13_ = bf16[256,1536]{1,0:T(8,128)(2,1)} collective-permute-done((bf16[256,1536]{1,0:T(8,128)(2,1)}, bf16[256,1536]{1,0:T(8,128)(2,1)}, u32[]{:S(2)}, u32[]{:S(2)}) %collective-permute-start.3) | collective-permute-done | bytes 786464 | tf_op jit(solution)/shard_map/ppermute | solution.py:16
  57.7 1.2 %broadcast_select_fusion = bf16[256,1536]{1,0:T(8,128)(2,1)S(1)} fusion(bf16[256,1536]{1,0:T(8,128)(2,1)} %collective-permute-done.3.refs_4_.refs_13_, bf16[256,1536]{1,0:T(8,128)(2,1)S(1)} %collective-permute-done.2.refs_3_.refs_12_, pred[]{:T(512)S(6)} %eq.102), kind=kLoop, calls=%fused_computation.109 | loop fusion | flops 393216 | bytes 2359297 | tf_op jit(solution)/shard_map/select_n | solution.py:147
  59.2 0.7 slice_compare_fusion.29
  59.9 0.7 slice_compare_fusion.30
  60.6 0.8 collective-permute-done.7.refs_8_.refs_17_
  61.4 15.6 %shard_map.118 = bf16[256,768]{1,0:T(8,128)(2,1)} custom-call(s32[256,1]{1,0:T(8,128)} %copy.17.recq_ref, s32[16,256]{1,0:T(8,128)} %pad.4.reck_ref, bf16[256,768]{1,0:T(8,128)(2,1)} %q_ref.1, bf16[256,1536]{1,0:T(8,128)(2,1)} %constant_dynamic-update-slice_fusion.refs_0_.refs_9_, bf16[256,1536]{1,0:T(8,128)(2,1)} %collective-permute-done.refs_1_.refs_10_, ...), custom_call_target="tpu_custom_call" | custom-call | tf_op jit(solution)/shard_map/pallas_call | solution.py:98
  77.0 2.0 %fusion.1 = bf16[256,1536]{1,0:T(8,128)(2,1)S(1)} fusion(bf16[256,768]{1,0:T(8,128)(2,1)} %shard_map.118, bf16[768,1536]{1,0:T(8,128)(2,1)S(1)} %copy-done, bf16[256,1536]{1,0:T(8,128)(2,1)} %param.12), kind=kOutput, calls=%fused_computation.3 | convolution fusion | flops 605159424 | bytes 4325376 | tf_op jit(solution)/shard_map/dot_general | solution.py:166
  79.8 0.4 fusion.7
  80.2 8.3 %collective-permute-start.8 = (bf16[15,1536]{1,0:T(8,128)(2,1)S(1)}, bf16[15,1536]{1,0:T(8,128)(2,1)S(1)}, u32[]{:S(2)}, u32[]{:S(2)}) collective-permute-start(bf16[15,1536]{1,0:T(8,128)(2,1)S(1)} %get-tuple-element.36), channel_id=1, source_target_pairs={{1,2},{3,4},{5,6},{7,8},{9,10},{11,12},{13,14},{15,16},{17,18},{19... | collective-permute-start | bytes 138248 | tf_op jit(solution)/shard_map/ppermute | solution.py:181
  89.0 1.3 %collective-permute-done.8 = bf16[15,1536]{1,0:T(8,128)(2,1)S(1)} collective-permute-done((bf16[15,1536]{1,0:T(8,128)(2,1)S(1)}, bf16[15,1536]{1,0:T(8,128)(2,1)S(1)}, u32[]{:S(2)}, u32[]{:S(2)}) %collective-permute-start.8) | collective-permute-done | bytes 46112 | tf_op jit(solution)/shard_map/ppermute | solution.py:181
  91.4 9.3 %multiply_convert_fusion = bf16[256,1536]{1,0:T(8,128)(2,1)S(1)} fusion(f32[286,1536]{1,0:T(8,128)S(1)} %convert_element_type.37, f32[1536]{0:T(1024)S(1)} %copy-done.5, f32[1536]{0:T(1024)S(1)} %copy-done.6, f32[1536]{0:T(1024)S(1)} %get-tuple-element.34, f32[1536]{0:T(1024)S(1)} %get-tuple-element.35, f32[1536]{0:T(1024)S(1)} %get-tuple-element.6, ...), kind=kLoop, calls=%fused_computation.106 | loop fusion | flops 38928384 | bytes 49755904 | tf_op jit(solution)/shard_map/convert_element_type | solution.py:203
  100.7 2.3 %fusion = bf16[256,1536]{1,0:T(8,128)(2,1)} fusion(bf16[256,1536]{1,0:T(8,128)(2,1)S(1)} %multiply_convert_fusion, bf16[1536,1536]{1,0:T(8,128)(2,1)S(1)} %bitcast.18, bf16[256,1536]{1,0:T(8,128)(2,1)S(1)} %fusion.1), kind=kOutput, calls=%fused_computation.2 | convolution fusion | flops 1209139200 | bytes 7077888 | tf_op jit(solution)/shard_map/dot_general | solution.py:204
  (94 shorter events, 3.7 us)
Async XLA Ops:
  0.0 77.0 %copy-start = (bf16[768,1536]{1,0:T(8,128)(2,1)S(1)}, bf16[768,1536]{1,0:T(8,128)(2,1)}, u32[]{:S(2)}) copy-start(bf16[768,1536]{1,0:T(8,128)(2,1)} %param.17) | copy-start | bytes 7077892
  0.0 15.8 %copy-start.25 = (s32[128]{0:T(128)S(1)}, s32[128]{0:T(128)}, u32[]{:S(2)}) copy-start(s32[128]{0:T(128)} %param.16) | copy-start | bytes 1540
  0.0 43.0 %copy-start.2 = (f32[31,1536]{1,0:T(8,128)S(1)}, f32[31,1536]{1,0:T(8,128)}, u32[]{:S(2)}) copy-start(f32[31,1536]{1,0:T(8,128)} %param.20) | copy-start | bytes 571396
  3.7 27.7 %collective-permute-start = (bf16[256,1536]{1,0:T(8,128)(2,1)}, bf16[256,1536]{1,0:T(8,128)(2,1)}, u32[]{:S(2)}, u32[]{:S(2)}) collective-permute-start(bf16[256,1536]{1,0:T(8,128)(2,1)} %constant_dynamic-update-slice_fusion.refs_0_.refs_9_), channel_id=1, source_target_pairs={{0,2},{1,3},{2,4},{3,5},{4,6},{5,7},{6,8},{7,9},{8,10},{9,11},{10,... | collective-permute-start | bytes 2359304 | tf_op jit(solution)/shard_map/ppermute | solution.py:16
  7.5 25.8 %collective-permute-start.1 = (bf16[256,1536]{1,0:T(8,128)(2,1)}, bf16[256,1536]{1,0:T(8,128)(2,1)}, u32[]{:S(2)}, u32[]{:S(2)}) collective-permute-start(bf16[256,1536]{1,0:T(8,128)(2,1)} %constant_dynamic-update-slice_fusion.refs_0_.refs_9_), channel_id=1, source_target_pairs={{2,0},{3,1},{4,2},{5,3},{6,4},{7,5},{8,6},{9,7},{10,8},{11,9},{12,... | collective-permute-start | bytes 2359304 | tf_op jit(solution)/shard_map/ppermute | solution.py:16
  15.5 45.1 %collective-permute-start.4 = (bf16[256,1536]{1,0:T(8,128)(2,1)}, bf16[256,1536]{1,0:T(8,128)(2,1)}, u32[]{:S(2)}, u32[]{:S(2)}) collective-permute-start(bf16[256,1536]{1,0:T(8,128)(2,1)} %constant_dynamic-update-slice_fusion.refs_0_.refs_9_), channel_id=1, source_target_pairs={{0,1},{1,0},{2,3},{3,2},{4,5},{5,4},{6,7},{7,6},{8,9},{9,8},{10,11... | collective-permute-start | bytes 2359304 | tf_op jit(solution)/shard_map/ppermute | solution.py:150
  31.4 25.0 %collective-permute-start.2 = (bf16[256,1536]{1,0:T(8,128)(2,1)}, bf16[256,1536]{1,0:T(8,128)(2,1)S(1)}, u32[]{:S(2)}, u32[]{:S(2)}) collective-permute-start(bf16[256,1536]{1,0:T(8,128)(2,1)} %collective-permute-done.refs_1_.refs_10_), channel_id=1, source_target_pairs={{0,2},{1,3},{2,4},{3,5},{4,6},{5,7},{6,8},{7,9},{8,10},{9,11},{10,... | collective-permute-start | bytes 2359304 | tf_op jit(solution)/shard_map/ppermute | solution.py:16
  33.3 24.4 %collective-permute-start.3 = (bf16[256,1536]{1,0:T(8,128)(2,1)}, bf16[256,1536]{1,0:T(8,128)(2,1)}, u32[]{:S(2)}, u32[]{:S(2)}) collective-permute-start(bf16[256,1536]{1,0:T(8,128)(2,1)} %collective-permute-done.1.refs_2_.refs_11_), channel_id=1, source_target_pairs={{2,0},{3,1},{4,2},{5,3},{6,4},{7,5},{8,6},{9,7},{10,8},{11,9},{12,... | collective-permute-start | bytes 2359304 | tf_op jit(solution)/shard_map/ppermute | solution.py:16
  43.3 17.3 %collective-permute-start.5 = (bf16[256,1536]{1,0:T(8,128)(2,1)}, bf16[256,1536]{1,0:T(8,128)(2,1)}, u32[]{:S(2)}, u32[]{:S(2)}) collective-permute-start(bf16[256,1536]{1,0:T(8,128)(2,1)} %collective-permute-done.refs_1_.refs_10_), channel_id=1, source_target_pairs={{0,1},{1,0},{2,3},{3,2},{4,5},{5,4},{6,7},{7,6},{8,9},{9,8},{10,11... | collective-permute-start | bytes 2359304 | tf_op jit(solution)/shard_map/ppermute | solution.py:150
  43.4 17.2 %collective-permute-start.6 = (bf16[256,1536]{1,0:T(8,128)(2,1)}, bf16[256,1536]{1,0:T(8,128)(2,1)}, u32[]{:S(2)}, u32[]{:S(2)}) collective-permute-start(bf16[256,1536]{1,0:T(8,128)(2,1)} %collective-permute-done.1.refs_2_.refs_11_), channel_id=1, source_target_pairs={{0,1},{1,0},{2,3},{3,2},{4,5},{5,4},{6,7},{7,6},{8,9},{9,8},{10,11... | collective-permute-start | bytes 2359304 | tf_op jit(solution)/shard_map/ppermute | solution.py:150
  56.4 5.0 %copy-start.1 = (bf16[256,1536]{1,0:T(8,128)(2,1)}, bf16[256,1536]{1,0:T(8,128)(2,1)S(1)}, u32[]{:S(2)}) copy-start(bf16[256,1536]{1,0:T(8,128)(2,1)S(1)} %collective-permute-done.2.refs_3_.refs_12_) | copy-start | bytes 2359300
  58.9 2.5 %collective-permute-start.7 = (bf16[256,1536]{1,0:T(8,128)(2,1)S(1)}, bf16[256,1536]{1,0:T(8,128)(2,1)}, u32[]{:S(2)}, u32[]{:S(2)}) collective-permute-start(bf16[256,1536]{1,0:T(8,128)(2,1)S(1)} %broadcast_select_fusion), channel_id=1, source_target_pairs={{0,1},{1,0},{2,3},{3,2},{4,5},{5,4},{6,7},{7,6},{8,9},{9,8},{10,11... | collective-permute-start | bytes 2359304 | tf_op jit(solution)/shard_map/ppermute | solution.py:150
  79.1 0.7 copy-start.3
  79.1 0.7 copy-start.4
  80.2 10.1 %collective-permute-start.8 = (bf16[15,1536]{1,0:T(8,128)(2,1)S(1)}, bf16[15,1536]{1,0:T(8,128)(2,1)S(1)}, u32[]{:S(2)}, u32[]{:S(2)}) collective-permute-start(bf16[15,1536]{1,0:T(8,128)(2,1)S(1)} %get-tuple-element.36), channel_id=1, source_target_pairs={{1,2},{3,4},{5,6},{7,8},{9,10},{11,12},{13,14},{15,16},{17,18},{19... | collective-permute-start | bytes 138248 | tf_op jit(solution)/shard_map/ppermute | solution.py:181
  88.5 1.8 %collective-permute-start.9 = (bf16[15,1536]{1,0:T(8,128)(2,1)S(1)}, bf16[15,1536]{1,0:T(8,128)(2,1)S(1)}, u32[]{:S(2)}, u32[]{:S(2)}) collective-permute-start(bf16[15,1536]{1,0:T(8,128)(2,1)S(1)} %get-tuple-element.37), channel_id=1, source_target_pairs={{0,1},{1,0},{2,3},{3,2},{4,5},{5,4},{6,7},{7,6},{8,9},{9,8},{10,11... | collective-permute-start | bytes 138248 | tf_op jit(solution)/shard_map/ppermute | solution.py:184
  90.5 0.7 copy-start.5
  90.5 0.7 copy-start.6
  90.5 0.7 copy-start.7
  90.6 0.7 copy-start.8
  90.6 0.7 copy-start.9
  90.6 0.7 copy-start.10
  90.7 10.0 %slice-start = ((s8[4718592]{0:T(1024)(128)(4,1)}), s8[4194304]{0:T(1024)(128)(4,1)S(1)}, s32[]{:S(2)}) async-start(s8[4718592]{0:T(1024)(128)(4,1)} %bitcast.17), calls=%async_computation | async-start | bytes 8388608
  91.4 9.3 %slice-start.1 = ((s8[4718592]{0:T(1024)(128)(4,1)}), s8[524288]{0:T(1024)(128)(4,1)S(1)}, s32[]{:S(2)}) async-start(s8[4718592]{0:T(1024)(128)(4,1)} %bitcast.17), calls=%async_computation.1 | async-start | bytes 1048576
  (14 other events, 9.4 us)

commit v10 on v9

--- a/solution.py
+++ b/solution.py
@@ -94,7 +94,7 @@
     frames, width = query.shape
     pair = 4 * HD
     tile = pl.BlockSpec((frames, pair), lambda g: (0, g))
-    v_tile = pl.BlockSpec((frames, pair), lambda g: (0, g + width // pair))
+    v_tile = pl.BlockSpec((frames, pair), lambda g: (1, g))
     return pl.pallas_call(
         attend_kernel,
         grid=(width // pair,),
@@ -137,7 +137,7 @@
     def hop(pair, distance):
         return tuple(shifted_2(x, ("grp", "blk"), distance) for x in pair)
 
-    own_pair = (jnp.concatenate([key_vectors, values], axis=1),)
+    own_pair = (jnp.concatenate([key_vectors, values], axis=0),)
     from_m2 = hop(own_pair, 2)
     from_p2 = hop(own_pair, -2)
     from_m4 = hop(from_m2, 2)

time: 103 us -> 103 us (level)
  no operation moved by 1% of the time
where the time goes in v10:
time: 103 us
  starting transfers between devices  31.2 us (30%)
  waiting for transfers between devices  29.4 us (29%)
  Pallas kernels  15.6 us (15%)
  other arithmetic  15.5 us (15%)
  local copies, waits for them, and re-layouts  6.36 us (6%)
  matrix products  4.3 us (4%)
    ppermute x4, waiting for transfers between devices, shifted_2(): return lax.ppermute(block, axis, route)  27.3 us
    ppermute x4, starting transfers between devices, shifted_2(): return lax.ppermute(block, axis, route)  21.8 us
    pallas_call x1, Pallas kernels, attend(): pl.pallas_call(attend_kernel, grid=(width // pair,), in_specs=[pl.BlockSp...  15.6 us
    convert_element_type x1, other arithmetic, shards(): (shifted * jax.nn.sigmoid(shifted)).astype(jnp.bfloat16)  9.27 us
    ppermute x1, starting transfers between devices, shards(): lax.ppermute(lax.select(parity == 0, head_rows, tail_rows), ('grp', 'blk'...  8.33 us
    unnamed x57, local copies, waits for them, and re-layouts  2.47 us
    dot_general x1, matrix products, shards(): jnp.dot(act, pointwise_weight, preferred_element_type=jnp.float32)  2.27 us
  transfers between devices with their start and end apart: 10, of which 5 were waited for; matrix products, arithmetic and copies ran while one was open for 7% of the time, Pallas kernels for 0%

profile of v10, /device:TPU:16, one launch (start us, length us, event | category | flops | bytes accessed | tf_op | source)
XLA Modules:
  0.0 102.9 jit_solution(17205392900884950122)
XLA Ops:
  0.0 1.9 %constant_dynamic-update-slice_fusion.1 = bf16[512,768]{1,0:T(8,128)(2,1)} fusion(bf16[256,768]{1,0:T(8,128)(2,1)} %param.14), kind=kLoop, calls=%fused_computation.119 | loop fusion | bytes 786432
  1.9 1.8 %constant_dynamic-update-slice_fusion.refs_0_.refs_9_ = bf16[512,768]{1,0:T(8,128)(2,1)} fusion(bf16[512,768]{1,0:T(8,128)(2,1)} %constant_dynamic-update-slice_fusion.1, bf16[256,768]{1,0:T(8,128)(2,1)} %param.15), kind=kLoop, calls=%fused_computation.118 | loop fusion | bytes 786432 | tf_op jit(solution)/shard_map/concatenate | solution.py:140
  3.7 3.8 %collective-permute-start = (bf16[512,768]{1,0:T(8,128)(2,1)}, bf16[512,768]{1,0:T(8,128)(2,1)}, u32[]{:S(2)}, u32[]{:S(2)}) collective-permute-start(bf16[512,768]{1,0:T(8,128)(2,1)} %constant_dynamic-update-slice_fusion.refs_0_.refs_9_), channel_id=1, source_target_pairs={{0,2},{1,3},{2,4},{3,5},{4,6},{5,7},{6,8},{7,9},{8,10},{9,11},{10,... | collective-permute-start | bytes 2359304 | tf_op jit(solution)/shard_map/ppermute | solution.py:16
  7.5 7.9 %collective-permute-start.1 = (bf16[512,768]{1,0:T(8,128)(2,1)}, bf16[512,768]{1,0:T(8,128)(2,1)}, u32[]{:S(2)}, u32[]{:S(2)}) collective-permute-start(bf16[512,768]{1,0:T(8,128)(2,1)} %constant_dynamic-update-slice_fusion.refs_0_.refs_9_), channel_id=1, source_target_pairs={{2,0},{3,1},{4,2},{5,3},{6,4},{7,5},{8,6},{9,7},{10,8},{11,9},{12,... | collective-permute-start | bytes 2359304 | tf_op jit(solution)/shard_map/ppermute | solution.py:16
  16.4 1.5 %convert_reduce_fusion.1 = s32[2304]{0:T(1024)S(1)} fusion(s32[128]{0:T(128)S(1)} %sub.49, s32[2304]{0:T(1024)S(1)} %add.220), kind=kLoop, calls=%fused_computation.107 | loop fusion | flops 882432 | bytes 18944 | tf_op jit(solution)/shard_map/reduce_sum | solution.py:33
  17.8 13.5 %collective-permute-done.refs_1_.refs_10_ = bf16[512,768]{1,0:T(8,128)(2,1)} collective-permute-done((bf16[512,768]{1,0:T(8,128)(2,1)}, bf16[512,768]{1,0:T(8,128)(2,1)}, u32[]{:S(2)}, u32[]{:S(2)}) %collective-permute-start) | collective-permute-done | bytes 786464 | tf_op jit(solution)/shard_map/ppermute | solution.py:16
  31.4 1.9 %collective-permute-start.2 = (bf16[512,768]{1,0:T(8,128)(2,1)}, bf16[512,768]{1,0:T(8,128)(2,1)S(1)}, u32[]{:S(2)}, u32[]{:S(2)}) collective-permute-start(bf16[512,768]{1,0:T(8,128)(2,1)} %collective-permute-done.refs_1_.refs_10_), channel_id=1, source_target_pairs={{0,2},{1,3},{2,4},{3,5},{4,6},{5,7},{6,8},{7,9},{8,10},{9,11},{10,... | collective-permute-start | bytes 2359304 | tf_op jit(solution)/shard_map/ppermute | solution.py:16
  33.3 8.1 %collective-permute-start.3 = (bf16[512,768]{1,0:T(8,128)(2,1)}, bf16[512,768]{1,0:T(8,128)(2,1)}, u32[]{:S(2)}, u32[]{:S(2)}) collective-permute-start(bf16[512,768]{1,0:T(8,128)(2,1)} %collective-permute-done.1.refs_2_.refs_11_), channel_id=1, source_target_pairs={{2,0},{3,1},{4,2},{5,3},{6,4},{7,5},{8,6},{9,7},{10,8},{11,9},{12,... | collective-permute-start | bytes 2359304 | tf_op jit(solution)/shard_map/ppermute | solution.py:16
  41.5 0.8 copy.17.recq_ref
  42.4 0.6 pad.4.reck_ref
  43.4 0.5 collective-permute-start.6
  43.9 12.5 %collective-permute-done.2.refs_3_.refs_12_ = bf16[512,768]{1,0:T(8,128)(2,1)S(1)} collective-permute-done((bf16[512,768]{1,0:T(8,128)(2,1)}, bf16[512,768]{1,0:T(8,128)(2,1)S(1)}, u32[]{:S(2)}, u32[]{:S(2)}) %collective-permute-start.2) | collective-permute-done | bytes 786464 | tf_op jit(solution)/shard_map/ppermute | solution.py:16
  56.4 1.3 %collective-permute-done.3.refs_4_.refs_13_ = bf16[512,768]{1,0:T(8,128)(2,1)} collective-permute-done((bf16[512,768]{1,0:T(8,128)(2,1)}, bf16[512,768]{1,0:T(8,128)(2,1)}, u32[]{:S(2)}, u32[]{:S(2)}) %collective-permute-start.3) | collective-permute-done | bytes 786464 | tf_op jit(solution)/shard_map/ppermute | solution.py:16
  57.7 1.2 %broadcast_select_fusion = bf16[512,768]{1,0:T(8,128)(2,1)S(1)} fusion(bf16[512,768]{1,0:T(8,128)(2,1)} %collective-permute-done.3.refs_4_.refs_13_, bf16[512,768]{1,0:T(8,128)(2,1)S(1)} %collective-permute-done.2.refs_3_.refs_12_, pred[]{:T(512)S(6)} %eq.102), kind=kLoop, calls=%fused_computation.109 | loop fusion | flops 393216 | bytes 2359297 | tf_op jit(solution)/shard_map/select_n | solution.py:147
  59.2 0.7 slice_compare_fusion.29
  59.9 0.7 slice_compare_fusion.30
  60.6 0.8 collective-permute-done.7.refs_8_.refs_17_
  61.4 15.6 %shard_map.118 = bf16[256,768]{1,0:T(8,128)(2,1)} custom-call(s32[256,1]{1,0:T(8,128)} %copy.17.recq_ref, s32[16,256]{1,0:T(8,128)} %pad.4.reck_ref, bf16[256,768]{1,0:T(8,128)(2,1)} %q_ref.1, bf16[512,768]{1,0:T(8,128)(2,1)} %constant_dynamic-update-slice_fusion.refs_0_.refs_9_, bf16[512,768]{1,0:T(8,128)(2,1)} %collective-permute-done.refs_1_.refs_10_, ...), custom_call_target="tpu_custom_call" | custom-call | tf_op jit(solution)/shard_map/pallas_call | solution.py:98
  77.0 2.0 %fusion.1 = bf16[256,1536]{1,0:T(8,128)(2,1)S(1)} fusion(bf16[256,768]{1,0:T(8,128)(2,1)} %shard_map.118, bf16[768,1536]{1,0:T(8,128)(2,1)S(1)} %copy-done, bf16[256,1536]{1,0:T(8,128)(2,1)} %param.12), kind=kOutput, calls=%fused_computation.3 | convolution fusion | flops 605159424 | bytes 4325376 | tf_op jit(solution)/shard_map/dot_general | solution.py:166
  79.8 0.4 fusion.7
  80.2 8.3 %collective-permute-start.8 = (bf16[15,1536]{1,0:T(8,128)(2,1)S(1)}, bf16[15,1536]{1,0:T(8,128)(2,1)S(1)}, u32[]{:S(2)}, u32[]{:S(2)}) collective-permute-start(bf16[15,1536]{1,0:T(8,128)(2,1)S(1)} %get-tuple-element.36), channel_id=1, source_target_pairs={{1,2},{3,4},{5,6},{7,8},{9,10},{11,12},{13,14},{15,16},{17,18},{19... | collective-permute-start | bytes 138248 | tf_op jit(solution)/shard_map/ppermute | solution.py:181
  89.0 1.3 %collective-permute-done.8 = bf16[15,1536]{1,0:T(8,128)(2,1)S(1)} collective-permute-done((bf16[15,1536]{1,0:T(8,128)(2,1)S(1)}, bf16[15,1536]{1,0:T(8,128)(2,1)S(1)}, u32[]{:S(2)}, u32[]{:S(2)}) %collective-permute-start.8) | collective-permute-done | bytes 46112 | tf_op jit(solution)/shard_map/ppermute | solution.py:181
  91.4 9.3 %multiply_convert_fusion = bf16[256,1536]{1,0:T(8,128)(2,1)S(1)} fusion(f32[286,1536]{1,0:T(8,128)S(1)} %convert_element_type.37, f32[1536]{0:T(1024)S(1)} %copy-done.5, f32[1536]{0:T(1024)S(1)} %copy-done.6, f32[1536]{0:T(1024)S(1)} %get-tuple-element.34, f32[1536]{0:T(1024)S(1)} %get-tuple-element.35, f32[1536]{0:T(1024)S(1)} %get-tuple-element.6, ...), kind=kLoop, calls=%fused_computation.106 | loop fusion | flops 38928384 | bytes 49755904 | tf_op jit(solution)/shard_map/convert_element_type | solution.py:203
  100.7 2.3 %fusion = bf16[256,1536]{1,0:T(8,128)(2,1)} fusion(bf16[256,1536]{1,0:T(8,128)(2,1)S(1)} %multiply_convert_fusion, bf16[1536,1536]{1,0:T(8,128)(2,1)S(1)} %bitcast.18, bf16[256,1536]{1,0:T(8,128)(2,1)S(1)} %fusion.1), kind=kOutput, calls=%fused_computation.2 | convolution fusion | flops 1209139200 | bytes 7077888 | tf_op jit(solution)/shard_map/dot_general | solution.py:204
  (94 shorter events, 3.7 us)
Async XLA Ops:
  0.0 77.0 %copy-start = (bf16[768,1536]{1,0:T(8,128)(2,1)S(1)}, bf16[768,1536]{1,0:T(8,128)(2,1)}, u32[]{:S(2)}) copy-start(bf16[768,1536]{1,0:T(8,128)(2,1)} %param.17) | copy-start | bytes 7077892
  0.0 15.8 %copy-start.25 = (s32[128]{0:T(128)S(1)}, s32[128]{0:T(128)}, u32[]{:S(2)}) copy-start(s32[128]{0:T(128)} %param.16) | copy-start | bytes 1540
  0.0 43.0 %copy-start.2 = (f32[31,1536]{1,0:T(8,128)S(1)}, f32[31,1536]{1,0:T(8,128)}, u32[]{:S(2)}) copy-start(f32[31,1536]{1,0:T(8,128)} %param.20) | copy-start | bytes 571396
  3.7 27.7 %collective-permute-start = (bf16[512,768]{1,0:T(8,128)(2,1)}, bf16[512,768]{1,0:T(8,128)(2,1)}, u32[]{:S(2)}, u32[]{:S(2)}) collective-permute-start(bf16[512,768]{1,0:T(8,128)(2,1)} %constant_dynamic-update-slice_fusion.refs_0_.refs_9_), channel_id=1, source_target_pairs={{0,2},{1,3},{2,4},{3,5},{4,6},{5,7},{6,8},{7,9},{8,10},{9,11},{10,... | collective-permute-start | bytes 2359304 | tf_op jit(solution)/shard_map/ppermute | solution.py:16
  7.5 25.8 %collective-permute-start.1 = (bf16[512,768]{1,0:T(8,128)(2,1)}, bf16[512,768]{1,0:T(8,128)(2,1)}, u32[]{:S(2)}, u32[]{:S(2)}) collective-permute-start(bf16[512,768]{1,0:T(8,128)(2,1)} %constant_dynamic-update-slice_fusion.refs_0_.refs_9_), channel_id=1, source_target_pairs={{2,0},{3,1},{4,2},{5,3},{6,4},{7,5},{8,6},{9,7},{10,8},{11,9},{12,... | collective-permute-start | bytes 2359304 | tf_op jit(solution)/shard_map/ppermute | solution.py:16
  15.5 45.1 %collective-permute-start.4 = (bf16[512,768]{1,0:T(8,128)(2,1)}, bf16[512,768]{1,0:T(8,128)(2,1)}, u32[]{:S(2)}, u32[]{:S(2)}) collective-permute-start(bf16[512,768]{1,0:T(8,128)(2,1)} %constant_dynamic-update-slice_fusion.refs_0_.refs_9_), channel_id=1, source_target_pairs={{0,1},{1,0},{2,3},{3,2},{4,5},{5,4},{6,7},{7,6},{8,9},{9,8},{10,11... | collective-permute-start | bytes 2359304 | tf_op jit(solution)/shard_map/ppermute | solution.py:150
  31.4 25.0 %collective-permute-start.2 = (bf16[512,768]{1,0:T(8,128)(2,1)}, bf16[512,768]{1,0:T(8,128)(2,1)S(1)}, u32[]{:S(2)}, u32[]{:S(2)}) collective-permute-start(bf16[512,768]{1,0:T(8,128)(2,1)} %collective-permute-done.refs_1_.refs_10_), channel_id=1, source_target_pairs={{0,2},{1,3},{2,4},{3,5},{4,6},{5,7},{6,8},{7,9},{8,10},{9,11},{10,... | collective-permute-start | bytes 2359304 | tf_op jit(solution)/shard_map/ppermute | solution.py:16
  33.3 24.4 %collective-permute-start.3 = (bf16[512,768]{1,0:T(8,128)(2,1)}, bf16[512,768]{1,0:T(8,128)(2,1)}, u32[]{:S(2)}, u32[]{:S(2)}) collective-permute-start(bf16[512,768]{1,0:T(8,128)(2,1)} %collective-permute-done.1.refs_2_.refs_11_), channel_id=1, source_target_pairs={{2,0},{3,1},{4,2},{5,3},{6,4},{7,5},{8,6},{9,7},{10,8},{11,9},{12,... | collective-permute-start | bytes 2359304 | tf_op jit(solution)/shard_map/ppermute | solution.py:16
  43.3 17.3 %collective-permute-start.5 = (bf16[512,768]{1,0:T(8,128)(2,1)}, bf16[512,768]{1,0:T(8,128)(2,1)}, u32[]{:S(2)}, u32[]{:S(2)}) collective-permute-start(bf16[512,768]{1,0:T(8,128)(2,1)} %collective-permute-done.refs_1_.refs_10_), channel_id=1, source_target_pairs={{0,1},{1,0},{2,3},{3,2},{4,5},{5,4},{6,7},{7,6},{8,9},{9,8},{10,11... | collective-permute-start | bytes 2359304 | tf_op jit(solution)/shard_map/ppermute | solution.py:150
  43.4 17.2 %collective-permute-start.6 = (bf16[512,768]{1,0:T(8,128)(2,1)}, bf16[512,768]{1,0:T(8,128)(2,1)}, u32[]{:S(2)}, u32[]{:S(2)}) collective-permute-start(bf16[512,768]{1,0:T(8,128)(2,1)} %collective-permute-done.1.refs_2_.refs_11_), channel_id=1, source_target_pairs={{0,1},{1,0},{2,3},{3,2},{4,5},{5,4},{6,7},{7,6},{8,9},{9,8},{10,11... | collective-permute-start | bytes 2359304 | tf_op jit(solution)/shard_map/ppermute | solution.py:150
  56.4 5.0 %copy-start.1 = (bf16[512,768]{1,0:T(8,128)(2,1)}, bf16[512,768]{1,0:T(8,128)(2,1)S(1)}, u32[]{:S(2)}) copy-start(bf16[512,768]{1,0:T(8,128)(2,1)S(1)} %collective-permute-done.2.refs_3_.refs_12_) | copy-start | bytes 2359300
  58.9 2.5 %collective-permute-start.7 = (bf16[512,768]{1,0:T(8,128)(2,1)S(1)}, bf16[512,768]{1,0:T(8,128)(2,1)}, u32[]{:S(2)}, u32[]{:S(2)}) collective-permute-start(bf16[512,768]{1,0:T(8,128)(2,1)S(1)} %broadcast_select_fusion), channel_id=1, source_target_pairs={{0,1},{1,0},{2,3},{3,2},{4,5},{5,4},{6,7},{7,6},{8,9},{9,8},{10,11... | collective-permute-start | bytes 2359304 | tf_op jit(solution)/shard_map/ppermute | solution.py:150
  79.0 0.7 copy-start.3
  79.0 0.7 copy-start.4
  80.2 10.1 %collective-permute-start.8 = (bf16[15,1536]{1,0:T(8,128)(2,1)S(1)}, bf16[15,1536]{1,0:T(8,128)(2,1)S(1)}, u32[]{:S(2)}, u32[]{:S(2)}) collective-permute-start(bf16[15,1536]{1,0:T(8,128)(2,1)S(1)} %get-tuple-element.36), channel_id=1, source_target_pairs={{1,2},{3,4},{5,6},{7,8},{9,10},{11,12},{13,14},{15,16},{17,18},{19... | collective-permute-start | bytes 138248 | tf_op jit(solution)/shard_map/ppermute | solution.py:181
  88.5 1.8 %collective-permute-start.9 = (bf16[15,1536]{1,0:T(8,128)(2,1)S(1)}, bf16[15,1536]{1,0:T(8,128)(2,1)S(1)}, u32[]{:S(2)}, u32[]{:S(2)}) collective-permute-start(bf16[15,1536]{1,0:T(8,128)(2,1)S(1)} %get-tuple-element.37), channel_id=1, source_target_pairs={{0,1},{1,0},{2,3},{3,2},{4,5},{5,4},{6,7},{7,6},{8,9},{9,8},{10,11... | collective-permute-start | bytes 138248 | tf_op jit(solution)/shard_map/ppermute | solution.py:184
  90.5 0.7 copy-start.5
  90.5 0.7 copy-start.6
  90.5 0.7 copy-start.7
  90.5 0.7 copy-start.8
  90.5 0.7 copy-start.9
  90.5 0.7 copy-start.10
  90.7 10.0 %slice-start = ((s8[4718592]{0:T(1024)(128)(4,1)}), s8[4194304]{0:T(1024)(128)(4,1)S(1)}, s32[]{:S(2)}) async-start(s8[4718592]{0:T(1024)(128)(4,1)} %bitcast.17), calls=%async_computation | async-start | bytes 8388608
  91.4 9.3 %slice-start.1 = ((s8[4718592]{0:T(1024)(128)(4,1)}), s8[524288]{0:T(1024)(128)(4,1)S(1)}, s32[]{:S(2)}) async-start(s8[4718592]{0:T(1024)(128)(4,1)} %bitcast.17), calls=%async_computation.1 | async-start | bytes 1048576
  (14 other events, 9.4 us)

commit v11 on v10

--- a/solution.py
+++ b/solution.py
@@ -111,6 +111,27 @@
     )(rec_q, rec_k, query, *keys, *vals)
 
 
+def stack_kernel(k_hbm, v_hbm, out_hbm, sems):
+    rows = k_hbm.shape[0]
+    first = pltpu.make_async_copy(k_hbm, out_hbm.at[pl.ds(0, rows)], sems.at[0])
+    second = pltpu.make_async_copy(v_hbm, out_hbm.at[pl.ds(rows, rows)], sems.at[1])
+    first.start()
+    second.start()
+    first.wait()
+    second.wait()
+
+
+def stack_rows(top, bottom):
+    rows, width = top.shape
+    return pl.pallas_call(
+        stack_kernel,
+        in_specs=[pl.BlockSpec(memory_space=pl.ANY)] * 2,
+        out_specs=pl.BlockSpec(memory_space=pl.ANY),
+        out_shape=jax.ShapeDtypeStruct((2 * rows, width), top.dtype),
+        scratch_shapes=[pltpu.SemaphoreType.DMA((2,))],
+    )(top, bottom)
+
+
 def shards(
     features,
     queries,
@@ -137,7 +158,7 @@
     def hop(pair, distance):
         return tuple(shifted_2(x, ("grp", "blk"), distance) for x in pair)
 
-    own_pair = (jnp.concatenate([key_vectors, values], axis=0),)
+    own_pair = (stack_rows(key_vectors, values),)
     from_m2 = hop(own_pair, 2)
     from_p2 = hop(own_pair, -2)
     from_m4 = hop(from_m2, 2)

time: 103 us -> 125 us (1.21)
  Pallas kernels: 15.6 us -> 40.5 us
  local copies, waits for them, and re-layouts: 6.36 us -> 2.67 us
    pallas_call x0 -> x1, Pallas kernels: none -> 24.9 us  [stack_rows(): pl.pallas_call(stack_kernel, in_specs=[pl.BlockSpec(memory_space=pl.ANY)]...]
    unnamed x57 -> x56, local copies, waits for them, and re-layouts: 2.47 us -> 0.55 us
    concatenate x1 -> x0, local copies, waits for them, and re-layouts: 1.77 us -> none  [shards(): own_pair = (jnp.concatenate([key_vectors, values], axis=0),)]
  transfers between devices with their start and end apart: 10 -> 10, of which waited for: 5 -> 5; matrix products, arithmetic and copies ran while one was open for 7% -> 6% of each run, Pallas kernels for 0% -> 0%
where the time goes in v11:
time: 125 us; the launch traced here: 124 us
  Pallas kernels  40.5 us (32%)
  starting transfers between devices  31.2 us (25%)
  waiting for transfers between devices  29.4 us (24%)
  other arithmetic  15.5 us (12%)
  matrix products  4.3 us (3%)
  local copies, waits for them, and re-layouts  2.67 us (2%)
    ppermute x4, waiting for transfers between devices, shifted_2(): return lax.ppermute(block, axis, route)  27.3 us
    pallas_call x1, Pallas kernels, stack_rows(): pl.pallas_call(stack_kernel, in_specs=[pl.BlockSpec(memory_space=pl.ANY)]...  24.9 us
    ppermute x4, starting transfers between devices, shifted_2(): return lax.ppermute(block, axis, route)  21.8 us
    pallas_call x1, Pallas kernels, attend(): pl.pallas_call(attend_kernel, grid=(width // pair,), in_specs=[pl.BlockSp...  15.5 us
    convert_element_type x1, other arithmetic, shards(): (shifted * jax.nn.sigmoid(shifted)).astype(jnp.bfloat16)  9.27 us
    ppermute x1, starting transfers between devices, shards(): lax.ppermute(lax.select(parity == 0, head_rows, tail_rows), ('grp', 'blk'...  8.35 us
  transfers between devices with their start and end apart: 10, of which 5 were waited for; matrix products, arithmetic and copies ran while one was open for 6% of the time, Pallas kernels for 0%

profile of v11, /device:TPU:16, one launch (start us, length us, event | category | flops | bytes accessed | tf_op | source)
XLA Modules:
  0.0 124.2 jit_solution(16240634147135339726)
XLA Ops:
  0.0 24.9 %shard_map.118.refs_0_.refs_9_ = bf16[512,768]{1,0:T(8,128)(2,1)} custom-call(bf16[256,768]{1,0:T(8,128)(2,1)} %k_hbm.1, bf16[256,768]{1,0:T(8,128)(2,1)} %v_hbm.1), custom_call_target="tpu_custom_call" | custom-call | tf_op jit(solution)/shard_map/pallas_call | solution.py:126
  25.0 3.8 %collective-permute-start = (bf16[512,768]{1,0:T(8,128)(2,1)}, bf16[512,768]{1,0:T(8,128)(2,1)}, u32[]{:S(2)}, u32[]{:S(2)}) collective-permute-start(bf16[512,768]{1,0:T(8,128)(2,1)} %shard_map.118.refs_0_.refs_9_), channel_id=1, source_target_pairs={{0,2},{1,3},{2,4},{3,5},{4,6},{5,7},{6,8},{7,9},{8,10},{9,11},{10,... | collective-permute-start | bytes 2359304 | tf_op jit(solution)/shard_map/ppermute | solution.py:16
  28.8 7.9 %collective-permute-start.1 = (bf16[512,768]{1,0:T(8,128)(2,1)}, bf16[512,768]{1,0:T(8,128)(2,1)}, u32[]{:S(2)}, u32[]{:S(2)}) collective-permute-start(bf16[512,768]{1,0:T(8,128)(2,1)} %shard_map.118.refs_0_.refs_9_), channel_id=1, source_target_pairs={{2,0},{3,1},{4,2},{5,3},{6,4},{7,5},{8,6},{9,7},{10,8},{11,9},{12,... | collective-permute-start | bytes 2359304 | tf_op jit(solution)/shard_map/ppermute | solution.py:16
  37.7 1.5 %convert_reduce_fusion.1 = s32[2304]{0:T(1024)S(1)} fusion(s32[128]{0:T(128)S(1)} %sub.49, s32[2304]{0:T(1024)S(1)} %add.220), kind=kLoop, calls=%fused_computation.107 | loop fusion | flops 882432 | bytes 18944 | tf_op jit(solution)/shard_map/reduce_sum | solution.py:33
  39.1 13.5 %collective-permute-done.refs_1_.refs_10_ = bf16[512,768]{1,0:T(8,128)(2,1)} collective-permute-done((bf16[512,768]{1,0:T(8,128)(2,1)}, bf16[512,768]{1,0:T(8,128)(2,1)}, u32[]{:S(2)}, u32[]{:S(2)}) %collective-permute-start) | collective-permute-done | bytes 786464 | tf_op jit(solution)/shard_map/ppermute | solution.py:16
  52.7 1.9 %collective-permute-start.2 = (bf16[512,768]{1,0:T(8,128)(2,1)}, bf16[512,768]{1,0:T(8,128)(2,1)S(1)}, u32[]{:S(2)}, u32[]{:S(2)}) collective-permute-start(bf16[512,768]{1,0:T(8,128)(2,1)} %collective-permute-done.refs_1_.refs_10_), channel_id=1, source_target_pairs={{0,2},{1,3},{2,4},{3,5},{4,6},{5,7},{6,8},{7,9},{8,10},{9,11},{10,... | collective-permute-start | bytes 2359304 | tf_op jit(solution)/shard_map/ppermute | solution.py:16
  54.6 8.1 %collective-permute-start.3 = (bf16[512,768]{1,0:T(8,128)(2,1)}, bf16[512,768]{1,0:T(8,128)(2,1)}, u32[]{:S(2)}, u32[]{:S(2)}) collective-permute-start(bf16[512,768]{1,0:T(8,128)(2,1)} %collective-permute-done.1.refs_2_.refs_11_), channel_id=1, source_target_pairs={{2,0},{3,1},{4,2},{5,3},{6,4},{7,5},{8,6},{9,7},{10,8},{11,9},{12,... | collective-permute-start | bytes 2359304 | tf_op jit(solution)/shard_map/ppermute | solution.py:16
  62.8 0.8 copy.17.recq_ref
  63.6 0.6 pad.4.reck_ref
  64.7 0.5 collective-permute-start.6
  65.2 12.5 %collective-permute-done.2.refs_3_.refs_12_ = bf16[512,768]{1,0:T(8,128)(2,1)S(1)} collective-permute-done((bf16[512,768]{1,0:T(8,128)(2,1)}, bf16[512,768]{1,0:T(8,128)(2,1)S(1)}, u32[]{:S(2)}, u32[]{:S(2)}) %collective-permute-start.2) | collective-permute-done | bytes 786464 | tf_op jit(solution)/shard_map/ppermute | solution.py:16
  77.7 1.3 %collective-permute-done.3.refs_4_.refs_13_ = bf16[512,768]{1,0:T(8,128)(2,1)} collective-permute-done((bf16[512,768]{1,0:T(8,128)(2,1)}, bf16[512,768]{1,0:T(8,128)(2,1)}, u32[]{:S(2)}, u32[]{:S(2)}) %collective-permute-start.3) | collective-permute-done | bytes 786464 | tf_op jit(solution)/shard_map/ppermute | solution.py:16
  79.0 1.2 broadcast_select_fusion
  80.5 0.7 slice_compare_fusion.29
  81.2 0.7 slice_compare_fusion.30
  81.9 0.8 collective-permute-done.7.refs_8_.refs_17_
  82.7 15.5 %shard_map.119 = bf16[256,768]{1,0:T(8,128)(2,1)} custom-call(s32[256,1]{1,0:T(8,128)} %copy.17.recq_ref, s32[16,256]{1,0:T(8,128)} %pad.4.reck_ref, bf16[256,768]{1,0:T(8,128)(2,1)} %q_ref.1, bf16[512,768]{1,0:T(8,128)(2,1)} %shard_map.118.refs_0_.refs_9_, bf16[512,768]{1,0:T(8,128)(2,1)} %collective-permute-done.refs_1_.refs_10_, ...), custom_call_target="tpu_custom_call" | custom-call | tf_op jit(solution)/shard_map/pallas_call | solution.py:98
  98.3 2.0 %fusion.1 = bf16[256,1536]{1,0:T(8,128)(2,1)S(1)} fusion(bf16[256,768]{1,0:T(8,128)(2,1)} %shard_map.119, bf16[768,1536]{1,0:T(8,128)(2,1)S(1)} %copy-done, bf16[256,1536]{1,0:T(8,128)(2,1)} %param.12), kind=kOutput, calls=%fused_computation.3 | convolution fusion | flops 605159424 | bytes 4325376 | tf_op jit(solution)/shard_map/dot_general | solution.py:187
  100.5 0.3 fusion.4
  101.0 0.4 fusion.7
  101.4 8.3 %collective-permute-start.8 = (bf16[15,1536]{1,0:T(8,128)(2,1)S(1)}, bf16[15,1536]{1,0:T(8,128)(2,1)S(1)}, u32[]{:S(2)}, u32[]{:S(2)}) collective-permute-start(bf16[15,1536]{1,0:T(8,128)(2,1)S(1)} %get-tuple-element.36), channel_id=1, source_target_pairs={{1,2},{3,4},{5,6},{7,8},{9,10},{11,12},{13,14},{15,16},{17,18},{19... | collective-permute-start | bytes 138248 | tf_op jit(solution)/shard_map/ppermute | solution.py:202
  110.3 1.3 %collective-permute-done.8 = bf16[15,1536]{1,0:T(8,128)(2,1)S(1)} collective-permute-done((bf16[15,1536]{1,0:T(8,128)(2,1)S(1)}, bf16[15,1536]{1,0:T(8,128)(2,1)S(1)}, u32[]{:S(2)}, u32[]{:S(2)}) %collective-permute-start.8) | collective-permute-done | bytes 46112 | tf_op jit(solution)/shard_map/ppermute | solution.py:202
  112.7 9.3 %multiply_convert_fusion = bf16[256,1536]{1,0:T(8,128)(2,1)S(1)} fusion(f32[286,1536]{1,0:T(8,128)S(1)} %convert_element_type.37, f32[1536]{0:T(1024)S(1)} %copy-done.5, f32[1536]{0:T(1024)S(1)} %copy-done.6, f32[1536]{0:T(1024)S(1)} %get-tuple-element.34, f32[1536]{0:T(1024)S(1)} %get-tuple-element.35, f32[1536]{0:T(1024)S(1)} %get-tuple-element.6, ...), kind=kLoop, calls=%fused_computation.106 | loop fusion | flops 38928384 | bytes 49755904 | tf_op jit(solution)/shard_map/convert_element_type | solution.py:224
  122.0 2.3 %fusion = bf16[256,1536]{1,0:T(8,128)(2,1)} fusion(bf16[256,1536]{1,0:T(8,128)(2,1)S(1)} %multiply_convert_fusion, bf16[1536,1536]{1,0:T(8,128)(2,1)S(1)} %bitcast.18, bf16[256,1536]{1,0:T(8,128)(2,1)S(1)} %fusion.1), kind=kOutput, calls=%fused_computation.2 | convolution fusion | flops 1209139200 | bytes 7077888 | tf_op jit(solution)/shard_map/dot_general | solution.py:225
  (93 shorter events, 3.3 us)
Async XLA Ops:
  0.0 98.3 %copy-start = (bf16[768,1536]{1,0:T(8,128)(2,1)S(1)}, bf16[768,1536]{1,0:T(8,128)(2,1)}, u32[]{:S(2)}) copy-start(bf16[768,1536]{1,0:T(8,128)(2,1)} %param.17) | copy-start | bytes 7077892
  0.0 37.0 %copy-start.25 = (s32[128]{0:T(128)S(1)}, s32[128]{0:T(128)}, u32[]{:S(2)}) copy-start(s32[128]{0:T(128)} %param.16) | copy-start | bytes 1540
  0.0 64.2 %copy-start.2 = (f32[31,1536]{1,0:T(8,128)S(1)}, f32[31,1536]{1,0:T(8,128)}, u32[]{:S(2)}) copy-start(f32[31,1536]{1,0:T(8,128)} %param.20) | copy-start | bytes 571396
  25.0 27.7 %collective-permute-start = (bf16[512,768]{1,0:T(8,128)(2,1)}, bf16[512,768]{1,0:T(8,128)(2,1)}, u32[]{:S(2)}, u32[]{:S(2)}) collective-permute-start(bf16[512,768]{1,0:T(8,128)(2,1)} %shard_map.118.refs_0_.refs_9_), channel_id=1, source_target_pairs={{0,2},{1,3},{2,4},{3,5},{4,6},{5,7},{6,8},{7,9},{8,10},{9,11},{10,... | collective-permute-start | bytes 2359304 | tf_op jit(solution)/shard_map/ppermute | solution.py:16
  28.8 25.8 %collective-permute-start.1 = (bf16[512,768]{1,0:T(8,128)(2,1)}, bf16[512,768]{1,0:T(8,128)(2,1)}, u32[]{:S(2)}, u32[]{:S(2)}) collective-permute-start(bf16[512,768]{1,0:T(8,128)(2,1)} %shard_map.118.refs_0_.refs_9_), channel_id=1, source_target_pairs={{2,0},{3,1},{4,2},{5,3},{6,4},{7,5},{8,6},{9,7},{10,8},{11,9},{12,... | collective-permute-start | bytes 2359304 | tf_op jit(solution)/shard_map/ppermute | solution.py:16
  36.7 45.1 %collective-permute-start.4 = (bf16[512,768]{1,0:T(8,128)(2,1)}, bf16[512,768]{1,0:T(8,128)(2,1)}, u32[]{:S(2)}, u32[]{:S(2)}) collective-permute-start(bf16[512,768]{1,0:T(8,128)(2,1)} %shard_map.118.refs_0_.refs_9_), channel_id=1, source_target_pairs={{0,1},{1,0},{2,3},{3,2},{4,5},{5,4},{6,7},{7,6},{8,9},{9,8},{10,11... | collective-permute-start | bytes 2359304 | tf_op jit(solution)/shard_map/ppermute | solution.py:171
  52.7 25.0 %collective-permute-start.2 = (bf16[512,768]{1,0:T(8,128)(2,1)}, bf16[512,768]{1,0:T(8,128)(2,1)S(1)}, u32[]{:S(2)}, u32[]{:S(2)}) collective-permute-start(bf16[512,768]{1,0:T(8,128)(2,1)} %collective-permute-done.refs_1_.refs_10_), channel_id=1, source_target_pairs={{0,2},{1,3},{2,4},{3,5},{4,6},{5,7},{6,8},{7,9},{8,10},{9,11},{10,... | collective-permute-start | bytes 2359304 | tf_op jit(solution)/shard_map/ppermute | solution.py:16
  54.6 24.4 %collective-permute-start.3 = (bf16[512,768]{1,0:T(8,128)(2,1)}, bf16[512,768]{1,0:T(8,128)(2,1)}, u32[]{:S(2)}, u32[]{:S(2)}) collective-permute-start(bf16[512,768]{1,0:T(8,128)(2,1)} %collective-permute-done.1.refs_2_.refs_11_), channel_id=1, source_target_pairs={{2,0},{3,1},{4,2},{5,3},{6,4},{7,5},{8,6},{9,7},{10,8},{11,9},{12,... | collective-permute-start | bytes 2359304 | tf_op jit(solution)/shard_map/ppermute | solution.py:16
  64.6 17.3 %collective-permute-start.5 = (bf16[512,768]{1,0:T(8,128)(2,1)}, bf16[512,768]{1,0:T(8,128)(2,1)}, u32[]{:S(2)}, u32[]{:S(2)}) collective-permute-start(bf16[512,768]{1,0:T(8,128)(2,1)} %collective-permute-done.refs_1_.refs_10_), channel_id=1, source_target_pairs={{0,1},{1,0},{2,3},{3,2},{4,5},{5,4},{6,7},{7,6},{8,9},{9,8},{10,11... | collective-permute-start | bytes 2359304 | tf_op jit(solution)/shard_map/ppermute | solution.py:171
  64.7 17.2 %collective-permute-start.6 = (bf16[512,768]{1,0:T(8,128)(2,1)}, bf16[512,768]{1,0:T(8,128)(2,1)}, u32[]{:S(2)}, u32[]{:S(2)}) collective-permute-start(bf16[512,768]{1,0:T(8,128)(2,1)} %collective-permute-done.1.refs_2_.refs_11_), channel_id=1, source_target_pairs={{0,1},{1,0},{2,3},{3,2},{4,5},{5,4},{6,7},{7,6},{8,9},{9,8},{10,11... | collective-permute-start | bytes 2359304 | tf_op jit(solution)/shard_map/ppermute | solution.py:171
  77.7 5.0 %copy-start.1 = (bf16[512,768]{1,0:T(8,128)(2,1)}, bf16[512,768]{1,0:T(8,128)(2,1)S(1)}, u32[]{:S(2)}) copy-start(bf16[512,768]{1,0:T(8,128)(2,1)S(1)} %collective-permute-done.2.refs_3_.refs_12_) | copy-start | bytes 2359300
  80.2 2.5 %collective-permute-start.7 = (bf16[512,768]{1,0:T(8,128)(2,1)S(1)}, bf16[512,768]{1,0:T(8,128)(2,1)}, u32[]{:S(2)}, u32[]{:S(2)}) collective-permute-start(bf16[512,768]{1,0:T(8,128)(2,1)S(1)} %broadcast_select_fusion), channel_id=1, source_target_pairs={{0,1},{1,0},{2,3},{3,2},{4,5},{5,4},{6,7},{7,6},{8,9},{9,8},{10,11... | collective-permute-start | bytes 2359304 | tf_op jit(solution)/shard_map/ppermute | solution.py:171
  100.3 0.7 copy-start.3
  100.3 0.7 copy-start.4
  101.4 10.1 %collective-permute-start.8 = (bf16[15,1536]{1,0:T(8,128)(2,1)S(1)}, bf16[15,1536]{1,0:T(8,128)(2,1)S(1)}, u32[]{:S(2)}, u32[]{:S(2)}) collective-permute-start(bf16[15,1536]{1,0:T(8,128)(2,1)S(1)} %get-tuple-element.36), channel_id=1, source_target_pairs={{1,2},{3,4},{5,6},{7,8},{9,10},{11,12},{13,14},{15,16},{17,18},{19... | collective-permute-start | bytes 138248 | tf_op jit(solution)/shard_map/ppermute | solution.py:202
  109.8 1.8 %collective-permute-start.9 = (bf16[15,1536]{1,0:T(8,128)(2,1)S(1)}, bf16[15,1536]{1,0:T(8,128)(2,1)S(1)}, u32[]{:S(2)}, u32[]{:S(2)}) collective-permute-start(bf16[15,1536]{1,0:T(8,128)(2,1)S(1)} %get-tuple-element.37), channel_id=1, source_target_pairs={{0,1},{1,0},{2,3},{3,2},{4,5},{5,4},{6,7},{7,6},{8,9},{9,8},{10,11... | collective-permute-start | bytes 138248 | tf_op jit(solution)/shard_map/ppermute | solution.py:205
  111.8 0.7 copy-start.5
  111.8 0.7 copy-start.6
  111.8 0.7 copy-start.7
  111.8 0.7 copy-start.8
  111.8 0.7 copy-start.9
  111.8 0.7 copy-start.10
  112.0 10.0 %slice-start = ((s8[4718592]{0:T(1024)(128)(4,1)}), s8[4194304]{0:T(1024)(128)(4,1)S(1)}, s32[]{:S(2)}) async-start(s8[4718592]{0:T(1024)(128)(4,1)} %bitcast.17), calls=%async_computation | async-start | bytes 8388608
  112.6 9.3 %slice-start.1 = ((s8[4718592]{0:T(1024)(128)(4,1)}), s8[524288]{0:T(1024)(128)(4,1)S(1)}, s32[]{:S(2)}) async-start(s8[4718592]{0:T(1024)(128)(4,1)} %bitcast.17), calls=%async_computation.1 | async-start | bytes 1048576
  (14 other events, 9.4 us)

commit v12 on v10

--- a/solution.py
+++ b/solution.py
@@ -52,11 +52,11 @@
     return out
 
 
-def attend_kernel(recq_ref, reck_ref, q_ref, *refs):
+def attend_kernel(recq_ref, reck_ref, q_ref, w_ref, feat_ref, *refs):
     k_refs = refs[:NBLK]
     v_refs = refs[NBLK : 2 * NBLK]
-    out_ref = refs[2 * NBLK]
-    s_scr, bias_scr = refs[2 * NBLK + 1 :]
+    resid_ref = refs[2 * NBLK]
+    s_scr, bias_scr, att_scr, proj_scr = refs[2 * NBLK + 1 :]
 
     @pl.when(pl.program_id(0) == 0)
     def _():
@@ -87,14 +87,30 @@
             wide_total = part if wide_total is None else wide_total + part
             acc = prod if acc is None else acc + prod
         total = jnp.sum(wide_total, axis=1, keepdims=True)
-        out_ref[:, cols] = (acc / total).astype(out_ref.dtype)
-
-
-def attend(rec_q, rec_k, query, keys, vals):
+        att_scr[:, cols] = (acc / total).astype(att_scr.dtype)
+
+    step = pl.program_id(0)
+    prod = jnp.dot(att_scr[...], w_ref[...], preferred_element_type=jnp.float32)
+
+    @pl.when(step == 0)
+    def _():
+        proj_scr[...] = prod
+
+    @pl.when(step > 0)
+    def _():
+        proj_scr[...] += prod
+
+    @pl.when(step == pl.num_programs(0) - 1)
+    def _():
+        resid_ref[...] = (feat_ref[...].astype(jnp.float32) + proj_scr[...]).astype(resid_ref.dtype)
+
+
+def attend(rec_q, rec_k, query, keys, vals, out_w, features):
     frames, width = query.shape
     pair = 4 * HD
     tile = pl.BlockSpec((frames, pair), lambda g: (0, g))
     v_tile = pl.BlockSpec((frames, pair), lambda g: (1, g))
+    whole = pl.BlockSpec(features.shape, lambda g: (0, 0))
     return pl.pallas_call(
         attend_kernel,
         grid=(width // pair,),
@@ -102,13 +118,16 @@
             pl.BlockSpec(rec_q.shape, lambda g: (0, 0)),
             pl.BlockSpec(rec_k.shape, lambda g: (0, 0)),
             tile,
+            pl.BlockSpec((pair, out_w.shape[1]), lambda g: (g, 0)),
+            whole,
         ]
         + [tile] * NBLK
         + [v_tile] * NBLK,
-        out_specs=tile,
-        out_shape=jax.ShapeDtypeStruct((frames, width), jnp.bfloat16),
-        scratch_shapes=[pltpu.VMEM((NBLK, frames, frames), jnp.float32)] * 2,
-    )(rec_q, rec_k, query, *keys, *vals)
+        out_specs=whole,
+        out_shape=jax.ShapeDtypeStruct(features.shape, jnp.bfloat16),
+        scratch_shapes=[pltpu.VMEM((NBLK, frames, frames), jnp.float32)] * 2
+        + [pltpu.VMEM((frames, pair), jnp.bfloat16), pltpu.VMEM(features.shape, jnp.float32)],
+    )(rec_q, rec_k, query, out_w, features, *keys, *vals)
 
 
 def shards(
@@ -162,10 +181,8 @@
     key_rec = jnp.pad(key_rec, ((0, rows - NBLK), (0, 0)), constant_values=-1)
     keys = [p[0] for p in pairs]
     vals = keys
-    attended = attend(own_rec[:, None], key_rec, queries, keys, vals)
-    projected = jnp.dot(attended, output_weight, preferred_element_type=jnp.float32)
     resid = lax.optimization_barrier(
-        (features.astype(jnp.float32) + projected).astype(jnp.bfloat16)
+        attend(own_rec[:, None], key_rec, queries, keys, vals, output_weight, features)
     )
     resid32 = resid.astype(jnp.float32)
     center = jnp.mean(resid32, axis=1, keepdims=True)

time: 103 us -> 104 us (level)
  Pallas kernels: 15.6 us -> 17.6 us
  matrix products: 4.3 us -> 2.3 us
  other arithmetic: 15.5 us -> 16.7 us
  waiting for transfers between devices: 29.4 us -> 28.3 us
    dot_general x1 -> x0, matrix products: 2.03 us -> none  [shards(): jnp.dot(attended, output_weight, preferred_element_type=jnp.float32)]
    pallas_call x1, Pallas kernels: 15.6 us -> 17.6 us  [attend(): pl.pallas_call(attend_kernel, grid=(width // pair,), in_specs=[pl.BlockSp...]
    reduce_sum x1, other arithmetic: 0.18 us -> 1.38 us  [shards(): center = jnp.mean(resid32, axis=1, keepdims=True)]
    select_n x1, other arithmetic: 1.22 us -> 0.08 us  [shards(): lax.select(parity == 0, p4, m4)]
    reduce_sum x1, other arithmetic: 0.35 us -> 1.48 us  [shards(): spread = jnp.mean((resid32 - center) ** 2, axis=1, keepdims=True)]
    unnamed x57 -> x67, local copies, waits for them, and re-layouts: 2.47 us -> 3.35 us
  transfers between devices with their start and end apart: 10 -> 10, of which waited for: 5 -> 4; matrix products, arithmetic and copies ran while one was open for 7% -> 6% of each run, Pallas kernels for 0% -> 0%
where the time goes in v12:
time: 104 us; the launch traced here: 103 us
  starting transfers between devices  31.5 us (30%)
  waiting for transfers between devices  28.3 us (27%)
  Pallas kernels  17.6 us (17%)
  other arithmetic  16.7 us (16%)
  local copies, waits for them, and re-layouts  6.48 us (6%)
  matrix products  2.3 us (2%)
    ppermute x4, waiting for transfers between devices, shifted_2(): return lax.ppermute(block, axis, route)  27 us
    ppermute x4, starting transfers between devices, shifted_2(): return lax.ppermute(block, axis, route)  21.8 us
    pallas_call x1, Pallas kernels, attend(): pl.pallas_call(attend_kernel, grid=(width // pair,), in_specs=[pl.BlockSp...  17.6 us
    convert_element_type x1, other arithmetic, shards(): (shifted * jax.nn.sigmoid(shifted)).astype(jnp.bfloat16)  9.25 us
    ppermute x1, starting transfers between devices, shards(): lax.ppermute(lax.select(parity == 0, head_rows, tail_rows), ('grp', 'blk'...  8.59 us
    unnamed x67, local copies, waits for them, and re-layouts  3.35 us
    dot_general x1, matrix products, shards(): jnp.dot(act, pointwise_weight, preferred_element_type=jnp.float32)  2.3 us
  transfers between devices with their start and end apart: 10, of which 4 were waited for; matrix products, arithmetic and copies ran while one was open for 6% of the time, Pallas kernels for 0%

profile of v12, /device:TPU:16, one launch (start us, length us, event | category | flops | bytes accessed | tf_op | source)
XLA Modules:
  0.0 103.5 jit_solution(16763210804900613960)
XLA Ops:
  0.0 1.1 %constant_dynamic-update-slice_fusion.1 = bf16[512,768]{1,0:T(8,128)(2,1)S(1)} fusion(bf16[256,768]{1,0:T(8,128)(2,1)} %param.14), kind=kLoop, calls=%fused_computation.117 | loop fusion | bytes 786432
  1.1 1.0 constant_dynamic-update-slice_fusion.refs_0_.refs_9_
  2.1 3.8 %collective-permute-start = (bf16[512,768]{1,0:T(8,128)(2,1)S(1)}, bf16[512,768]{1,0:T(8,128)(2,1)S(1)}, u32[]{:S(2)}, u32[]{:S(2)}) collective-permute-start(bf16[512,768]{1,0:T(8,128)(2,1)S(1)} %constant_dynamic-update-slice_fusion.refs_0_.refs_9_), channel_id=1, source_target_pairs={{0,2},{1,3},{2,4},{3,5},{4,6},{5,7},{6,8},{7,9},{8,10},{9,11},{10,... | collective-permute-start | bytes 2359304 | tf_op jit(solution)/shard_map/ppermute | solution.py:16
  5.9 7.9 %collective-permute-start.1 = (bf16[512,768]{1,0:T(8,128)(2,1)S(1)}, bf16[512,768]{1,0:T(8,128)(2,1)}, u32[]{:S(2)}, u32[]{:S(2)}) collective-permute-start(bf16[512,768]{1,0:T(8,128)(2,1)S(1)} %constant_dynamic-update-slice_fusion.refs_0_.refs_9_), channel_id=1, source_target_pairs={{2,0},{3,1},{4,2},{5,3},{6,4},{7,5},{8,6},{9,7},{10,8},{11,9},{12,... | collective-permute-start | bytes 2359304 | tf_op jit(solution)/shard_map/ppermute | solution.py:16
  14.8 1.5 %convert_reduce_fusion.1 = s32[2304]{0:T(1024)S(1)} fusion(s32[128]{0:T(128)S(1)} %sub.49, s32[2304]{0:T(1024)S(1)} %add.217), kind=kLoop, calls=%fused_computation.105 | loop fusion | flops 882432 | bytes 18944 | tf_op jit(solution)/shard_map/reduce_sum | solution.py:33
  16.3 13.2 %collective-permute-done.refs_1_.refs_10_ = bf16[512,768]{1,0:T(8,128)(2,1)S(1)} collective-permute-done((bf16[512,768]{1,0:T(8,128)(2,1)S(1)}, bf16[512,768]{1,0:T(8,128)(2,1)S(1)}, u32[]{:S(2)}, u32[]{:S(2)}) %collective-permute-start) | collective-permute-done | bytes 786464 | tf_op jit(solution)/shard_map/ppermute | solution.py:16
  29.5 1.9 %collective-permute-start.2 = (bf16[512,768]{1,0:T(8,128)(2,1)S(1)}, bf16[512,768]{1,0:T(8,128)(2,1)S(1)}, u32[]{:S(2)}, u32[]{:S(2)}) collective-permute-start(bf16[512,768]{1,0:T(8,128)(2,1)S(1)} %collective-permute-done.refs_1_.refs_10_), channel_id=1, source_target_pairs={{0,2},{1,3},{2,4},{3,5},{4,6},{5,7},{6,8},{7,9},{8,10},{9,11},{10,... | collective-permute-start | bytes 2359304 | tf_op jit(solution)/shard_map/ppermute | solution.py:16
  31.4 8.1 %collective-permute-start.3 = (bf16[512,768]{1,0:T(8,128)(2,1)}, bf16[512,768]{1,0:T(8,128)(2,1)S(1)}, u32[]{:S(2)}, u32[]{:S(2)}) collective-permute-start(bf16[512,768]{1,0:T(8,128)(2,1)} %collective-permute-done.1.refs_2_.refs_11_), channel_id=1, source_target_pairs={{2,0},{3,1},{4,2},{5,3},{6,4},{7,5},{8,6},{9,7},{10,8},{11,9},{12,... | collective-permute-start | bytes 2359304 | tf_op jit(solution)/shard_map/ppermute | solution.py:16
  39.6 0.8 copy.17.recq_ref
  40.5 0.6 pad.4.reck_ref
  41.5 0.5 collective-permute-start.6
  42.0 12.3 %collective-permute-done.2.refs_3_.refs_12_ = bf16[512,768]{1,0:T(8,128)(2,1)S(1)} collective-permute-done((bf16[512,768]{1,0:T(8,128)(2,1)S(1)}, bf16[512,768]{1,0:T(8,128)(2,1)S(1)}, u32[]{:S(2)}, u32[]{:S(2)}) %collective-permute-start.2) | collective-permute-done | bytes 786464 | tf_op jit(solution)/shard_map/ppermute | solution.py:16
  54.3 1.5 %collective-permute-done.3.refs_4_.refs_13_ = bf16[512,768]{1,0:T(8,128)(2,1)S(1)} collective-permute-done((bf16[512,768]{1,0:T(8,128)(2,1)}, bf16[512,768]{1,0:T(8,128)(2,1)S(1)}, u32[]{:S(2)}, u32[]{:S(2)}) %collective-permute-start.3) | collective-permute-done | bytes 786464 | tf_op jit(solution)/shard_map/ppermute | solution.py:16
  56.2 0.7 slice_compare_fusion.29
  56.9 0.7 slice_compare_fusion.30
  57.6 0.9 copy-done.5
  58.5 0.9 copy-done.6
  59.5 17.6 %shard_map.118 = bf16[256,1536]{1,0:T(8,128)(2,1)} custom-call(s32[256,1]{1,0:T(8,128)} %copy.17.recq_ref, s32[16,256]{1,0:T(8,128)} %pad.4.reck_ref, bf16[256,768]{1,0:T(8,128)(2,1)} %q_ref.1, bf16[768,1536]{1,0:T(8,128)(2,1)} %w_ref.1, bf16[256,1536]{1,0:T(8,128)(2,1)} %feat_ref.1, bf16[512,768]{1,0:T(8,128)(2,1)} %copy-done.3, ...), custom_call_target="tpu_custom_call" | custom-call | tf_op jit(solution)/shard_map/pallas_call | solution.py:114
  77.1 1.4 %convert_reduce_fusion = f32[256]{0:T(256)S(1)} fusion(bf16[256,1536]{1,0:T(8,128)(2,1)} %shard_map.118), kind=kLoop, calls=%fused_computation.3 | loop fusion | flops 786176 | bytes 787456 | tf_op jit(solution)/shard_map/reduce_sum | solution.py:188
  78.5 1.5 %fusion.3 = f32[256]{0:T(256)S(1)} fusion(bf16[256,1536]{1,0:T(8,128)(2,1)} %shard_map.118, f32[256]{0:T(256)S(1)} %broadcast_multiply_fusion), kind=kLoop, calls=%fused_computation.6 | loop fusion | flops 1572608 | bytes 788480 | tf_op jit(solution)/shard_map/reduce_sum | solution.py:189
  80.4 8.6 %collective-permute-start.8 = (bf16[15,1536]{1,0:T(8,128)(2,1)S(1)}, bf16[15,1536]{1,0:T(8,128)(2,1)S(1)}, u32[]{:S(2)}, u32[]{:S(2)}) collective-permute-start(bf16[15,1536]{1,0:T(8,128)(2,1)S(1)} %get-tuple-element.36), channel_id=1, source_target_pairs={{1,2},{3,4},{5,6},{7,8},{9,10},{11,12},{13,14},{15,16},{17,18},{19... | collective-permute-start | bytes 138248 | tf_op jit(solution)/shard_map/ppermute | solution.py:198
  89.5 1.3 %collective-permute-done.8 = bf16[15,1536]{1,0:T(8,128)(2,1)S(1)} collective-permute-done((bf16[15,1536]{1,0:T(8,128)(2,1)S(1)}, bf16[15,1536]{1,0:T(8,128)(2,1)S(1)}, u32[]{:S(2)}, u32[]{:S(2)}) %collective-permute-start.8) | collective-permute-done | bytes 46112 | tf_op jit(solution)/shard_map/ppermute | solution.py:198
  91.9 9.2 %multiply_convert_fusion = bf16[256,1536]{1,0:T(8,128)(2,1)S(1)} fusion(f32[286,1536]{1,0:T(8,128)S(1)} %convert_element_type.29, f32[1536]{0:T(1024)S(1)} %copy-done.10, f32[1536]{0:T(1024)S(1)} %copy-done.11, f32[1536]{0:T(1024)S(1)} %get-tuple-element.34, f32[1536]{0:T(1024)S(1)} %get-tuple-element.35, f32[1536]{0:T(1024)S(1)} %get-tuple-element.6, ...), kind=kLoop, calls=%fused_computation.104 | loop fusion | flops 38928384 | bytes 49755904 | tf_op jit(solution)/shard_map/convert_element_type | solution.py:220
  101.2 2.3 %fusion = bf16[256,1536]{1,0:T(8,128)(2,1)} fusion(bf16[256,1536]{1,0:T(8,128)(2,1)S(1)} %multiply_convert_fusion, bf16[1536,1536]{1,0:T(8,128)(2,1)S(1)} %bitcast.16, bf16[256,1536]{1,0:T(8,128)(2,1)S(1)} %copy-done), kind=kOutput, calls=%fused_computation.1 | convolution fusion | flops 1209139200 | bytes 7077888 | tf_op jit(solution)/shard_map/dot_general | solution.py:221
  (103 shorter events, 3.5 us)
Async XLA Ops:
  0.0 14.2 %copy-start.30 = (s32[128]{0:T(128)S(1)}, s32[128]{0:T(128)}, u32[]{:S(2)}) copy-start(s32[128]{0:T(128)} %param.16) | copy-start | bytes 1540
  0.0 41.1 %copy-start.7 = (f32[31,1536]{1,0:T(8,128)S(1)}, f32[31,1536]{1,0:T(8,128)}, u32[]{:S(2)}) copy-start(f32[31,1536]{1,0:T(8,128)} %param.20) | copy-start | bytes 571396
  2.1 53.8 %copy-start.3 = (bf16[512,768]{1,0:T(8,128)(2,1)}, bf16[512,768]{1,0:T(8,128)(2,1)S(1)}, u32[]{:S(2)}) copy-start(bf16[512,768]{1,0:T(8,128)(2,1)S(1)} %constant_dynamic-update-slice_fusion.refs_0_.refs_9_) | copy-start | bytes 2359300
  2.1 27.4 %collective-permute-start = (bf16[512,768]{1,0:T(8,128)(2,1)S(1)}, bf16[512,768]{1,0:T(8,128)(2,1)S(1)}, u32[]{:S(2)}, u32[]{:S(2)}) collective-permute-start(bf16[512,768]{1,0:T(8,128)(2,1)S(1)} %constant_dynamic-update-slice_fusion.refs_0_.refs_9_), channel_id=1, source_target_pairs={{0,2},{1,3},{2,4},{3,5},{4,6},{5,7},{6,8},{7,9},{8,10},{9,11},{10,... | collective-permute-start | bytes 2359304 | tf_op jit(solution)/shard_map/ppermute | solution.py:16
  5.9 25.5 %collective-permute-start.1 = (bf16[512,768]{1,0:T(8,128)(2,1)S(1)}, bf16[512,768]{1,0:T(8,128)(2,1)}, u32[]{:S(2)}, u32[]{:S(2)}) collective-permute-start(bf16[512,768]{1,0:T(8,128)(2,1)S(1)} %constant_dynamic-update-slice_fusion.refs_0_.refs_9_), channel_id=1, source_target_pairs={{2,0},{3,1},{4,2},{5,3},{6,4},{7,5},{8,6},{9,7},{10,8},{11,9},{12,... | collective-permute-start | bytes 2359304 | tf_op jit(solution)/shard_map/ppermute | solution.py:16
  13.9 43.7 %collective-permute-start.4 = (bf16[512,768]{1,0:T(8,128)(2,1)S(1)}, bf16[512,768]{1,0:T(8,128)(2,1)}, u32[]{:S(2)}, u32[]{:S(2)}) collective-permute-start(bf16[512,768]{1,0:T(8,128)(2,1)S(1)} %constant_dynamic-update-slice_fusion.refs_0_.refs_9_), channel_id=1, source_target_pairs={{0,1},{1,0},{2,3},{3,2},{4,5},{5,4},{6,7},{7,6},{8,9},{9,8},{10,11... | collective-permute-start | bytes 2359304 | tf_op jit(solution)/shard_map/ppermute | solution.py:169
  29.5 30.0 %copy-start.4 = (bf16[512,768]{1,0:T(8,128)(2,1)}, bf16[512,768]{1,0:T(8,128)(2,1)S(1)}, u32[]{:S(2)}) copy-start(bf16[512,768]{1,0:T(8,128)(2,1)S(1)} %collective-permute-done.refs_1_.refs_10_) | copy-start | bytes 2359300
  29.5 24.8 %collective-permute-start.2 = (bf16[512,768]{1,0:T(8,128)(2,1)S(1)}, bf16[512,768]{1,0:T(8,128)(2,1)S(1)}, u32[]{:S(2)}, u32[]{:S(2)}) collective-permute-start(bf16[512,768]{1,0:T(8,128)(2,1)S(1)} %collective-permute-done.refs_1_.refs_10_), channel_id=1, source_target_pairs={{0,2},{1,3},{2,4},{3,5},{4,6},{5,7},{6,8},{7,9},{8,10},{9,11},{10,... | collective-permute-start | bytes 2359304 | tf_op jit(solution)/shard_map/ppermute | solution.py:16
  31.4 24.4 %collective-permute-start.3 = (bf16[512,768]{1,0:T(8,128)(2,1)}, bf16[512,768]{1,0:T(8,128)(2,1)S(1)}, u32[]{:S(2)}, u32[]{:S(2)}) collective-permute-start(bf16[512,768]{1,0:T(8,128)(2,1)} %collective-permute-done.1.refs_2_.refs_11_), channel_id=1, source_target_pairs={{2,0},{3,1},{4,2},{5,3},{6,4},{7,5},{8,6},{9,7},{10,8},{11,9},{12,... | collective-permute-start | bytes 2359304 | tf_op jit(solution)/shard_map/ppermute | solution.py:16
  41.4 16.2 %collective-permute-start.5 = (bf16[512,768]{1,0:T(8,128)(2,1)S(1)}, bf16[512,768]{1,0:T(8,128)(2,1)S(1)}, u32[]{:S(2)}, u32[]{:S(2)}) collective-permute-start(bf16[512,768]{1,0:T(8,128)(2,1)S(1)} %collective-permute-done.refs_1_.refs_10_), channel_id=1, source_target_pairs={{0,1},{1,0},{2,3},{3,2},{4,5},{5,4},{6,7},{7,6},{8,9},{9,8},{10,11... | collective-permute-start | bytes 2359304 | tf_op jit(solution)/shard_map/ppermute | solution.py:169
  41.5 17.0 %collective-permute-start.6 = (bf16[512,768]{1,0:T(8,128)(2,1)}, bf16[512,768]{1,0:T(8,128)(2,1)S(1)}, u32[]{:S(2)}, u32[]{:S(2)}) collective-permute-start(bf16[512,768]{1,0:T(8,128)(2,1)} %collective-permute-done.1.refs_2_.refs_11_), channel_id=1, source_target_pairs={{0,1},{1,0},{2,3},{3,2},{4,5},{5,4},{6,7},{7,6},{8,9},{9,8},{10,11... | collective-permute-start | bytes 2359304 | tf_op jit(solution)/shard_map/ppermute | solution.py:169
  54.3 5.2 %copy-start.1 = (bf16[512,768]{1,0:T(8,128)(2,1)}, bf16[512,768]{1,0:T(8,128)(2,1)S(1)}, u32[]{:S(2)}) copy-start(bf16[512,768]{1,0:T(8,128)(2,1)S(1)} %collective-permute-done.2.refs_3_.refs_12_) | copy-start | bytes 2359300
  55.8 3.7 %copy-start.2 = (bf16[512,768]{1,0:T(8,128)(2,1)}, bf16[512,768]{1,0:T(8,128)(2,1)S(1)}, u32[]{:S(2)}) copy-start(bf16[512,768]{1,0:T(8,128)(2,1)S(1)} %collective-permute-done.3.refs_4_.refs_13_) | copy-start | bytes 2359300
  55.9 3.5 %collective-permute-start.7 = (bf16[512,768]{1,0:T(8,128)(2,1)S(1)}, bf16[512,768]{1,0:T(8,128)(2,1)}, u32[]{:S(2)}, u32[]{:S(2)}) collective-permute-start(bf16[512,768]{1,0:T(8,128)(2,1)S(1)} %broadcast_select_fusion), channel_id=1, source_target_pairs={{0,1},{1,0},{2,3},{3,2},{4,5},{5,4},{6,7},{7,6},{8,9},{9,8},{10,11... | collective-permute-start | bytes 2359304 | tf_op jit(solution)/shard_map/ppermute | solution.py:169
  57.6 0.9 copy-start.5
  58.5 0.9 copy-start.6
  77.0 2.9 %copy-start = (bf16[256,1536]{1,0:T(8,128)(2,1)S(1)}, bf16[256,1536]{1,0:T(8,128)(2,1)}, u32[]{:S(2)}) copy-start(bf16[256,1536]{1,0:T(8,128)(2,1)} %shard_map.118) | copy-start | bytes 2359300
  77.1 2.9 %copy-start.8 = (f32[1536]{0:T(1024)S(1)}, f32[1536]{0:T(1024)}, u32[]{:S(2)}) copy-start(f32[1536]{0:T(1024)} %param.19) | copy-start | bytes 18436
  77.1 2.9 %copy-start.9 = (f32[1536]{0:T(1024)S(1)}, f32[1536]{0:T(1024)}, u32[]{:S(2)}) copy-start(f32[1536]{0:T(1024)} %param.18) | copy-start | bytes 18436
  80.4 10.4 %collective-permute-start.8 = (bf16[15,1536]{1,0:T(8,128)(2,1)S(1)}, bf16[15,1536]{1,0:T(8,128)(2,1)S(1)}, u32[]{:S(2)}, u32[]{:S(2)}) collective-permute-start(bf16[15,1536]{1,0:T(8,128)(2,1)S(1)} %get-tuple-element.36), channel_id=1, source_target_pairs={{1,2},{3,4},{5,6},{7,8},{9,10},{11,12},{13,14},{15,16},{17,18},{19... | collective-permute-start | bytes 138248 | tf_op jit(solution)/shard_map/ppermute | solution.py:198
  89.0 1.8 %collective-permute-start.9 = (bf16[15,1536]{1,0:T(8,128)(2,1)S(1)}, bf16[15,1536]{1,0:T(8,128)(2,1)S(1)}, u32[]{:S(2)}, u32[]{:S(2)}) collective-permute-start(bf16[15,1536]{1,0:T(8,128)(2,1)S(1)} %get-tuple-element.37), channel_id=1, source_target_pairs={{0,1},{1,0},{2,3},{3,2},{4,5},{5,4},{6,7},{7,6},{8,9},{9,8},{10,11... | collective-permute-start | bytes 138248 | tf_op jit(solution)/shard_map/ppermute | solution.py:201
  91.0 0.7 copy-start.11
  91.2 9.9 %slice-start = ((s8[4718592]{0:T(1024)(128)(4,1)}), s8[4194304]{0:T(1024)(128)(4,1)S(1)}, s32[]{:S(2)}) async-start(s8[4718592]{0:T(1024)(128)(4,1)} %bitcast.15), calls=%async_computation | async-start | bytes 8388608
  91.9 9.3 %slice-start.1 = ((s8[4718592]{0:T(1024)(128)(4,1)}), s8[524288]{0:T(1024)(128)(4,1)S(1)}, s32[]{:S(2)}) async-start(s8[4718592]{0:T(1024)(128)(4,1)} %bitcast.15), calls=%async_computation.1 | async-start | bytes 1048576
  (19 other events, 12.8 us)

commit v13 on v10

--- a/solution.py
+++ b/solution.py
@@ -137,7 +137,14 @@
     def hop(pair, distance):
         return tuple(shifted_2(x, ("grp", "blk"), distance) for x in pair)
 
-    own_pair = (jnp.concatenate([key_vectors, values], axis=0),)
+    stacked_rows = lax.broadcasted_iota(jnp.int32, (2 * frames, 1), 0)
+    own_pair = (
+        jnp.where(
+            stacked_rows < frames,
+            jnp.pad(key_vectors, ((0, frames), (0, 0))),
+            jnp.pad(values, ((frames, 0), (0, 0))),
+        ),
+    )
     from_m2 = hop(own_pair, 2)
     from_p2 = hop(own_pair, -2)
     from_m4 = hop(from_m2, 2)

time: 103 us -> 102 us (level)
  local copies, waits for them, and re-layouts: 6.36 us -> 2.67 us
  other arithmetic: 15.5 us -> 17.9 us
    select_n x0 -> x1, other arithmetic: none -> 2.35 us  [shards(): jnp.where(stacked_rows < frames, jnp.pad(key_vectors, ((0, frames), (0, 0...]
    unnamed x57 -> x56, local copies, waits for them, and re-layouts: 2.47 us -> 0.55 us
    concatenate x1 -> x0, local copies, waits for them, and re-layouts: 1.77 us -> none  [shards(): own_pair = (jnp.concatenate([key_vectors, values], axis=0),)]
where the time goes in v13:
time: 102 us
  starting transfers between devices  31.2 us (31%)
  waiting for transfers between devices  29.4 us (29%)
  other arithmetic  17.9 us (18%)
  Pallas kernels  15.5 us (15%)
  matrix products  4.3 us (4%)
  local copies, waits for them, and re-layouts  2.67 us (3%)
    ppermute x4, waiting for transfers between devices, shifted_2(): return lax.ppermute(block, axis, route)  27.3 us
    ppermute x4, starting transfers between devices, shifted_2(): return lax.ppermute(block, axis, route)  21.8 us
    pallas_call x1, Pallas kernels, attend(): pl.pallas_call(attend_kernel, grid=(width // pair,), in_specs=[pl.BlockSp...  15.5 us
    convert_element_type x1, other arithmetic, shards(): (shifted * jax.nn.sigmoid(shifted)).astype(jnp.bfloat16)  9.27 us
    ppermute x1, starting transfers between devices, shards(): lax.ppermute(lax.select(parity == 0, head_rows, tail_rows), ('grp', 'blk'...  8.37 us
    select_n x1, other arithmetic, shards(): jnp.where(stacked_rows < frames, jnp.pad(key_vectors, ((0, frames), (0, 0...  2.35 us
    dot_general x1, matrix products, shards(): jnp.dot(act, pointwise_weight, preferred_element_type=jnp.float32)  2.27 us
  transfers between devices with their start and end apart: 10, of which 5 were waited for; matrix products, arithmetic and copies ran while one was open for 7% of the time, Pallas kernels for 0%

profile of v13, /device:TPU:16, one launch (start us, length us, event | category | flops | bytes accessed | tf_op | source)
XLA Modules:
  0.0 101.6 jit_solution(6060937872049269722)
XLA Ops:
  0.0 2.4 %pad_select_fusion.refs_0_.refs_9_ = bf16[512,768]{1,0:T(8,128)(2,1)} fusion(bf16[256,768]{1,0:T(8,128)(2,1)} %param.15, bf16[256,768]{1,0:T(8,128)(2,1)} %param.14, pred[512]{0:T(512)(128)(4,1)S(1)} %iota_compare_fusion), kind=kLoop, calls=%fused_computation.109 | loop fusion | flops 393216 | bytes 1573376 | tf_op jit(solution)/shard_map/jit(_where)/select_n | solution.py:142
  2.4 3.8 %collective-permute-start = (bf16[512,768]{1,0:T(8,128)(2,1)}, bf16[512,768]{1,0:T(8,128)(2,1)}, u32[]{:S(2)}, u32[]{:S(2)}) collective-permute-start(bf16[512,768]{1,0:T(8,128)(2,1)} %pad_select_fusion.refs_0_.refs_9_), channel_id=1, source_target_pairs={{0,2},{1,3},{2,4},{3,5},{4,6},{5,7},{6,8},{7,9},{8,10},{9,11},{10,... | collective-permute-start | bytes 2359304 | tf_op jit(solution)/shard_map/ppermute | solution.py:16
  6.2 7.9 %collective-permute-start.1 = (bf16[512,768]{1,0:T(8,128)(2,1)}, bf16[512,768]{1,0:T(8,128)(2,1)}, u32[]{:S(2)}, u32[]{:S(2)}) collective-permute-start(bf16[512,768]{1,0:T(8,128)(2,1)} %pad_select_fusion.refs_0_.refs_9_), channel_id=1, source_target_pairs={{2,0},{3,1},{4,2},{5,3},{6,4},{7,5},{8,6},{9,7},{10,8},{11,9},{12,... | collective-permute-start | bytes 2359304 | tf_op jit(solution)/shard_map/ppermute | solution.py:16
  15.0 1.5 %convert_reduce_fusion.1 = s32[2304]{0:T(1024)S(1)} fusion(s32[128]{0:T(128)S(1)} %sub.49, s32[2304]{0:T(1024)S(1)} %add.224), kind=kLoop, calls=%fused_computation.107 | loop fusion | flops 882432 | bytes 18944 | tf_op jit(solution)/shard_map/reduce_sum | solution.py:33
  16.5 13.5 %collective-permute-done.refs_1_.refs_10_ = bf16[512,768]{1,0:T(8,128)(2,1)} collective-permute-done((bf16[512,768]{1,0:T(8,128)(2,1)}, bf16[512,768]{1,0:T(8,128)(2,1)}, u32[]{:S(2)}, u32[]{:S(2)}) %collective-permute-start) | collective-permute-done | bytes 786464 | tf_op jit(solution)/shard_map/ppermute | solution.py:16
  30.1 1.9 %collective-permute-start.2 = (bf16[512,768]{1,0:T(8,128)(2,1)}, bf16[512,768]{1,0:T(8,128)(2,1)S(1)}, u32[]{:S(2)}, u32[]{:S(2)}) collective-permute-start(bf16[512,768]{1,0:T(8,128)(2,1)} %collective-permute-done.refs_1_.refs_10_), channel_id=1, source_target_pairs={{0,2},{1,3},{2,4},{3,5},{4,6},{5,7},{6,8},{7,9},{8,10},{9,11},{10,... | collective-permute-start | bytes 2359304 | tf_op jit(solution)/shard_map/ppermute | solution.py:16
  32.0 8.1 %collective-permute-start.3 = (bf16[512,768]{1,0:T(8,128)(2,1)}, bf16[512,768]{1,0:T(8,128)(2,1)}, u32[]{:S(2)}, u32[]{:S(2)}) collective-permute-start(bf16[512,768]{1,0:T(8,128)(2,1)} %collective-permute-done.1.refs_2_.refs_11_), channel_id=1, source_target_pairs={{2,0},{3,1},{4,2},{5,3},{6,4},{7,5},{8,6},{9,7},{10,8},{11,9},{12,... | collective-permute-start | bytes 2359304 | tf_op jit(solution)/shard_map/ppermute | solution.py:16
  40.2 0.8 copy.17.recq_ref
  41.0 0.6 pad.12.reck_ref
  42.1 0.5 collective-permute-start.6
  42.6 12.5 %collective-permute-done.2.refs_3_.refs_12_ = bf16[512,768]{1,0:T(8,128)(2,1)S(1)} collective-permute-done((bf16[512,768]{1,0:T(8,128)(2,1)}, bf16[512,768]{1,0:T(8,128)(2,1)S(1)}, u32[]{:S(2)}, u32[]{:S(2)}) %collective-permute-start.2) | collective-permute-done | bytes 786464 | tf_op jit(solution)/shard_map/ppermute | solution.py:16
  55.1 1.3 %collective-permute-done.3.refs_4_.refs_13_ = bf16[512,768]{1,0:T(8,128)(2,1)} collective-permute-done((bf16[512,768]{1,0:T(8,128)(2,1)}, bf16[512,768]{1,0:T(8,128)(2,1)}, u32[]{:S(2)}, u32[]{:S(2)}) %collective-permute-start.3) | collective-permute-done | bytes 786464 | tf_op jit(solution)/shard_map/ppermute | solution.py:16
  56.4 1.2 %broadcast_select_fusion = bf16[512,768]{1,0:T(8,128)(2,1)S(1)} fusion(bf16[512,768]{1,0:T(8,128)(2,1)} %collective-permute-done.3.refs_4_.refs_13_, bf16[512,768]{1,0:T(8,128)(2,1)S(1)} %collective-permute-done.2.refs_3_.refs_12_, pred[]{:T(512)S(6)} %eq.102), kind=kLoop, calls=%fused_computation.110 | loop fusion | flops 393216 | bytes 2359297 | tf_op jit(solution)/shard_map/select_n | solution.py:154
  57.9 0.7 slice_compare_fusion.29
  58.6 0.7 slice_compare_fusion.30
  59.3 0.8 collective-permute-done.7.refs_8_.refs_17_
  60.1 15.5 %shard_map.118 = bf16[256,768]{1,0:T(8,128)(2,1)} custom-call(s32[256,1]{1,0:T(8,128)} %copy.17.recq_ref, s32[16,256]{1,0:T(8,128)} %pad.12.reck_ref, bf16[256,768]{1,0:T(8,128)(2,1)} %q_ref.1, bf16[512,768]{1,0:T(8,128)(2,1)} %pad_select_fusion.refs_0_.refs_9_, bf16[512,768]{1,0:T(8,128)(2,1)} %collective-permute-done.refs_1_.refs_10_, ...), custom_call_target="tpu_custom_call" | custom-call | tf_op jit(solution)/shard_map/pallas_call | solution.py:98
  75.7 2.0 %fusion.1 = bf16[256,1536]{1,0:T(8,128)(2,1)S(1)} fusion(bf16[256,768]{1,0:T(8,128)(2,1)} %shard_map.118, bf16[768,1536]{1,0:T(8,128)(2,1)S(1)} %copy-done, bf16[256,1536]{1,0:T(8,128)(2,1)} %param.12), kind=kOutput, calls=%fused_computation.3 | convolution fusion | flops 605159424 | bytes 4325376 | tf_op jit(solution)/shard_map/dot_general | solution.py:173
  77.9 0.3 fusion.4
  78.4 0.4 fusion.7
  78.8 8.4 %collective-permute-start.8 = (bf16[15,1536]{1,0:T(8,128)(2,1)S(1)}, bf16[15,1536]{1,0:T(8,128)(2,1)S(1)}, u32[]{:S(2)}, u32[]{:S(2)}) collective-permute-start(bf16[15,1536]{1,0:T(8,128)(2,1)S(1)} %get-tuple-element.36), channel_id=1, source_target_pairs={{1,2},{3,4},{5,6},{7,8},{9,10},{11,12},{13,14},{15,16},{17,18},{19... | collective-permute-start | bytes 138248 | tf_op jit(solution)/shard_map/ppermute | solution.py:188
  87.7 1.3 %collective-permute-done.8 = bf16[15,1536]{1,0:T(8,128)(2,1)S(1)} collective-permute-done((bf16[15,1536]{1,0:T(8,128)(2,1)S(1)}, bf16[15,1536]{1,0:T(8,128)(2,1)S(1)}, u32[]{:S(2)}, u32[]{:S(2)}) %collective-permute-start.8) | collective-permute-done | bytes 46112 | tf_op jit(solution)/shard_map/ppermute | solution.py:188
  90.1 9.3 %multiply_convert_fusion = bf16[256,1536]{1,0:T(8,128)(2,1)S(1)} fusion(f32[286,1536]{1,0:T(8,128)S(1)} %convert_element_type.41, f32[1536]{0:T(1024)S(1)} %copy-done.5, f32[1536]{0:T(1024)S(1)} %copy-done.6, f32[1536]{0:T(1024)S(1)} %get-tuple-element.34, f32[1536]{0:T(1024)S(1)} %get-tuple-element.35, f32[1536]{0:T(1024)S(1)} %get-tuple-element.6, ...), kind=kLoop, calls=%fused_computation.106 | loop fusion | flops 38928384 | bytes 49755904 | tf_op jit(solution)/shard_map/convert_element_type | solution.py:210
  99.4 2.3 %fusion = bf16[256,1536]{1,0:T(8,128)(2,1)} fusion(bf16[256,1536]{1,0:T(8,128)(2,1)S(1)} %multiply_convert_fusion, bf16[1536,1536]{1,0:T(8,128)(2,1)S(1)} %bitcast.18, bf16[256,1536]{1,0:T(8,128)(2,1)S(1)} %fusion.1), kind=kOutput, calls=%fused_computation.2 | convolution fusion | flops 1209139200 | bytes 7077888 | tf_op jit(solution)/shard_map/dot_general | solution.py:211
  (94 shorter events, 3.3 us)
Async XLA Ops:
  0.0 75.7 %copy-start = (bf16[768,1536]{1,0:T(8,128)(2,1)S(1)}, bf16[768,1536]{1,0:T(8,128)(2,1)}, u32[]{:S(2)}) copy-start(bf16[768,1536]{1,0:T(8,128)(2,1)} %param.17) | copy-start | bytes 7077892
  0.0 14.4 %copy-start.25 = (s32[128]{0:T(128)S(1)}, s32[128]{0:T(128)}, u32[]{:S(2)}) copy-start(s32[128]{0:T(128)} %param.16) | copy-start | bytes 1540
  0.0 41.7 %copy-start.2 = (f32[31,1536]{1,0:T(8,128)S(1)}, f32[31,1536]{1,0:T(8,128)}, u32[]{:S(2)}) copy-start(f32[31,1536]{1,0:T(8,128)} %param.20) | copy-start | bytes 571396
  2.4 27.7 %collective-permute-start = (bf16[512,768]{1,0:T(8,128)(2,1)}, bf16[512,768]{1,0:T(8,128)(2,1)}, u32[]{:S(2)}, u32[]{:S(2)}) collective-permute-start(bf16[512,768]{1,0:T(8,128)(2,1)} %pad_select_fusion.refs_0_.refs_9_), channel_id=1, source_target_pairs={{0,2},{1,3},{2,4},{3,5},{4,6},{5,7},{6,8},{7,9},{8,10},{9,11},{10,... | collective-permute-start | bytes 2359304 | tf_op jit(solution)/shard_map/ppermute | solution.py:16
  6.2 25.8 %collective-permute-start.1 = (bf16[512,768]{1,0:T(8,128)(2,1)}, bf16[512,768]{1,0:T(8,128)(2,1)}, u32[]{:S(2)}, u32[]{:S(2)}) collective-permute-start(bf16[512,768]{1,0:T(8,128)(2,1)} %pad_select_fusion.refs_0_.refs_9_), channel_id=1, source_target_pairs={{2,0},{3,1},{4,2},{5,3},{6,4},{7,5},{8,6},{9,7},{10,8},{11,9},{12,... | collective-permute-start | bytes 2359304 | tf_op jit(solution)/shard_map/ppermute | solution.py:16
  14.1 45.1 %collective-permute-start.4 = (bf16[512,768]{1,0:T(8,128)(2,1)}, bf16[512,768]{1,0:T(8,128)(2,1)}, u32[]{:S(2)}, u32[]{:S(2)}) collective-permute-start(bf16[512,768]{1,0:T(8,128)(2,1)} %pad_select_fusion.refs_0_.refs_9_), channel_id=1, source_target_pairs={{0,1},{1,0},{2,3},{3,2},{4,5},{5,4},{6,7},{7,6},{8,9},{9,8},{10,11... | collective-permute-start | bytes 2359304 | tf_op jit(solution)/shard_map/ppermute | solution.py:157
  30.1 25.0 %collective-permute-start.2 = (bf16[512,768]{1,0:T(8,128)(2,1)}, bf16[512,768]{1,0:T(8,128)(2,1)S(1)}, u32[]{:S(2)}, u32[]{:S(2)}) collective-permute-start(bf16[512,768]{1,0:T(8,128)(2,1)} %collective-permute-done.refs_1_.refs_10_), channel_id=1, source_target_pairs={{0,2},{1,3},{2,4},{3,5},{4,6},{5,7},{6,8},{7,9},{8,10},{9,11},{10,... | collective-permute-start | bytes 2359304 | tf_op jit(solution)/shard_map/ppermute | solution.py:16
  32.0 24.4 %collective-permute-start.3 = (bf16[512,768]{1,0:T(8,128)(2,1)}, bf16[512,768]{1,0:T(8,128)(2,1)}, u32[]{:S(2)}, u32[]{:S(2)}) collective-permute-start(bf16[512,768]{1,0:T(8,128)(2,1)} %collective-permute-done.1.refs_2_.refs_11_), channel_id=1, source_target_pairs={{2,0},{3,1},{4,2},{5,3},{6,4},{7,5},{8,6},{9,7},{10,8},{11,9},{12,... | collective-permute-start | bytes 2359304 | tf_op jit(solution)/shard_map/ppermute | solution.py:16
  42.0 17.3 %collective-permute-start.5 = (bf16[512,768]{1,0:T(8,128)(2,1)}, bf16[512,768]{1,0:T(8,128)(2,1)}, u32[]{:S(2)}, u32[]{:S(2)}) collective-permute-start(bf16[512,768]{1,0:T(8,128)(2,1)} %collective-permute-done.refs_1_.refs_10_), channel_id=1, source_target_pairs={{0,1},{1,0},{2,3},{3,2},{4,5},{5,4},{6,7},{7,6},{8,9},{9,8},{10,11... | collective-permute-start | bytes 2359304 | tf_op jit(solution)/shard_map/ppermute | solution.py:157
  42.1 17.2 %collective-permute-start.6 = (bf16[512,768]{1,0:T(8,128)(2,1)}, bf16[512,768]{1,0:T(8,128)(2,1)}, u32[]{:S(2)}, u32[]{:S(2)}) collective-permute-start(bf16[512,768]{1,0:T(8,128)(2,1)} %collective-permute-done.1.refs_2_.refs_11_), channel_id=1, source_target_pairs={{0,1},{1,0},{2,3},{3,2},{4,5},{5,4},{6,7},{7,6},{8,9},{9,8},{10,11... | collective-permute-start | bytes 2359304 | tf_op jit(solution)/shard_map/ppermute | solution.py:157
  55.1 5.0 %copy-start.1 = (bf16[512,768]{1,0:T(8,128)(2,1)}, bf16[512,768]{1,0:T(8,128)(2,1)S(1)}, u32[]{:S(2)}) copy-start(bf16[512,768]{1,0:T(8,128)(2,1)S(1)} %collective-permute-done.2.refs_3_.refs_12_) | copy-start | bytes 2359300
  57.6 2.5 %collective-permute-start.7 = (bf16[512,768]{1,0:T(8,128)(2,1)S(1)}, bf16[512,768]{1,0:T(8,128)(2,1)}, u32[]{:S(2)}, u32[]{:S(2)}) collective-permute-start(bf16[512,768]{1,0:T(8,128)(2,1)S(1)} %broadcast_select_fusion), channel_id=1, source_target_pairs={{0,1},{1,0},{2,3},{3,2},{4,5},{5,4},{6,7},{7,6},{8,9},{9,8},{10,11... | collective-permute-start | bytes 2359304 | tf_op jit(solution)/shard_map/ppermute | solution.py:157
  77.7 0.7 copy-start.3
  77.7 0.7 copy-start.4
  78.8 10.1 %collective-permute-start.8 = (bf16[15,1536]{1,0:T(8,128)(2,1)S(1)}, bf16[15,1536]{1,0:T(8,128)(2,1)S(1)}, u32[]{:S(2)}, u32[]{:S(2)}) collective-permute-start(bf16[15,1536]{1,0:T(8,128)(2,1)S(1)} %get-tuple-element.36), channel_id=1, source_target_pairs={{1,2},{3,4},{5,6},{7,8},{9,10},{11,12},{13,14},{15,16},{17,18},{19... | collective-permute-start | bytes 138248 | tf_op jit(solution)/shard_map/ppermute | solution.py:188
  87.2 1.8 %collective-permute-start.9 = (bf16[15,1536]{1,0:T(8,128)(2,1)S(1)}, bf16[15,1536]{1,0:T(8,128)(2,1)S(1)}, u32[]{:S(2)}, u32[]{:S(2)}) collective-permute-start(bf16[15,1536]{1,0:T(8,128)(2,1)S(1)} %get-tuple-element.37), channel_id=1, source_target_pairs={{0,1},{1,0},{2,3},{3,2},{4,5},{5,4},{6,7},{7,6},{8,9},{9,8},{10,11... | collective-permute-start | bytes 138248 | tf_op jit(solution)/shard_map/ppermute | solution.py:191
  89.2 0.7 copy-start.5
  89.2 0.7 copy-start.6
  89.2 0.7 copy-start.7
  89.2 0.7 copy-start.8
  89.2 0.7 copy-start.9
  89.2 0.7 copy-start.10
  89.4 10.0 %slice-start = ((s8[4718592]{0:T(1024)(128)(4,1)}), s8[4194304]{0:T(1024)(128)(4,1)S(1)}, s32[]{:S(2)}) async-start(s8[4718592]{0:T(1024)(128)(4,1)} %bitcast.17), calls=%async_computation | async-start | bytes 8388608
  90.1 9.3 %slice-start.1 = ((s8[4718592]{0:T(1024)(128)(4,1)}), s8[524288]{0:T(1024)(128)(4,1)S(1)}, s32[]{:S(2)}) async-start(s8[4718592]{0:T(1024)(128)(4,1)} %bitcast.17), calls=%async_computation.1 | async-start | bytes 1048576
  (14 other events, 9.4 us)
